TPU v7x, 32 devices: a whole 2x2x4 slice. The times are simulated.
32 devices in a mesh: expert: 8 (over z, x), tensor: 4 (over y, core).
Axes of the slice: x: 2, y: 2, z: 4, core: 2. Of those that a mesh axis runs over, the one named last changes fastest.
Arguments:
- attn_heads: bfloat16 [1024, 4096], P('expert', 'tensor'), may hold values from -6 to 6
- out_proj: bfloat16 [4096, 4096], P('tensor', 'expert'), may hold values from -0.09375 to 0.09375
- residual: bfloat16 [1024, 4096], P('expert'), may hold values from -6 to 6
- norm_gain: bfloat16 [4096], replicated, may hold values from 0.099609375 to 1.8984375
- gate_proj: bfloat16 [16, 1536, 4096], P('expert', 'tensor'), may hold values from -0.09375 to 0.09375
- up_proj: bfloat16 [16, 1536, 4096], P('expert', 'tensor'), may hold values from -0.09375 to 0.09375
- down_proj: bfloat16 [16, 1536, 4096], P('expert', None, 'tensor'), may hold values from -0.15625 to 0.15625
- expert_ids: int32 [1024, 8], P('expert'), may hold values from 0 to 15, all different within a row; in each aligned block of 128 rows (0 to 127, 128 to 255, ...) at most 96 rows name the same one
- gate_scores: float32 [1024, 8], P('expert'), may hold values from 0.25 to 1
Outputs:
- layer_out: bfloat16 [1024, 4096], P('expert', 'tensor')
Inputs may be any that keep to these rules, and one draw needn't show every extreme that they name: `expert_ids`: each row names 8 different experts. Among the 128 rows of one device no expert is named by more than 96 rows, a bound that some block reaches.
All inputs are finite; a program needn't handle non-finite values.
Results may differ from a plain program's by a relative error of at most 0.0051.
Values may be sent and summed in bfloat16 or wider, within the bound.
No kernel may reach another device: no remote copies, remote signals or barrier semaphores. Data moves between devices by JAX's collectives and lax.ppermute only.
A program may use at most 128 MiB of HBM per device.

v0:
```python
import jax
import jax.numpy as jnp
from jax import lax
from jax.sharding import PartitionSpec as P

EPS = 1e-06


def on_device(
    attn_heads,
    out_proj,
    residual,
    norm_gain,
    gate_proj,
    up_proj,
    down_proj,
    expert_ids,
    gate_scores,
):
    tok_count = residual.shape[0]
    width = residual.shape[1]
    topk = expert_ids.shape[1]
    groups = lax.axis_size("expert")
    tensor_ways = lax.axis_size("tensor")
    exp_local = gate_proj.shape[0]
    experts_all = groups * exp_local
    slot_cap = 3 * tok_count * topk // (2 * experts_all)
    share = width // tensor_ways
    offset = lax.axis_index("tensor") * share
    partial_proj = jnp.dot(
        attn_heads,
        lax.all_gather(out_proj, "expert", axis=1, tiled=True),
        preferred_element_type=jnp.float32,
    )
    attn_part = lax.psum_scatter(partial_proj, "tensor", scatter_dimension=1, tiled=True)
    res_part = lax.dynamic_slice_in_dim(residual, offset, share, 1)
    state_part = (res_part.astype(jnp.float32) + attn_part).astype(jnp.bfloat16)
    state_f = state_part.astype(jnp.float32)
    squares = lax.psum(jnp.sum(state_f * state_f, axis=1), "tensor")
    gain_part = lax.dynamic_slice_in_dim(norm_gain, offset, share, 0)
    normed = (
        state_f * lax.rsqrt(squares / width + EPS)[:, None] * gain_part.astype(jnp.float32)
    ).astype(jnp.bfloat16)
    picks = expert_ids[:, :, None] == jnp.arange(experts_all, dtype=jnp.int32)[None, None, :]
    flag = jnp.sum(picks.astype(jnp.int32), axis=1)
    before = jnp.cumsum(flag, axis=0) - flag
    rank = jnp.sum(jnp.where(picks, before[:, None, :], 0), axis=2)
    slot = expert_ids * slot_cap + rank
    token_ids = jnp.arange(tok_count * topk, dtype=jnp.int32) // topk + 1
    owner = jnp.zeros((experts_all * slot_cap,), jnp.int32).at[slot.reshape(-1)].set(token_ids)
    rows = jnp.take(normed, jnp.maximum(owner - 1, 0), axis=0)
    rows = jnp.where((owner > 0)[:, None], rows, jnp.zeros((), jnp.bfloat16))
    send = rows.reshape(groups, exp_local, slot_cap, rows.shape[1])
    block = lax.all_gather(
        lax.all_to_all(send, "expert", split_axis=0, concat_axis=0, tiled=True),
        "tensor",
        axis=3,
        tiled=True,
    )
    count = block.shape[2]
    stacked = jnp.transpose(block, (1, 0, 2, 3)).reshape(exp_local, groups * count, width)
    gate = jnp.einsum("erd,efd->erf", stacked, gate_proj, preferred_element_type=jnp.float32)
    upper = jnp.einsum("erd,efd->erf", stacked, up_proj, preferred_element_type=jnp.float32)
    act = (jax.nn.silu(gate) * upper).astype(jnp.bfloat16)
    whole_act = lax.all_gather(act, "tensor", axis=2, tiled=True)
    result = jnp.einsum(
        "erf,efd->erd", whole_act, down_proj, preferred_element_type=jnp.float32
    ).astype(jnp.bfloat16)
    result = jnp.transpose(result.reshape(exp_local, groups, count, share), (1, 0, 2, 3))
    back = lax.all_to_all(result, "expert", split_axis=0, concat_axis=0, tiled=True)
    flat = back.reshape(experts_all * slot_cap, share)
    picked = jnp.take(flat, slot.reshape(-1), axis=0).reshape(tok_count, topk, share)
    weights = gate_scores / jnp.sum(gate_scores, axis=1, keepdims=True)
    mixture = jnp.einsum("tk,tkd->td", weights, picked.astype(jnp.float32))
    return (state_part.astype(jnp.float32) + mixture).astype(jnp.bfloat16)


def solution(mesh):
    in_specs = (
        P("expert", "tensor"),
        P("tensor", "expert"),
        P("expert", None),
        P(),
        P("expert", "tensor", None),
        P("expert", "tensor", None),
        P("expert", None, "tensor"),
        P("expert", None),
        P("expert", None),
    )
    out_specs = P("expert", "tensor")
    return jax.shard_map(
        on_device, mesh=mesh, in_specs=in_specs, out_specs=out_specs, check_vma=False
    )
```

profile of v0, /device:TPU:0, one launch (start us, length us, event | category | flops | bytes accessed | tf_op | source)
XLA Modules:
  0.0 507.4 jit_solution(3773535396827234200)
XLA Ops:
  6.5 0.7 all-gather.4.cloned.1.call-update
  7.3 130.2 %all-gather.4.cloned.1.call-done = bf16[1024,4096]{1,0:T(8,128)(2,1)} async-done(((bf16[1024,512]{1,0:T(8,128)(2,1)}), bf16[1024,4096]{1,0:T(8,128)(2,1)}) %all-gather.4.cloned.1.call-update) | async-done | bytes 8388624 | tf_op jit(solution)/shard_map/all_gather | solution.py:32
  137.5 6.0 %fusion.14 = f32[128,4096]{1,0:T(8,128)} fusion(bf16[128,1024]{1,0:T(8,128)(2,1)S(1)} %copy-done, bf16[1024,4096]{1,0:T(8,128)(2,1)} %all-gather.4.cloned.1.call-done), kind=kOutput, calls=%fused_computation.45 | convolution fusion | flops 1073741824 | bytes 10747904 | tf_op jit(solution)/shard_map/dot_general | solution.py:30
  143.6 0.1 copy.26
  143.7 0.2 reduce_window_sum.11
  144.0 0.1 copy.30
  144.1 0.1 reshape.84
  144.3 4.3 scatter_custom_fusion
  148.6 0.1 broadcast_in_dim.61
  148.8 0.7 dynamic-slice_convert_fusion
  149.5 23.8 %reduce-scatter.2.cloned.1.call-done = f32[128,1024]{1,0:T(8,128)} async-done(((f32[128,4096]{1,0:T(8,128)}), f32[128,1024]{1,0:T(8,128)}) %reduce-scatter.2.cloned.1.call-update) | async-done | bytes 524304 | tf_op jit(solution)/shard_map/reduce_scatter | solution.py:35
  173.3 1.3 fusion.3
  174.6 5.8 %psum.7 = f32[128]{0:T(128)S(1)} all-reduce(f32[128]{0:T(128)S(1)} %get-tuple-element.7), channel_id=1, replica_groups=mesh['expert'=8,'tensor'=4] {'tensor'}, use_global_device_ids=true, to_apply=%region_7.8 | all-reduce | flops 128 | bytes 1024 | tf_op jit(solution)/shard_map/psum | solution.py:39
  180.4 0.1 fusion.5
  180.5 5.1 gather_fusion
  185.6 0.6 select_select_fusion
  186.2 76.2 %all_to_all.10 = bf16[8,2,96,1024]{3,2,1,0:T(8,128)(2,1)} all-to-all(bf16[8,2,96,1024]{3,2,1,0:T(8,128)(2,1)S(1)} %select_select_fusion), channel_id=1, replica_groups=mesh['expert'=8,'tensor'=4] {'expert'}, dimensions={0} | all-to-all | bytes 6291456 | tf_op jit(solution)/shard_map/all_to_all | solution.py:55
  262.5 0.2 all-gather.8.cloned.1.call-start
  262.7 80.0 %all-gather.6.cloned.1.call-done = bf16[8,2,96,4096]{3,2,1,0:T(8,128)(2,1)} async-done(((bf16[8,2,96,1024]{3,2,1,0:T(8,128)(2,1)}), bf16[8,2,96,4096]{3,2,1,0:T(8,128)(2,1)}) %all-gather.6.cloned.1.call-update) | async-done | bytes 12582928 | tf_op jit(solution)/shard_map/all_gather | solution.py:54
  342.7 6.6 %copy.31 = bf16[2,8,96,4096]{3,2,1,0:T(8,128)(2,1)S(1)} copy(bf16[2,8,96,4096]{3,2,0,1:T(8,128)(2,1)} %bitcast.26) | data formatting | bytes 25165824 | tf_op jit(solution)/shard_map/transpose | solution.py:61
  349.3 8.1 %fusion.15 = f32[2,768,384]{2,1,0:T(8,128)} fusion(bf16[2,768,4096]{2,1,0:T(8,128)(2,1)S(1)} %bitcast.27, bf16[2,384,4096]{2,1,0:T(8,128)(2,1)S(1)} %bitcast.35), kind=kOutput, calls=%fused_computation.46 | convolution fusion | flops 4831838208 | bytes 21233664 | tf_op jit(solution)/shard_map/erd,efd->erf/dot_general | solution.py:62
  357.4 10.0 %multiply_convert_fusion = bf16[2,768,384]{2,1,0:T(8,128)(2,1)} fusion(f32[2,768,384]{2,1,0:T(8,128)} %fusion.15, bf16[2,768,4096]{2,1,0:T(8,128)(2,1)S(1)} %bitcast.28, bf16[2,384,4096]{2,1,0:T(8,128)(2,1)} %param.14), kind=kOutput, calls=%fused_computation.5 | convolution fusion | flops 4835377152 | bytes 22413312 | tf_op jit(solution)/shard_map/erd,efd->erf/dot_general | solution.py:63
  367.5 37.6 %all-gather.8.cloned.1.call-done = bf16[2,768,1536]{2,1,0:T(8,128)(2,1)} async-done(((bf16[2,768,384]{2,1,0:T(8,128)(2,1)}), bf16[2,768,1536]{2,1,0:T(8,128)(2,1)}) %all-gather.8.cloned.1.call-update) | async-done | bytes 4718608 | tf_op jit(solution)/shard_map/all_gather | solution.py:65
  405.0 8.6 %convolution_convert_fusion = bf16[2,768,1024]{2,1,0:T(8,128)(2,1)S(1)} fusion(bf16[2,768,1536]{2,1,0:T(8,128)(2,1)} %all-gather.8.cloned.1.call-done, bf16[2,1536,1024]{2,1,0:T(8,128)(2,1)} %param.15), kind=kOutput, calls=%fused_computation.6 | convolution fusion | flops 4833411072 | bytes 14155776 | tf_op jit(solution)/shard_map/erf,efd->erd/dot_general | solution.py:66
  413.6 1.9 copy.37
  415.5 5.6 %all-to-all-start.1 = ((bf16[8,2,96,1024]{3,2,1,0:T(8,128)(2,1)}), bf16[8,2,96,1024]{3,2,1,0:T(8,128)(2,1)S(1)}, u32[]{:S(2)}, u32[]{:S(2)}) async-start(bf16[8,2,96,1024]{3,2,1,0:T(8,128)(2,1)} %bitcast.29), calls=%async_computation.2 | async-start | bytes 6291456 | tf_op jit(solution)/shard_map/all_to_all | solution.py:70
  421.2 0.1 copy.29
  421.3 0.1 copy.33
  421.5 70.8 %all-to-all-done.1 = bf16[8,2,96,1024]{3,2,1,0:T(8,128)(2,1)S(1)} async-done(((bf16[8,2,96,1024]{3,2,1,0:T(8,128)(2,1)}), bf16[8,2,96,1024]{3,2,1,0:T(8,128)(2,1)S(1)}, u32[]{:S(2)}, u32[]{:S(2)}) %all-to-all-start.1) | async-done | bytes 3145760 | tf_op jit(solution)/shard_map/all_to_all | solution.py:70
  492.3 5.3 %gather_fusion.1 = bf16[1024,1024]{1,0:T(8,128)(2,1)} fusion(bf16[1536,1024]{1,0:T(8,128)(2,1)S(1)} %bitcast.25, s32[1024]{0:T(1024)S(1)} %broadcast_clamp_fusion), kind=kCustom, calls=%fused_computation.1 | custom fusion | bytes 4198400 | tf_op jit(solution)/shard_map/jit(_take)/gather | solution.py:72
  497.6 2.4 fusion
  500.1 0.8 fusion.6
  (38 shorter events, 0.4 us)
Async XLA Ops:
  6.5 131.0 %copy-start = (bf16[128,1024]{1,0:T(8,128)(2,1)S(1)}, bf16[128,1024]{1,0:T(8,128)(2,1)}, u32[]{:S(2)}) copy-start(bf16[128,1024]{1,0:T(8,128)(2,1)} %param.9) | copy-start | bytes 786436
  6.5 131.0 %all-gather.4.cloned.1.call-start = ((), (), s32[]{:S(2)}) async-start(), calls=%async_computation.3 | async-start | bytes 9437184 | tf_op jit(solution)/shard_map/all_gather | solution.py:32
  7.3 136.3 %copy-start.4 = (s32[128,8]{0,1:T(8,128)S(1)}, s32[128,8]{0,1:T(8,128)}, u32[]{:S(2)}) copy-start(s32[128,8]{0,1:T(8,128)} %param.16) | copy-start | bytes 12292
  7.3 166.0 %reduce-scatter.2.cloned.1.call-start = ((), (), s32[]{:S(2)}) async-start(), calls=%async_computation.4 | async-start | bytes 2621440 | tf_op jit(solution)/shard_map/reduce_scatter | solution.py:35
  143.5 199.1 %all-gather.6.cloned.1.call-start = ((), (), s32[]{:S(2)}) async-start(), calls=%async_computation.5 | async-start | bytes 15728640 | tf_op jit(solution)/shard_map/all_gather | solution.py:54
  174.6 5.8 %copy-start.2 = (bf16[128,1024]{1,0:T(8,128)(2,1)}, bf16[128,1024]{1,0:T(8,128)(2,1)S(1)}, u32[]{:S(2)}) copy-start(bf16[128,1024]{1,0:T(8,128)(2,1)S(1)} %get-tuple-element.8) | copy-start | bytes 786436
  262.4 86.8 %slice-start = ((s8[6291456]{0:T(1024)(128)(4,1)}), s8[2097152]{0:T(1024)(128)(4,1)S(1)}, s32[]{:S(2)}) async-start(s8[6291456]{0:T(1024)(128)(4,1)} %bitcast.34), calls=%async_computation.7 | async-start | bytes 4194304
  262.5 142.5 %all-gather.8.cloned.1.call-start = ((), (), s32[]{:S(2)}) async-start(), calls=%async_computation.6 | async-start | bytes 5898240 | tf_op jit(solution)/shard_map/all_gather | solution.py:65
  342.7 6.6 %slice-start.1 = ((s8[6291456]{0:T(1024)(128)(4,1)}), s8[4194304]{0:T(1024)(128)(4,1)S(1)}, s32[]{:S(2)}) async-start(s8[6291456]{0:T(1024)(128)(4,1)} %bitcast.34), calls=%async_computation.8 | async-start | bytes 8388608
  415.5 5.8 %copy-start.5 = (f32[128,8]{0,1:T(8,128)S(1)}, f32[128,8]{0,1:T(8,128)}, u32[]{:S(2)}) copy-start(f32[128,8]{0,1:T(8,128)} %param.17) | copy-start | bytes 12292
  415.5 76.8 %all-to-all-start.1 = ((bf16[8,2,96,1024]{3,2,1,0:T(8,128)(2,1)}), bf16[8,2,96,1024]{3,2,1,0:T(8,128)(2,1)S(1)}, u32[]{:S(2)}, u32[]{:S(2)}) async-start(bf16[8,2,96,1024]{3,2,1,0:T(8,128)(2,1)} %bitcast.29), calls=%async_computation.2 | async-start | bytes 6291456 | tf_op jit(solution)/shard_map/all_to_all | solution.py:70
  492.3 8.6 %copy-start.1 = (bf16[128,1024]{1,0:T(8,128)(2,1)S(1)}, bf16[128,1024]{1,0:T(8,128)(2,1)}, u32[]{:S(2)}) copy-start(bf16[128,1024]{1,0:T(8,128)(2,1)} %param.9) | copy-start | bytes 786436
  497.6 2.4 copy-start.3
Sparse Core Ops, SparseCore 0:
  9.4 128.0 all-gather.3
  143.7 29.5 reduce-scatter.1
  262.6 80.0 all-gather.5
  367.6 37.3 all-gather.7
where the time goes:
time: 508 us; the launch traced here: 507 us
  waiting for transfers between devices  343 us (68%)
  blocking collectives  82 us (16%)
  matrix products  35.1 us (7%)
  local copies, waits for them, and re-layouts  24.1 us (5%)
  between operations  13.3 us (3%)
  starting transfers between devices  5.95 us (1%)
    all_gather x1, waiting for transfers between devices, on_device(): lax.all_gather(out_proj, 'expert', axis=1, tiled=True)  130 us
    all_gather x1, waiting for transfers between devices, on_device(): lax.all_gather(lax.all_to_all(send, 'expert', split_axis=0, concat_axis=0...  80 us
    all_to_all x1, blocking collectives, on_device(): lax.all_to_all(send, 'expert', split_axis=0, concat_axis=0, tiled=True)  76.2 us
    all_to_all x1, waiting for transfers between devices, on_device(): lax.all_to_all(result, 'expert', split_axis=0, concat_axis=0, tiled=True)  70.8 us
    all_gather x1, waiting for transfers between devices, on_device(): whole_act = lax.all_gather(act, 'tensor', axis=2, tiled=True)  37.6 us
    reduce_scatter x1, waiting for transfers between devices, on_device(): lax.psum_scatter(partial_proj, 'tensor', scatter_dimension=1, tiled=True)  23.8 us
  transfers between devices with their start and end apart: 5, of which 5 were waited for; matrix products, arithmetic and copies ran while one was open for 1% of the time, Pallas kernels for 0%

commit v1 on v0

v1 whole, which is shorter than its diff:
```python
import jax
import jax.numpy as jnp
from jax import lax
from jax.sharding import PartitionSpec as P

EPS = 1e-06


def on_device(
    attn_heads,
    out_proj,
    residual,
    norm_gain,
    gate_proj,
    up_proj,
    down_proj,
    expert_ids,
    gate_scores,
):
    tok_count = residual.shape[0]
    width = residual.shape[1]
    groups = lax.axis_size("expert")
    tensor_ways = lax.axis_size("tensor")
    exp_local = gate_proj.shape[0]
    hidden_local = gate_proj.shape[1]
    share = width // tensor_ways
    cols_e = out_proj.shape[1]
    cols_et = cols_e // tensor_ways
    me_e = lax.axis_index("expert")
    me_t = lax.axis_index("tensor")
    all_tok = groups * tok_count

    heads_all = lax.all_gather(attn_heads, "expert", axis=0, tiled=True)
    partial = jnp.dot(heads_all, out_proj, preferred_element_type=jnp.float32)
    summed = lax.psum_scatter(partial, "tensor", scatter_dimension=1, tiled=True)
    mine = lax.all_to_all(
        summed.reshape(groups, tok_count, cols_et), "expert", 0, 0, tiled=False
    )
    res_cols = lax.dynamic_index_in_dim(
        residual.reshape(tok_count, groups, tensor_ways, cols_et), me_t, 2, keepdims=False
    )
    state_ct = (jnp.transpose(res_cols, (1, 0, 2)).astype(jnp.float32) + mine).astype(
        jnp.bfloat16
    )
    state_all = lax.all_gather(state_ct, "tensor", axis=0, tiled=False)
    state = jnp.transpose(state_all, (2, 1, 0, 3)).reshape(tok_count, width)
    state_f = state.astype(jnp.float32)

    squares = jnp.sum(state_f * state_f, axis=1, keepdims=True)
    scale = lax.rsqrt(squares / width + EPS)
    state_q = lax.dynamic_slice_in_dim(state_f, me_t * share, share, 1)
    gain_q = lax.dynamic_slice_in_dim(norm_gain, me_t * share, share, 0).astype(jnp.float32)
    normed_q = (state_q * scale * gain_q).astype(jnp.bfloat16)

    rows_q = lax.all_gather(normed_q, "expert", axis=0, tiled=True)
    rows = lax.all_gather(rows_q, "tensor", axis=0, tiled=False)

    ids_all = lax.all_gather(expert_ids, "expert", axis=0, tiled=True)
    scores_all = lax.all_gather(gate_scores, "expert", axis=0, tiled=True)
    weights = scores_all / jnp.sum(scores_all, axis=1, keepdims=True)

    total = jnp.zeros((all_tok, share), jnp.float32)
    for loc in range(exp_local):
        glob = me_e * exp_local + loc
        hit = ids_all == glob
        w_tok = jnp.sum(jnp.where(hit, weights, 0.0), axis=1)
        chosen = jnp.any(hit, axis=1)
        gmat = gate_proj[loc].reshape(hidden_local, tensor_ways, share)
        umat = up_proj[loc].reshape(hidden_local, tensor_ways, share)
        gate = jnp.einsum("ard,fad->rf", rows, gmat, preferred_element_type=jnp.float32)
        upper = jnp.einsum("ard,fad->rf", rows, umat, preferred_element_type=jnp.float32)
        act = (jax.nn.silu(gate) * upper).astype(jnp.bfloat16)
        act_all = lax.all_gather(act, "tensor", axis=0, tiled=False)
        dmat = down_proj[loc].reshape(tensor_ways, hidden_local, share)
        out = jnp.einsum(
            "arf,afd->rd", act_all, dmat, preferred_element_type=jnp.float32
        ).astype(jnp.bfloat16)
        total = total + jnp.where(
            chosen[:, None], w_tok[:, None] * out.astype(jnp.float32), 0.0
        )
    mixture = lax.psum_scatter(total, "expert", scatter_dimension=0, tiled=True)
    state_out = lax.dynamic_slice_in_dim(state_f, me_t * share, share, 1)
    return (state_out + mixture).astype(jnp.bfloat16)


def solution(mesh):
    in_specs = (
        P("expert", "tensor"),
        P("tensor", "expert"),
        P("expert", None),
        P(),
        P("expert", "tensor", None),
        P("expert", "tensor", None),
        P("expert", None, "tensor"),
        P("expert", None),
        P("expert", None),
    )
    out_specs = P("expert", "tensor")
    return jax.shard_map(
        on_device, mesh=mesh, in_specs=in_specs, out_specs=out_specs, check_vma=False
    )
```

time: 508 us -> 467 us (0.919)
  waiting for transfers between devices: 343 us -> 287 us
  blocking collectives: 82 us -> 61.1 us
  local copies, waits for them, and re-layouts: 24.1 us -> 41.9 us
  matrix products: 35.1 us -> 49.4 us
    reduce_scatter x1 -> x2, waiting for transfers between devices: 23.8 us -> 118 us  [the longest x1 88.2 us: on_device(): mixture = lax.psum_scatter(total, 'expert', scatter_dimension=0, tiled=True)]
    all_gather x3 -> x6, waiting for transfers between devices: 248 us -> 154 us  [the longest x1 54.2 us: on_device(): heads_all = lax.all_gather(attn_heads, 'expert', axis=0, tiled=True)]
    all_to_all x1 -> x0, blocking collectives: 76.2 us -> none  [on_device(): lax.all_to_all(send, 'expert', split_axis=0, concat_axis=0, tiled=True)]
    all_gather x0 -> x2, blocking collectives: none -> 61.1 us  [the longest x1 30.6 us: on_device(): scores_all = lax.all_gather(gate_scores, 'expert', axis=0, tiled=True)]
    all_to_all x1, waiting for transfers between devices: 70.8 us -> 13.8 us  [on_device(): lax.all_to_all(summed.reshape(groups, tok_count, cols_et), 'expert', 0, 0...]
    unnamed x16 -> x23, local copies, waits for them, and re-layouts: 0.03 us -> 18.1 us
    slice x0 -> x3, local copies, waits for them, and re-layouts: none -> 17.7 us  [the longest x1 7.19 us: on_device(): umat = up_proj[loc].reshape(hidden_local, tensor_ways, share)]
    dot_general x5 -> x7, matrix products: 35.1 us -> 49.4 us  [the longest x2 15.6 us: on_device(): jnp.einsum('arf,afd->rd', act_all, dmat, preferred_element_type=jnp.float32)]
  transfers between devices with their start and end apart: 5 -> 9, of which waited for: 5 -> 7; matrix products, arithmetic and copies ran while one was open for 1% -> 13% of each run, Pallas kernels for 0% -> 0%
where the time goes in v1:
time: 467 us
  waiting for transfers between devices  287 us (61%)
  blocking collectives  61.1 us (13%)
  matrix products  49.4 us (11%)
  local copies, waits for them, and re-layouts  41.9 us (9%)
  between operations  13.6 us (3%)
  other arithmetic  7.63 us (2%)
  starting transfers between devices  5.95 us (1%)
    reduce_scatter x1, waiting for transfers between devices, on_device(): mixture = lax.psum_scatter(total, 'expert', scatter_dimension=0, tiled=True)  88.2 us
    all_gather x1, waiting for transfers between devices, on_device(): heads_all = lax.all_gather(attn_heads, 'expert', axis=0, tiled=True)  54.2 us
    all_gather x1, waiting for transfers between devices, on_device(): rows_q = lax.all_gather(normed_q, 'expert', axis=0, tiled=True)  49.4 us
    all_gather x1, waiting for transfers between devices, on_device(): rows = lax.all_gather(rows_q, 'tensor', axis=0, tiled=False)  36.2 us
    all_gather x1, blocking collectives, on_device(): scores_all = lax.all_gather(gate_scores, 'expert', axis=0, tiled=True)  30.6 us
    all_gather x1, blocking collectives, on_device(): ids_all = lax.all_gather(expert_ids, 'expert', axis=0, tiled=True)  30.4 us
    reduce_scatter x1, waiting for transfers between devices, on_device(): lax.psum_scatter(partial, 'tensor', scatter_dimension=1, tiled=True)  30.1 us
    unnamed x23, local copies, waits for them, and re-layouts  18.1 us
  transfers between devices with their start and end apart: 9, of which 7 were waited for; matrix products, arithmetic and copies ran while one was open for 13% of the time, Pallas kernels for 0%

profile of v1, /device:TPU:0, one launch (start us, length us, event | category | flops | bytes accessed | tf_op | source)
XLA Modules:
  0.0 466.5 jit_solution(11226527951776345849)
XLA Ops:
  7.3 54.2 %all-gather.11.cloned.1.call-done = bf16[1024,1024]{1,0:T(8,128)(2,1)} async-done(((bf16[128,1024]{1,0:T(8,128)(2,1)}), bf16[1024,1024]{1,0:T(8,128)(2,1)}) %all-gather.11.cloned.1.call-update) | async-done | bytes 2097168 | tf_op jit(solution)/shard_map/all_gather | solution.py:33
  61.5 4.2 fusion.15
  65.7 30.1 %reduce-scatter.3.cloned.1.call-done = f32[1024,128]{1,0:T(8,128)} async-done(((f32[1024,512]{1,0:T(8,128)}), f32[1024,128]{1,0:T(8,128)}) %reduce-scatter.3.cloned.1.call-update) | async-done | bytes 524304 | tf_op jit(solution)/shard_map/reduce_scatter | solution.py:35
  95.8 2.0 copy.32
  97.8 5.5 %all-to-all-start = ((f32[8,128,128]{1,2,0:T(8,128)}), f32[8,128,128]{1,2,0:T(8,128)S(1)}, u32[]{:S(2)}, u32[]{:S(2)}) async-start(f32[8,128,128]{1,2,0:T(8,128)} %copy.32), calls=%async_computation.1 | async-start | bytes 1048576 | tf_op jit(solution)/shard_map/all_to_all | solution.py:36
  104.0 13.8 %all-to-all-done = f32[8,128,128]{1,2,0:T(8,128)S(1)} async-done(((f32[8,128,128]{1,2,0:T(8,128)}), f32[8,128,128]{1,2,0:T(8,128)S(1)}, u32[]{:S(2)}, u32[]{:S(2)}) %all-to-all-start) | async-done | bytes 524320 | tf_op jit(solution)/shard_map/all_to_all | solution.py:36
  117.9 0.9 copy.33
  119.5 14.3 %all-gather.15.cloned.1.call-done = bf16[32,128,128]{2,1,0:T(8,128)(2,1)} async-done(((bf16[8,128,128]{2,1,0:T(8,128)(2,1)}), bf16[32,128,128]{2,1,0:T(8,128)(2,1)}) %all-gather.15.cloned.1.call-update) | async-done | bytes 1048592 | tf_op jit(solution)/shard_map/all_gather | solution.py:45
  133.8 1.5 multiply_reduce_fusion
  135.3 1.5 bitcast_convert_fusion.2
  136.8 1.4 copy.52
  138.1 1.9 reshape.27
  140.0 1.9 multiply_convert_fusion
  141.9 49.4 %all-gather.13.cloned.1.call-done = bf16[1024,1024]{1,0:T(8,128)(2,1)} async-done(((bf16[128,1024]{1,0:T(8,128)(2,1)}), bf16[1024,1024]{1,0:T(8,128)(2,1)}) %all-gather.13.cloned.1.call-update) | async-done | bytes 2097168 | tf_op jit(solution)/shard_map/all_gather | solution.py:55
  191.4 5.2 %fusion.14 = (bf16[1,384,4096]{2,1,0:T(8,128)(2,1)S(1)}, bf16[1,384,4096]{2,1,0:T(8,128)(2,1)}) fusion(bf16[2,384,4096]{2,1,0:T(8,128)(2,1)} %param.13), kind=kLoop, calls=%fused_computation.36 | loop fusion | bytes 12582912 | tf_op jit(solution)/shard_map/slice | solution.py:68
  196.6 5.0 %copy.49 = bf16[1,384,4096]{1,2,0:T(8,128)(2,1)} copy(bf16[1,384,4096]{2,1,0:T(8,128)(2,1)} %get-tuple-element.16) | data formatting | bytes 6291456
  201.6 7.2 %fusion.13 = (bf16[1,384,4096]{2,1,0:T(8,128)(2,1)}, bf16[1,384,4096]{2,1,0:T(8,128)(2,1)}) fusion(bf16[2,384,4096]{2,1,0:T(8,128)(2,1)} %param.14), kind=kLoop, calls=%fused_computation.35 | loop fusion | bytes 12582912 | tf_op jit(solution)/shard_map/slice | solution.py:69
  208.8 4.7 %copy.50 = bf16[1,384,4096]{1,2,0:T(8,128)(2,1)} copy(bf16[1,384,4096]{2,1,0:T(8,128)(2,1)} %get-tuple-element.14) | data formatting | bytes 6291456
  213.4 36.2 %all-gather.17.cloned.1.call-done = bf16[4096,1024]{1,0:T(8,128)(2,1)} async-done(((bf16[1024,1024]{1,0:T(8,128)(2,1)}), bf16[4096,1024]{1,0:T(8,128)(2,1)}) %all-gather.17.cloned.1.call-update) | async-done | bytes 8388624 | tf_op jit(solution)/shard_map/all_gather | solution.py:56
  249.6 8.0 %fusion.17 = f32[1024,384,1]{1,0,2:T(8,128)S(1)} fusion(bf16[4,1024,1024]{2,1,0:T(8,128)(2,1)} %bitcast.90, bf16[384,4,1024]{0,2,1:T(8,128)(2,1)} %bitcast.82), kind=kOutput, calls=%fused_computation.39 | convolution fusion | flops 3221225472 | bytes 13107200 | tf_op jit(solution)/shard_map/ard,fad->rf/dot_general | solution.py:70
  257.6 5.5 %fusion = bf16[1024,384]{1,0:T(8,128)(2,1)} fusion(f32[1024,384,1]{1,0,2:T(8,128)S(1)} %fusion.17, bf16[4,1024,1024]{2,1,0:T(8,128)(2,1)S(1)} %bitcast.93, bf16[384,4,1024]{0,2,1:T(8,128)(2,1)S(1)} %bitcast.83), kind=kOutput, calls=%fused_computation.6 | convolution fusion | flops 3223584768 | bytes 13893632 | tf_op jit(solution)/shard_map/ard,fad->rf/dot_general | solution.py:71
  263.4 2.8 copy.47
  266.2 4.9 %copy.48 = bf16[1,384,4096]{1,2,0:T(8,128)(2,1)} copy(bf16[1,384,4096]{2,1,0:T(8,128)(2,1)} %get-tuple-element.13) | data formatting | bytes 6291456
  271.1 7.3 %fusion.16 = f32[1024,384,1]{1,0,2:T(8,128)S(1)} fusion(bf16[4,1024,1024]{2,1,0:T(8,128)(2,1)} %bitcast.91, bf16[384,4,1024]{0,2,1:T(8,128)(2,1)S(1)} %bitcast.84), kind=kOutput, calls=%fused_computation.38 | convolution fusion | flops 3221225472 | bytes 13107200 | tf_op jit(solution)/shard_map/ard,fad->rf/dot_general | solution.py:70
  278.5 8.9 %fusion.4 = bf16[1024,384]{1,0:T(8,128)(2,1)} fusion(f32[1024,384,1]{1,0,2:T(8,128)S(1)} %fusion.16, bf16[4,1024,1024]{2,1,0:T(8,128)(2,1)} %bitcast.92, bf16[384,4,1024]{0,2,1:T(8,128)(2,1)S(1)} %bitcast.85), kind=kOutput, calls=%fused_computation.13 | convolution fusion | flops 3223584768 | bytes 13893632 | tf_op jit(solution)/shard_map/ard,fad->rf/dot_general | solution.py:71
  287.5 30.6 %all_gather.40 = f32[1024,8]{0,1:T(8,128)S(1)} all-gather(f32[128,8]{0,1:T(8,128)S(1)} %copy-done.6), channel_id=1, replica_groups=mesh['expert'=8,'tensor'=4] {'expert'}, dimensions={0}, use_global_device_ids=true | all-gather | bytes 36864 | tf_op jit(solution)/shard_map/all_gather | solution.py:59
  318.1 30.4 %all_gather.39 = s32[1024,8]{0,1:T(8,128)S(1)} all-gather(s32[128,8]{0,1:T(8,128)S(1)} %copy-done.7), channel_id=1, replica_groups=mesh['expert'=8,'tensor'=4] {'expert'}, dimensions={0}, use_global_device_ids=true | all-gather | bytes 36864 | tf_op jit(solution)/shard_map/all_gather | solution.py:58
  348.6 5.3 %fusion.12 = (bf16[1,1536,1024]{2,1,0:T(8,128)(2,1)}, bf16[1,1536,1024]{2,1,0:T(8,128)(2,1)S(1)}) fusion(bf16[2,1536,1024]{2,1,0:T(8,128)(2,1)} %param.15), kind=kLoop, calls=%fused_computation.34 | loop fusion | bytes 12582912 | tf_op jit(solution)/shard_map/slice | solution.py:74
  353.9 6.5 %bitcast_convert_fusion = bf16[1024,1024]{1,0:T(8,128)(2,1)} fusion(bf16[4,1024,384]{2,1,0:T(8,128)(2,1)} %bitcast.94, bf16[4,384,1024]{2,1,0:T(8,128)(2,1)S(1)} %bitcast.87), kind=kOutput, calls=%fused_computation | convolution fusion | flops 3222274048 | bytes 8388608 | tf_op jit(solution)/shard_map/arf,afd->rd/dot_general | solution.py:75
  360.4 9.1 %select_add_fusion = f32[1024,1024]{1,0:T(8,128)} fusion(bf16[1024,1024]{1,0:T(8,128)(2,1)} %bitcast_convert_fusion, f32[1024]{0:T(1024)S(1)} %get-tuple-element.6, f32[1024]{0:T(1024)S(1)} %get-tuple-element.5, pred[1024]{0:T(1024)(128)(4,1)S(1)} %get-tuple-element.9, pred[1024]{0:T(1024)(128)(4,1)S(1)} %get-tuple-element.17, ...), kind=kOutput, calls=%fused_computation.2 | convolution fusion | flops 3229614080 | bytes 12593152 | tf_op jit(solution)/shard_map/arf,afd->rd/dot_general | solution.py:75
  369.5 88.2 %reduce-scatter.5.cloned.1.call-done = f32[128,1024]{1,0:T(8,128)} async-done(((f32[1024,1024]{1,0:T(8,128)}), f32[128,1024]{1,0:T(8,128)}) %reduce-scatter.5.cloned.1.call-update) | async-done | bytes 524304 | tf_op jit(solution)/shard_map/reduce_scatter | solution.py:81
  457.7 2.0 add_convert_fusion
  (43 shorter events, 2.8 us)
Async XLA Ops:
  6.5 55.0 %copy-start = (bf16[1024,512]{1,0:T(8,128)(2,1)S(1)}, bf16[1024,512]{1,0:T(8,128)(2,1)}, u32[]{:S(2)}) copy-start(bf16[1024,512]{1,0:T(8,128)(2,1)} %param.10) | copy-start | bytes 3145732
  6.5 55.0 %all-gather.11.cloned.1.call-start = ((), (), s32[]{:S(2)}) async-start(), calls=%async_computation.3 | async-start | bytes 2359296 | tf_op jit(solution)/shard_map/all_gather | solution.py:33
  7.3 88.5 %reduce-scatter.3.cloned.1.call-start = ((), (), s32[]{:S(2)}) async-start(), calls=%async_computation.4 | async-start | bytes 2621440 | tf_op jit(solution)/shard_map/reduce_scatter | solution.py:35
  65.7 37.7 %copy-start.5 = (bf16[128,4096]{1,0:T(8,128)(2,1)S(1)}, bf16[128,4096]{1,0:T(8,128)(2,1)}, u32[]{:S(2)}) copy-start(bf16[128,4096]{1,0:T(8,128)(2,1)} %param.11) | copy-start | bytes 3145732
  97.8 20.0 %all-to-all-start = ((f32[8,128,128]{1,2,0:T(8,128)}), f32[8,128,128]{1,2,0:T(8,128)S(1)}, u32[]{:S(2)}, u32[]{:S(2)}) async-start(f32[8,128,128]{1,2,0:T(8,128)} %copy.32), calls=%async_computation.1 | async-start | bytes 1048576 | tf_op jit(solution)/shard_map/all_to_all | solution.py:36
  103.3 30.5 %all-gather.15.cloned.1.call-start = ((), (), s32[]{:S(2)}) async-start(), calls=%async_computation.7 | async-start | bytes 1310720 | tf_op jit(solution)/shard_map/all_gather | solution.py:45
  118.8 72.6 %all-gather.13.cloned.1.call-start = ((), (), s32[]{:S(2)}) async-start(), calls=%async_computation.5 | async-start | bytes 2359296 | tf_op jit(solution)/shard_map/all_gather | solution.py:55
  141.9 107.7 %all-gather.17.cloned.1.call-start = ((), (), s32[]{:S(2)}) async-start(), calls=%async_computation.8 | async-start | bytes 10485760 | tf_op jit(solution)/shard_map/all_gather | solution.py:56
  191.4 162.6 %all-gather.21.cloned.1.call-start = ((), (), s32[]{:S(2)}) async-start(), calls=%async_computation.10 | async-start | bytes 3932160 | tf_op jit(solution)/shard_map/all_gather | solution.py:73
  249.6 8.0 %copy-start.2 = (bf16[1,384,4096]{1,2,0:T(8,128)(2,1)S(1)}, bf16[1,384,4096]{1,2,0:T(8,128)(2,1)}, u32[]{:S(2)}) copy-start(bf16[1,384,4096]{1,2,0:T(8,128)(2,1)} %copy.50) | copy-start | bytes 9437188
  249.6 8.0 %copy-start.8 = (bf16[4096,1024]{1,0:T(8,128)(2,1)S(1)}, bf16[4096,1024]{1,0:T(8,128)(2,1)}, u32[]{:S(2)}) copy-start(bf16[4096,1024]{1,0:T(8,128)(2,1)} %all-gather.17.cloned.1.call-done) | copy-start | bytes 25165828
  263.1 97.3 %all-gather.19.cloned.1.call-start = ((), (), s32[]{:S(2)}) async-start(), calls=%async_computation.9 | async-start | bytes 3932160 | tf_op jit(solution)/shard_map/all_gather | solution.py:73
  266.2 4.9 %copy-start.3 = (bf16[1,384,4096]{1,2,0:T(8,128)(2,1)S(1)}, bf16[1,384,4096]{1,2,0:T(8,128)(2,1)}, u32[]{:S(2)}) copy-start(bf16[1,384,4096]{1,2,0:T(8,128)(2,1)} %copy.47) | copy-start | bytes 9437188
  271.1 7.3 %copy-start.4 = (bf16[1,384,4096]{1,2,0:T(8,128)(2,1)S(1)}, bf16[1,384,4096]{1,2,0:T(8,128)(2,1)}, u32[]{:S(2)}) copy-start(bf16[1,384,4096]{1,2,0:T(8,128)(2,1)} %copy.48) | copy-start | bytes 9437188
  278.5 9.0 %copy-start.6 = (f32[128,8]{0,1:T(8,128)S(1)}, f32[128,8]{0,1:T(8,128)}, u32[]{:S(2)}) copy-start(f32[128,8]{0,1:T(8,128)} %param.17) | copy-start | bytes 12292
  278.5 39.7 %copy-start.7 = (s32[128,8]{0,1:T(8,128)S(1)}, s32[128,8]{0,1:T(8,128)}, u32[]{:S(2)}) copy-start(s32[128,8]{0,1:T(8,128)} %param.16) | copy-start | bytes 12292
  287.4 170.3 %reduce-scatter.5.cloned.1.call-start = ((), (), s32[]{:S(2)}) async-start(), calls=%async_computation.6 | async-start | bytes 4718592 | tf_op jit(solution)/shard_map/reduce_scatter | solution.py:81
  360.4 99.3 %copy-start.1 = (bf16[1024,512]{1,0:T(8,128)(2,1)S(1)}, bf16[1024,512]{1,0:T(8,128)(2,1)}, u32[]{:S(2)}) copy-start(bf16[1024,512]{1,0:T(8,128)(2,1)} %param.10) | copy-start | bytes 3145732
Sparse Core Ops, SparseCore 0:
  9.5 51.9 all-gather.10
  65.8 29.9 reduce-scatter.2
  118.9 14.8 all-gather.14
  142.0 49.2 all-gather.12
  192.8 56.7 all-gather.16
  263.3 28.5 all-gather.20
  293.5 28.5 all-gather.18
  369.6 88.0 reduce-scatter.4

commit v2 on v1

--- a/solution.py
+++ b/solution.py
@@ -4,6 +4,7 @@
 from jax.sharding import PartitionSpec as P
 
 EPS = 1e-06
+CHUNKS = 2
 
 
 def on_device(
@@ -52,33 +53,38 @@
     gain_q = lax.dynamic_slice_in_dim(norm_gain, me_t * share, share, 0).astype(jnp.float32)
     normed_q = (state_q * scale * gain_q).astype(jnp.bfloat16)
 
+    experts_all = groups * exp_local
+    hit_src = expert_ids[:, :, None] == jnp.arange(experts_all, dtype=jnp.int32)[None, None, :]
+    weights = gate_scores / jnp.sum(gate_scores, axis=1, keepdims=True)
+    w_src = jnp.sum(jnp.where(hit_src, weights[:, :, None], 0.0), axis=1)
+    w_all = lax.all_gather(w_src.reshape(-1), "expert", axis=0, tiled=True).reshape(
+        all_tok, experts_all
+    )
+    w_mine = lax.dynamic_slice_in_dim(w_all, me_e * exp_local, exp_local, 1)
+
     rows_q = lax.all_gather(normed_q, "expert", axis=0, tiled=True)
-    rows = lax.all_gather(rows_q, "tensor", axis=0, tiled=False)
+    rows = lax.all_gather(rows_q, "tensor", axis=1, tiled=True)
 
-    ids_all = lax.all_gather(expert_ids, "expert", axis=0, tiled=True)
-    scores_all = lax.all_gather(gate_scores, "expert", axis=0, tiled=True)
-    weights = scores_all / jnp.sum(scores_all, axis=1, keepdims=True)
-
-    total = jnp.zeros((all_tok, share), jnp.float32)
-    for loc in range(exp_local):
-        glob = me_e * exp_local + loc
-        hit = ids_all == glob
-        w_tok = jnp.sum(jnp.where(hit, weights, 0.0), axis=1)
-        chosen = jnp.any(hit, axis=1)
-        gmat = gate_proj[loc].reshape(hidden_local, tensor_ways, share)
-        umat = up_proj[loc].reshape(hidden_local, tensor_ways, share)
-        gate = jnp.einsum("ard,fad->rf", rows, gmat, preferred_element_type=jnp.float32)
-        upper = jnp.einsum("ard,fad->rf", rows, umat, preferred_element_type=jnp.float32)
-        act = (jax.nn.silu(gate) * upper).astype(jnp.bfloat16)
-        act_all = lax.all_gather(act, "tensor", axis=0, tiled=False)
-        dmat = down_proj[loc].reshape(tensor_ways, hidden_local, share)
-        out = jnp.einsum(
-            "arf,afd->rd", act_all, dmat, preferred_element_type=jnp.float32
-        ).astype(jnp.bfloat16)
-        total = total + jnp.where(
-            chosen[:, None], w_tok[:, None] * out.astype(jnp.float32), 0.0
-        )
-    mixture = lax.psum_scatter(total, "expert", scatter_dimension=0, tiled=True)
+    chunk = tok_count // CHUNKS
+    rows_c = rows.reshape(groups, CHUNKS, chunk, width)
+    w_c = w_mine.reshape(groups, CHUNKS, chunk, exp_local)
+    pieces = []
+    for c in range(CHUNKS):
+        x = rows_c[:, c].reshape(groups * chunk, width)
+        wc = w_c[:, c].reshape(groups * chunk, exp_local)
+        total = jnp.zeros((groups * chunk, share), jnp.float32)
+        for loc in range(exp_local):
+            gate = jnp.dot(x, gate_proj[loc].T, preferred_element_type=jnp.float32)
+            upper = jnp.dot(x, up_proj[loc].T, preferred_element_type=jnp.float32)
+            act = (jax.nn.silu(gate) * upper).astype(jnp.bfloat16)
+            act_all = lax.all_gather(act, "tensor", axis=1, tiled=True)
+            out = jnp.dot(
+                act_all, down_proj[loc], preferred_element_type=jnp.float32
+            ).astype(jnp.bfloat16)
+            w_tok = wc[:, loc][:, None]
+            total = total + jnp.where(w_tok > 0, w_tok * out.astype(jnp.float32), 0.0)
+        pieces.append(lax.psum_scatter(total, "expert", scatter_dimension=0, tiled=True))
+    mixture = jnp.concatenate(pieces, axis=0)
     state_out = lax.dynamic_slice_in_dim(state_f, me_t * share, share, 1)
     return (state_out + mixture).astype(jnp.bfloat16)
 

time: 467 us -> 497 us (1.064)
  waiting for transfers between devices: 287 us -> 362 us
  blocking collectives: 61.1 us -> 30.5 us
  local copies, waits for them, and re-layouts: 41.9 us -> 14.3 us
  matrix products: 49.4 us -> 63.7 us
    reduce_scatter x1 -> x2, waiting for transfers between devices: 88.2 us -> 137 us  [on_device(): lax.psum_scatter(total, 'expert', scatter_dimension=0, tiled=True)]
    all_gather x2 -> x1, blocking collectives: 61.1 us -> 30.5 us  [on_device(): lax.all_gather(w_src.reshape(-1), 'expert', axis=0, tiled=True)]
    all_gather x3 -> x5, waiting for transfers between devices: 36.2 us -> 62.6 us  [the longest x1 58.2 us: on_device(): rows = lax.all_gather(rows_q, 'tensor', axis=1, tiled=True)]
    unnamed x23 -> x29, local copies, waits for them, and re-layouts: 18.1 us -> 1.9 us
    dot_general x6 -> x12, matrix products: 45.2 us -> 59.5 us  [the longest x4 20.4 us: on_device(): upper = jnp.dot(x, up_proj[loc].T, preferred_element_type=jnp.float32)]
    slice x3 -> x4, local copies, waits for them, and re-layouts: 17.7 us -> 5.74 us  [the longest x1 5.44 us: on_device(): x = rows_c[:, c].reshape(groups * chunk, width)]
  transfers between devices with their start and end apart: 9 -> 12, of which waited for: 7 -> 9; matrix products, arithmetic and copies ran while one was open for 13% -> 11% of each run, Pallas kernels for 0% -> 0%
where the time goes in v2:
time: 497 us; the launch traced here: 496 us
  waiting for transfers between devices  362 us (73%)
  matrix products  63.7 us (13%)
  blocking collectives  30.5 us (6%)
  local copies, waits for them, and re-layouts  14.3 us (3%)
  between operations  13.5 us (3%)
  other arithmetic  6.44 us (1%)
  starting transfers between devices  6.3 us (1%)
    reduce_scatter x2, waiting for transfers between devices, on_device(): lax.psum_scatter(total, 'expert', scatter_dimension=0, tiled=True)  137 us
    all_gather x1, waiting for transfers between devices, on_device(): rows = lax.all_gather(rows_q, 'tensor', axis=1, tiled=True)  58.2 us
    all_gather x1, waiting for transfers between devices, on_device(): heads_all = lax.all_gather(attn_heads, 'expert', axis=0, tiled=True)  54.2 us
    all_gather x1, waiting for transfers between devices, on_device(): rows_q = lax.all_gather(normed_q, 'expert', axis=0, tiled=True)  49.4 us
    all_gather x1, blocking collectives, on_device(): lax.all_gather(w_src.reshape(-1), 'expert', axis=0, tiled=True)  30.5 us
    reduce_scatter x1, waiting for transfers between devices, on_device(): lax.psum_scatter(partial, 'tensor', scatter_dimension=1, tiled=True)  30.1 us
    dot_general x4, matrix products, on_device(): upper = jnp.dot(x, up_proj[loc].T, preferred_element_type=jnp.float32)  20.4 us
    dot_general x4, matrix products, on_device(): jnp.dot(act_all, down_proj[loc], preferred_element_type=jnp.float32)  19.8 us
  transfers between devices with their start and end apart: 12, of which 9 were waited for; matrix products, arithmetic and copies ran while one was open for 11% of the time, Pallas kernels for 0%

profile of v2, /device:TPU:0, one launch (start us, length us, event | category | flops | bytes accessed | tf_op | source)
XLA Modules:
  0.0 496.4 jit_solution(5891352584006589751)
XLA Ops:
  7.3 54.2 %all-gather.10.cloned.1.call-done = bf16[1024,1024]{1,0:T(8,128)(2,1)} async-done(((bf16[128,1024]{1,0:T(8,128)(2,1)}), bf16[1024,1024]{1,0:T(8,128)(2,1)}) %all-gather.10.cloned.1.call-update) | async-done | bytes 2097168 | tf_op jit(solution)/shard_map/all_gather | solution.py:34
  61.5 4.2 fusion.83
  65.7 30.1 %reduce-scatter.4.cloned.1.call-done = f32[1024,128]{1,0:T(8,128)} async-done(((f32[1024,512]{1,0:T(8,128)}), f32[1024,128]{1,0:T(8,128)}) %reduce-scatter.4.cloned.1.call-update) | async-done | bytes 524304 | tf_op jit(solution)/shard_map/reduce_scatter | solution.py:36
  95.8 2.0 copy.35
  97.8 5.5 %all-to-all-start = ((f32[8,128,128]{1,2,0:T(8,128)}), f32[8,128,128]{1,2,0:T(8,128)S(1)}, u32[]{:S(2)}, u32[]{:S(2)}) async-start(f32[8,128,128]{1,2,0:T(8,128)} %copy.35), calls=%async_computation.1 | async-start | bytes 1048576 | tf_op jit(solution)/shard_map/all_to_all | solution.py:37
  104.1 13.8 %all-to-all-done = f32[8,128,128]{1,2,0:T(8,128)S(1)} async-done(((f32[8,128,128]{1,2,0:T(8,128)}), f32[8,128,128]{1,2,0:T(8,128)S(1)}, u32[]{:S(2)}, u32[]{:S(2)}) %all-to-all-start) | async-done | bytes 524320 | tf_op jit(solution)/shard_map/all_to_all | solution.py:37
  117.9 0.8 copy.36
  119.5 14.3 %all-gather.24.cloned.1.call-done = bf16[32,128,128]{2,1,0:T(8,128)(2,1)} async-done(((bf16[8,128,128]{2,1,0:T(8,128)(2,1)}), bf16[32,128,128]{2,1,0:T(8,128)(2,1)}) %all-gather.24.cloned.1.call-update) | async-done | bytes 1048592 | tf_op jit(solution)/shard_map/all_gather | solution.py:46
  133.8 1.4 bitcast_convert_fusion
  135.2 1.4 copy.50
  136.6 1.9 reshape.41
  138.8 1.9 multiply_convert_fusion
  140.7 49.4 %all-gather.12.cloned.1.call-done = bf16[1024,1024]{1,0:T(8,128)(2,1)} async-done(((bf16[128,1024]{1,0:T(8,128)(2,1)}), bf16[1024,1024]{1,0:T(8,128)(2,1)}) %all-gather.12.cloned.1.call-update) | async-done | bytes 2097168 | tf_op jit(solution)/shard_map/all_gather | solution.py:65
  190.2 58.2 %all-gather.14.cloned.1.call-done = bf16[1024,4096]{1,0:T(8,128)(2,1)} async-done(((bf16[1024,1024]{1,0:T(8,128)(2,1)}), bf16[1024,4096]{1,0:T(8,128)(2,1)}) %all-gather.14.cloned.1.call-update) | async-done | bytes 8388624 | tf_op jit(solution)/shard_map/all_gather | solution.py:66
  248.4 5.4 %fusion.79 = (bf16[8,1,64,4096]{3,2,1,0:T(8,128)(2,1)S(1)}, bf16[8,1,64,4096]{3,2,1,0:T(8,128)(2,1)}) fusion(bf16[8,2,64,4096]{3,2,1,0:T(8,128)(2,1)} %bitcast.99), kind=kLoop, calls=%fused_computation.69 | loop fusion | bytes 16777216 | tf_op jit(solution)/shard_map/slice | solution.py:73
  254.6 2.3 fusion.22
  256.9 5.0 %fusion.69 = bf16[512,384]{1,0:T(8,128)(2,1)} fusion(bf16[512,4096]{1,0:T(8,128)(2,1)S(1)} %bitcast.107, bf16[2,384,4096]{2,1,0:T(8,128)(2,1)} %param.14, f32[512,384]{1,0:T(8,128)S(1)} %fusion.22), kind=kOutput, calls=%fused_computation.51 | convolution fusion | flops 1611792384 | bytes 8519680 | tf_op jit(solution)/shard_map/dot_general | solution.py:78
  262.0 5.6 %fusion.10 = f32[512,384]{1,0:T(8,128)S(1)} fusion(bf16[512,4096]{1,0:T(8,128)(2,1)} %bitcast.108, bf16[2,384,4096]{2,1,0:T(8,128)(2,1)} %param.13), kind=kOutput, calls=%fused_computation.10 | convolution fusion | flops 1610612736 | bytes 8126464 | tf_op jit(solution)/shard_map/dot_general | solution.py:77
  267.7 5.2 %fusion.63 = bf16[512,384]{1,0:T(8,128)(2,1)} fusion(bf16[512,4096]{1,0:T(8,128)(2,1)S(1)} %bitcast.109, bf16[2,384,4096]{2,1,0:T(8,128)(2,1)} %param.14, f32[512,384]{1,0:T(8,128)S(1)} %fusion.10), kind=kOutput, calls=%fused_computation.49 | convolution fusion | flops 1611792384 | bytes 8519680 | tf_op jit(solution)/shard_map/dot_general | solution.py:78
  273.1 5.7 %fusion.20 = f32[512,384]{1,0:T(8,128)S(1)} fusion(bf16[512,4096]{1,0:T(8,128)(2,1)} %bitcast.102, bf16[2,384,4096]{2,1,0:T(8,128)(2,1)} %param.13), kind=kOutput, calls=%fused_computation.20 | convolution fusion | flops 1610612736 | bytes 8126464 | tf_op jit(solution)/shard_map/dot_general | solution.py:77
  278.8 5.0 %fusion.66 = bf16[512,384]{1,0:T(8,128)(2,1)} fusion(bf16[512,4096]{1,0:T(8,128)(2,1)S(1)} %bitcast.104, bf16[2,384,4096]{2,1,0:T(8,128)(2,1)} %param.14, f32[512,384]{1,0:T(8,128)S(1)} %fusion.20), kind=kOutput, calls=%fused_computation.50 | convolution fusion | flops 1611792384 | bytes 8519680 | tf_op jit(solution)/shard_map/dot_general | solution.py:78
  283.9 5.6 %fusion.8 = f32[512,384]{1,0:T(8,128)S(1)} fusion(bf16[512,4096]{1,0:T(8,128)(2,1)} %bitcast.103, bf16[2,384,4096]{2,1,0:T(8,128)(2,1)} %param.13), kind=kOutput, calls=%fused_computation.8 | convolution fusion | flops 1610612736 | bytes 8126464 | tf_op jit(solution)/shard_map/dot_general | solution.py:77
  289.6 5.2 %fusion.60 = bf16[512,384]{1,0:T(8,128)(2,1)} fusion(bf16[512,4096]{1,0:T(8,128)(2,1)S(1)} %bitcast.105, bf16[2,384,4096]{2,1,0:T(8,128)(2,1)} %param.14, f32[512,384]{1,0:T(8,128)S(1)} %fusion.8), kind=kOutput, calls=%fused_computation.48 | convolution fusion | flops 1611792384 | bytes 8519680 | tf_op jit(solution)/shard_map/dot_general | solution.py:78
  295.2 30.5 %all_gather.33 = f32[16384]{0:T(1024)S(1)} all-gather(f32[2048]{0:T(1024)S(1)} %reshape.37), channel_id=1, replica_groups=mesh['expert'=8,'tensor'=4] {'expert'}, dimensions={0}, use_global_device_ids=true | all-gather | bytes 73728 | tf_op jit(solution)/shard_map/all_gather | solution.py:60
  326.5 4.2 fusion.36
  330.7 5.8 %select_add_fusion.1 = f32[512,1024]{1,0:T(8,128)} fusion(bf16[512,1024]{1,0:T(8,128)(2,1)S(1)} %fusion.36, bf16[512,1536]{1,0:T(8,128)(2,1)} %all-gather.18.cloned.1.call-done, bf16[2,1536,1024]{2,1,0:T(8,128)(2,1)} %param.15, f32[512]{0:T(512)S(1)} %bitcast.117, f32[512]{0:T(512)S(1)} %bitcast.115, pred[512]{0:T(512)(128)(4,1)S(1)} %get-tuple-element.15, ...), kind=kOutput, calls=%fused_computation.38 | convolution fusion | flops 1614807040 | bytes 7869440 | tf_op jit(solution)/shard_map/dot_general | solution.py:81
  337.3 4.2 fusion.39
  341.5 4.3 all-gather.22.cloned.1.call-done
  345.7 5.7 %select_add_fusion = f32[512,1024]{1,0:T(8,128)} fusion(bf16[512,1024]{1,0:T(8,128)(2,1)S(1)} %fusion.39, bf16[512,1536]{1,0:T(8,128)(2,1)} %all-gather.22.cloned.1.call-done, bf16[2,1536,1024]{2,1,0:T(8,128)(2,1)} %param.15, f32[512]{0:T(512)S(1)} %bitcast.118, f32[512]{0:T(512)S(1)} %bitcast.116, pred[512]{0:T(512)(128)(4,1)S(1)} %get-tuple-element.13, ...), kind=kOutput, calls=%fused_computation.37 | convolution fusion | flops 1614807040 | bytes 7869440 | tf_op jit(solution)/shard_map/dot_general | solution.py:81
  351.4 66.0 %reduce-scatter.6.cloned.1.call-done = f32[64,1024]{1,0:T(8,128)} async-done(((f32[512,1024]{1,0:T(8,128)}), f32[64,1024]{1,0:T(8,128)}) %reduce-scatter.6.cloned.1.call-update) | async-done | bytes 262160 | tf_op jit(solution)/shard_map/reduce_scatter | solution.py:86
  417.4 70.5 %reduce-scatter.8.cloned.1.call-done = f32[64,1024]{1,0:T(8,128)} async-done(((f32[512,1024]{1,0:T(8,128)}), f32[64,1024]{1,0:T(8,128)}) %reduce-scatter.8.cloned.1.call-update) | async-done | bytes 262160 | tf_op jit(solution)/shard_map/reduce_scatter | solution.py:86
  487.9 2.0 fusion.76
  (71 shorter events, 5.7 us)
Async XLA Ops:
  6.5 55.0 %copy-start = (bf16[1024,512]{1,0:T(8,128)(2,1)S(1)}, bf16[1024,512]{1,0:T(8,128)(2,1)}, u32[]{:S(2)}) copy-start(bf16[1024,512]{1,0:T(8,128)(2,1)} %param.10) | copy-start | bytes 3145732
  6.5 55.0 %all-gather.10.cloned.1.call-start = ((), (), s32[]{:S(2)}) async-start(), calls=%async_computation.4 | async-start | bytes 2359296 | tf_op jit(solution)/shard_map/all_gather | solution.py:34
  7.3 88.5 %reduce-scatter.4.cloned.1.call-start = ((), (), s32[]{:S(2)}) async-start(), calls=%async_computation.5 | async-start | bytes 2621440 | tf_op jit(solution)/shard_map/reduce_scatter | solution.py:36
  65.7 37.7 %copy-start.7 = (bf16[128,4096]{1,0:T(8,128)(2,1)S(1)}, bf16[128,4096]{1,0:T(8,128)(2,1)}, u32[]{:S(2)}) copy-start(bf16[128,4096]{1,0:T(8,128)(2,1)} %param.11) | copy-start | bytes 3145732
  97.8 20.0 %all-to-all-start = ((f32[8,128,128]{1,2,0:T(8,128)}), f32[8,128,128]{1,2,0:T(8,128)S(1)}, u32[]{:S(2)}, u32[]{:S(2)}) async-start(f32[8,128,128]{1,2,0:T(8,128)} %copy.35), calls=%async_computation.1 | async-start | bytes 1048576 | tf_op jit(solution)/shard_map/all_to_all | solution.py:37
  103.3 30.5 %all-gather.24.cloned.1.call-start = ((), (), s32[]{:S(2)}) async-start(), calls=%async_computation.14 | async-start | bytes 1310720 | tf_op jit(solution)/shard_map/all_gather | solution.py:46
  118.8 71.3 %all-gather.12.cloned.1.call-start = ((), (), s32[]{:S(2)}) async-start(), calls=%async_computation.6 | async-start | bytes 2359296 | tf_op jit(solution)/shard_map/all_gather | solution.py:65
  136.6 1.9 copy-start.2
  140.7 107.7 %all-gather.14.cloned.1.call-start = ((), (), s32[]{:S(2)}) async-start(), calls=%async_computation.7 | async-start | bytes 10485760 | tf_op jit(solution)/shard_map/all_gather | solution.py:66
  190.1 63.7 %slice-start = ((s8[6291456]{0:T(1024)(128)(4,1)}), s8[2097152]{0:T(1024)(128)(4,1)S(1)}, s32[]{:S(2)}) async-start(s8[6291456]{0:T(1024)(128)(4,1)} %bitcast.119), calls=%async_computation.15 | async-start | bytes 4194304
  190.1 136.4 %all-gather.16.cloned.1.call-start = ((), (), s32[]{:S(2)}) async-start(), calls=%async_computation.8 | async-start | bytes 1966080 | tf_op jit(solution)/shard_map/all_gather | solution.py:80
  248.4 6.2 %slice-start.1 = ((s8[6291456]{0:T(1024)(128)(4,1)}), s8[4194304]{0:T(1024)(128)(4,1)S(1)}, s32[]{:S(2)}) async-start(s8[6291456]{0:T(1024)(128)(4,1)} %bitcast.119), calls=%async_computation.16 | async-start | bytes 8388608
  253.8 3.1 copy-start.5
  262.0 68.7 %all-gather.18.cloned.1.call-start = ((), (), s32[]{:S(2)}) async-start(), calls=%async_computation.9 | async-start | bytes 1966080 | tf_op jit(solution)/shard_map/all_gather | solution.py:80
  262.0 5.7 %copy-start.6 = (bf16[8,1,64,4096]{3,2,1,0:T(8,128)(2,1)S(1)}, bf16[8,1,64,4096]{3,2,1,0:T(8,128)(2,1)}, u32[]{:S(2)}) copy-start(bf16[8,1,64,4096]{3,2,1,0:T(8,128)(2,1)} %copy-done.5) | copy-start | bytes 12582916
  272.9 64.4 %all-gather.20.cloned.1.call-start = ((), (), s32[]{:S(2)}) async-start(), calls=%async_computation.11 | async-start | bytes 1966080 | tf_op jit(solution)/shard_map/all_gather | solution.py:80
  273.1 5.7 %copy-start.3 = (bf16[8,1,64,4096]{3,2,1,0:T(8,128)(2,1)S(1)}, bf16[8,1,64,4096]{3,2,1,0:T(8,128)(2,1)}, u32[]{:S(2)}) copy-start(bf16[8,1,64,4096]{3,2,1,0:T(8,128)(2,1)} %get-tuple-element.6) | copy-start | bytes 12582916
  283.9 61.9 %all-gather.22.cloned.1.call-start = ((), (), s32[]{:S(2)}) async-start(), calls=%async_computation.12 | async-start | bytes 1966080 | tf_op jit(solution)/shard_map/all_gather | solution.py:80
  283.9 5.7 %copy-start.4 = (bf16[8,1,64,4096]{3,2,1,0:T(8,128)(2,1)S(1)}, bf16[8,1,64,4096]{3,2,1,0:T(8,128)(2,1)}, u32[]{:S(2)}) copy-start(bf16[8,1,64,4096]{3,2,1,0:T(8,128)(2,1)} %get-tuple-element.6) | copy-start | bytes 12582916
  289.6 5.3 %copy-start.8 = (f32[128,8]{0,1:T(8,128)S(1)}, f32[128,8]{0,1:T(8,128)}, u32[]{:S(2)}) copy-start(f32[128,8]{0,1:T(8,128)} %param.17) | copy-start | bytes 12292
  289.6 5.4 %copy-start.9 = (s32[128,8]{0,1:T(8,128)S(1)}, s32[128,8]{0,1:T(8,128)}, u32[]{:S(2)}) copy-start(s32[128,8]{0,1:T(8,128)} %param.16) | copy-start | bytes 12292
  294.9 122.6 %reduce-scatter.6.cloned.1.call-start = ((), (), s32[]{:S(2)}) async-start(), calls=%async_computation.10 | async-start | bytes 2359296 | tf_op jit(solution)/shard_map/reduce_scatter | solution.py:86
  336.6 151.4 %reduce-scatter.8.cloned.1.call-start = ((), (), s32[]{:S(2)}) async-start(), calls=%async_computation.13 | async-start | bytes 2359296 | tf_op jit(solution)/shard_map/reduce_scatter | solution.py:86
  345.7 144.2 %copy-start.1 = (bf16[1024,512]{1,0:T(8,128)(2,1)S(1)}, bf16[1024,512]{1,0:T(8,128)(2,1)}, u32[]{:S(2)}) copy-start(bf16[1024,512]{1,0:T(8,128)(2,1)} %param.10) | copy-start | bytes 3145732
Sparse Core Ops, SparseCore 0:
  9.5 51.9 all-gather.9
  65.8 29.9 reduce-scatter.3
  118.9 14.8 all-gather.23
  140.8 49.2 all-gather.11
  191.6 56.7 all-gather.13
  262.1 19.6 all-gather.15
  283.4 19.6 all-gather.17
  304.7 19.6 all-gather.19
  326.1 19.6 all-gather.21
  349.5 67.8 reduce-scatter.5
  421.4 66.5 reduce-scatter.7

commit v3 on v2

--- a/solution.py
+++ b/solution.py
@@ -4,7 +4,7 @@
 from jax.sharding import PartitionSpec as P
 
 EPS = 1e-06
-CHUNKS = 2
+CHUNKS = 1
 
 
 def on_device(
@@ -57,13 +57,23 @@
     hit_src = expert_ids[:, :, None] == jnp.arange(experts_all, dtype=jnp.int32)[None, None, :]
     weights = gate_scores / jnp.sum(gate_scores, axis=1, keepdims=True)
     w_src = jnp.sum(jnp.where(hit_src, weights[:, :, None], 0.0), axis=1)
-    w_all = lax.all_gather(w_src.reshape(-1), "expert", axis=0, tiled=True).reshape(
-        all_tok, experts_all
+    hi = w_src.astype(jnp.bfloat16)
+    rest = w_src - hi.astype(jnp.float32)
+    mid = rest.astype(jnp.bfloat16)
+    lo = (rest - mid.astype(jnp.float32)).astype(jnp.bfloat16)
+    coded = jnp.stack([hi, mid, lo]).reshape(-1)
+    extra = -(-coded.shape[0] // (share * 8)) * 8
+    coded = jnp.pad(coded, (0, extra * share - coded.shape[0])).reshape(extra, share)
+    packet = jnp.concatenate([normed_q, coded], axis=0)
+
+    got = lax.all_gather(packet, ("expert", "tensor"), axis=0, tiled=False).reshape(
+        groups, tensor_ways, tok_count + extra, share
     )
+    rows = jnp.transpose(got[:, :, :tok_count], (0, 2, 1, 3)).reshape(all_tok, width)
+    parts = got[:, 0, tok_count:].reshape(groups, -1)[:, : 3 * tok_count * experts_all]
+    parts = parts.reshape(groups, 3, tok_count, experts_all).astype(jnp.float32)
+    w_all = (parts[:, 0] + parts[:, 1] + parts[:, 2]).reshape(all_tok, experts_all)
     w_mine = lax.dynamic_slice_in_dim(w_all, me_e * exp_local, exp_local, 1)
-
-    rows_q = lax.all_gather(normed_q, "expert", axis=0, tiled=True)
-    rows = lax.all_gather(rows_q, "tensor", axis=1, tiled=True)
 
     chunk = tok_count // CHUNKS
     rows_c = rows.reshape(groups, CHUNKS, chunk, width)

time: 497 us -> 421 us (0.85)
  waiting for transfers between devices: 362 us -> 309 us
  blocking collectives: 30.5 us -> 0 us
  local copies, waits for them, and re-layouts: 14.3 us -> 30.1 us
  matrix products: 63.7 us -> 53.9 us
    reduce_scatter x2 -> x1, waiting for transfers between devices: 137 us -> 88.2 us  [on_device(): lax.psum_scatter(total, 'expert', scatter_dimension=0, tiled=True)]
    all_gather x1 -> x0, blocking collectives: 30.5 us -> none  [on_device(): lax.all_gather(w_src.reshape(-1), 'expert', axis=0, tiled=True)]
    all_gather x2 -> x1, waiting for transfers between devices: 108 us -> 79.6 us  [on_device(): lax.all_gather(packet, ('expert', 'tensor'), axis=0, tiled=False)]
    all_gather x4 -> x2, waiting for transfers between devices: 4.35 us -> 28 us  [on_device(): act_all = lax.all_gather(act, 'tensor', axis=1, tiled=True)]
    unnamed x29 -> x22, local copies, waits for them, and re-layouts: 1.9 us -> 14.6 us
    dot_general x4 -> x2, matrix products: 20.4 us -> 15.4 us  [on_device(): upper = jnp.dot(x, up_proj[loc].T, preferred_element_type=jnp.float32)]
    dot_general x4 -> x2, matrix products: 19.8 us -> 16.6 us  [on_device(): jnp.dot(act_all, down_proj[loc], preferred_element_type=jnp.float32)]
    dot_general x4 -> x2, matrix products: 19.3 us -> 17.8 us  [on_device(): gate = jnp.dot(x, gate_proj[loc].T, preferred_element_type=jnp.float32)]
  transfers between devices with their start and end apart: 12 -> 8, of which waited for: 9 -> 8; matrix products, arithmetic and copies ran while one was open for 11% -> 7% of each run, Pallas kernels for 0% -> 0%
where the time goes in v3:
time: 421 us; the launch traced here: 420 us
  waiting for transfers between devices  309 us (73%)
  matrix products  53.9 us (13%)
  local copies, waits for them, and re-layouts  30.1 us (7%)
  between operations  13.7 us (3%)
  other arithmetic  7.79 us (2%)
  starting transfers between devices  6.39 us (2%)
    reduce_scatter x1, waiting for transfers between devices, on_device(): lax.psum_scatter(total, 'expert', scatter_dimension=0, tiled=True)  88.2 us
    all_gather x1, waiting for transfers between devices, on_device(): lax.all_gather(packet, ('expert', 'tensor'), axis=0, tiled=False)  79.6 us
    all_gather x1, waiting for transfers between devices, on_device(): heads_all = lax.all_gather(attn_heads, 'expert', axis=0, tiled=True)  54.2 us
    reduce_scatter x1, waiting for transfers between devices, on_device(): lax.psum_scatter(partial, 'tensor', scatter_dimension=1, tiled=True)  30.1 us
    all_gather x2, waiting for transfers between devices, on_device(): act_all = lax.all_gather(act, 'tensor', axis=1, tiled=True)  28 us
    dot_general x2, matrix products, on_device(): gate = jnp.dot(x, gate_proj[loc].T, preferred_element_type=jnp.float32)  17.8 us
    dot_general x2, matrix products, on_device(): jnp.dot(act_all, down_proj[loc], preferred_element_type=jnp.float32)  16.6 us
    dot_general x2, matrix products, on_device(): upper = jnp.dot(x, up_proj[loc].T, preferred_element_type=jnp.float32)  15.4 us
  transfers between devices with their start and end apart: 8, of which 8 were waited for; matrix products, arithmetic and copies ran while one was open for 7% of the time, Pallas kernels for 0%

profile of v3, /device:TPU:0, one launch (start us, length us, event | category | flops | bytes accessed | tf_op | source)
XLA Modules:
  0.0 420.4 jit_solution(1289982820169816218)
XLA Ops:
  6.5 0.7 all-gather.8.cloned.1.call-update
  7.3 54.2 %all-gather.8.cloned.1.call-done = bf16[1024,1024]{1,0:T(8,128)(2,1)} async-done(((bf16[128,1024]{1,0:T(8,128)(2,1)}), bf16[1024,1024]{1,0:T(8,128)(2,1)}) %all-gather.8.cloned.1.call-update) | async-done | bytes 2097168 | tf_op jit(solution)/shard_map/all_gather | solution.py:34
  61.5 4.2 fusion.39
  65.7 30.1 %reduce-scatter.3.cloned.1.call-done = f32[1024,128]{1,0:T(8,128)} async-done(((f32[1024,512]{1,0:T(8,128)}), f32[1024,128]{1,0:T(8,128)}) %reduce-scatter.3.cloned.1.call-update) | async-done | bytes 524304 | tf_op jit(solution)/shard_map/reduce_scatter | solution.py:36
  95.8 2.0 copy.36
  97.8 5.5 %all-to-all-start = ((f32[8,128,128]{1,2,0:T(8,128)}), f32[8,128,128]{1,2,0:T(8,128)S(1)}, u32[]{:S(2)}, u32[]{:S(2)}) async-start(f32[8,128,128]{1,2,0:T(8,128)} %copy.36), calls=%async_computation.1 | async-start | bytes 1048576 | tf_op jit(solution)/shard_map/all_to_all | solution.py:37
  103.4 0.7 copy.35
  104.0 13.8 %all-to-all-done = f32[8,128,128]{1,2,0:T(8,128)S(1)} async-done(((f32[8,128,128]{1,2,0:T(8,128)}), f32[8,128,128]{1,2,0:T(8,128)S(1)}, u32[]{:S(2)}, u32[]{:S(2)}) %all-to-all-start) | async-done | bytes 524320 | tf_op jit(solution)/shard_map/all_to_all | solution.py:37
  117.9 0.8 copy.37
  119.2 0.7 dynamic-slice_convert_fusion
  119.9 13.9 %all-gather.14.cloned.1.call-done = bf16[32,128,128]{2,1,0:T(8,128)(2,1)} async-done(((bf16[8,128,128]{2,1,0:T(8,128)(2,1)}), bf16[32,128,128]{2,1,0:T(8,128)(2,1)}) %all-gather.14.cloned.1.call-update) | async-done | bytes 1048592 | tf_op jit(solution)/shard_map/all_gather | solution.py:46
  133.8 1.5 multiply_reduce_fusion
  135.3 1.5 bitcast_convert_fusion.1
  136.8 1.4 copy.69
  138.1 1.8 reshape.79
  140.0 1.1 multiply_convert_fusion.2
  141.1 0.7 pad_maximum_fusion
  142.1 79.6 %all-gather.16.cloned.1.call-done = bf16[4352,1024]{1,0:T(8,128)(2,1)} async-done(((bf16[136,1024]{1,0:T(8,128)(2,1)}), bf16[4352,1024]{1,0:T(8,128)(2,1)}) %all-gather.16.cloned.1.call-update) | async-done | bytes 8912912 | tf_op jit(solution)/shard_map/all_gather | solution.py:69
  221.7 8.3 %slice.61 = bf16[8,4,128,1024]{3,2,1,0:T(8,128)(2,1)} slice(bf16[8,4,136,1024]{3,2,1,0:T(8,128)(2,1)} %bitcast.89), slice={[0:8], [0:4], [0:128], [0:1024]} | slice | bytes 16777216 | tf_op jit(solution)/shard_map/slice | solution.py:72
  230.0 12.5 %copy.44 = bf16[8,4,128,1024]{2,0,3,1:T(8,128)(2,1)} copy(bf16[8,4,128,1024]{3,2,1,0:T(8,128)(2,1)} %slice.61) | data formatting | bytes 16777216
  242.5 9.0 %fusion.2 = f32[1024,384]{1,0:T(8,128)S(1)} fusion(bf16[512,8,8,128]{3,2,1,0:T(8,128)(2,1)} %bitcast.84, bf16[2,384,4096]{2,1,0:T(8,128)(2,1)} %param.13), kind=kOutput, calls=%fused_computation.2 | convolution fusion | flops 3221225472 | bytes 13107200 | tf_op jit(solution)/shard_map/dot_general | solution.py:87
  251.5 5.5 %multiply_convert_fusion = bf16[1024,384]{1,0:T(8,128)(2,1)} fusion(f32[1024,384]{1,0:T(8,128)S(1)} %fusion.2, bf16[2,384,4096]{2,1,0:T(8,128)(2,1)S(1)} %bitcast.99, bf16[512,8,8,128]{3,2,1,0:T(8,128)(2,1)S(1)} %bitcast.87), kind=kOutput, calls=%fused_computation.29 | convolution fusion | flops 3223584768 | bytes 13893632 | tf_op jit(solution)/shard_map/dot_general | solution.py:88
  257.3 8.8 %fusion.6 = f32[1024,384]{1,0:T(8,128)S(1)} fusion(bf16[512,8,8,128]{3,2,1,0:T(8,128)(2,1)} %bitcast.85, bf16[2,384,4096]{2,1,0:T(8,128)(2,1)} %param.13), kind=kOutput, calls=%fused_computation.6 | convolution fusion | flops 3221225472 | bytes 13107200 | tf_op jit(solution)/shard_map/dot_general | solution.py:87
  266.1 9.8 %multiply_convert_fusion.1 = bf16[1024,384]{1,0:T(8,128)(2,1)} fusion(f32[1024,384]{1,0:T(8,128)S(1)} %fusion.6, bf16[2,384,4096]{2,1,0:T(8,128)(2,1)} %param.14, bf16[512,8,8,128]{3,2,1,0:T(8,128)(2,1)} %bitcast.86), kind=kOutput, calls=%fused_computation.30 | convolution fusion | flops 3223584768 | bytes 13893632 | tf_op jit(solution)/shard_map/dot_general | solution.py:88
  276.3 0.9 slice_bitcast_fusion
  277.3 0.5 reshape.80
  278.7 5.6 %all-gather.12.cloned.1.call-done = bf16[1024,1536]{1,0:T(8,128)(2,1)} async-done(((bf16[1024,384]{1,0:T(8,128)(2,1)}), bf16[1024,1536]{1,0:T(8,128)(2,1)}) %all-gather.12.cloned.1.call-update) | async-done | bytes 3145744 | tf_op jit(solution)/shard_map/all_gather | solution.py:90
  284.3 7.6 %fusion.12 = bf16[1024,1024]{1,0:T(8,128)(2,1)} fusion(bf16[1024,1536]{1,0:T(8,128)(2,1)} %all-gather.12.cloned.1.call-done, bf16[2,1536,1024]{2,1,0:T(8,128)(2,1)} %param.15), kind=kOutput, calls=%fused_computation.13 | convolution fusion | flops 3221225472 | bytes 8388608 | tf_op jit(solution)/shard_map/dot_general | solution.py:91
  291.9 22.4 %all-gather.10.cloned.1.call-done = bf16[1024,1536]{1,0:T(8,128)(2,1)} async-done(((bf16[1024,384]{1,0:T(8,128)(2,1)}), bf16[1024,1536]{1,0:T(8,128)(2,1)}) %all-gather.10.cloned.1.call-update) | async-done | bytes 3145744 | tf_op jit(solution)/shard_map/all_gather | solution.py:90
  314.3 9.0 %select_add_fusion = f32[1024,1024]{1,0:T(8,128)} fusion(bf16[1024,1024]{1,0:T(8,128)(2,1)} %fusion.12, f32[1024]{0:T(1024)S(1)} %bitcast.97, f32[1024]{0:T(1024)S(1)} %bitcast.96, pred[1024]{0:T(1024)(128)(4,1)S(1)} %get-tuple-element.9, pred[1024]{0:T(1024)(128)(4,1)S(1)} %get-tuple-element.10, bf16[1024,1536]{1,0:T(8,128)(2,1)} %all-gather.10.cloned.1.call-done, ...), kind=kOutput, calls=%fused_computation.12 | convolution fusion | flops 3229614080 | bytes 12593152 | tf_op jit(solution)/shard_map/dot_general | solution.py:91
  323.4 88.2 %reduce-scatter.5.cloned.1.call-done = f32[128,1024]{1,0:T(8,128)} async-done(((f32[1024,1024]{1,0:T(8,128)}), f32[128,1024]{1,0:T(8,128)}) %reduce-scatter.5.cloned.1.call-update) | async-done | bytes 524304 | tf_op jit(solution)/shard_map/reduce_scatter | solution.py:96
  411.6 2.0 add_convert_fusion
  (49 shorter events, 2.4 us)
Async XLA Ops:
  6.5 55.0 %copy-start = (bf16[1024,512]{1,0:T(8,128)(2,1)S(1)}, bf16[1024,512]{1,0:T(8,128)(2,1)}, u32[]{:S(2)}) copy-start(bf16[1024,512]{1,0:T(8,128)(2,1)} %param.10) | copy-start | bytes 3145732
  6.5 55.0 %all-gather.8.cloned.1.call-start = ((), (), s32[]{:S(2)}) async-start(), calls=%async_computation.3 | async-start | bytes 2359296 | tf_op jit(solution)/shard_map/all_gather | solution.py:34
  7.3 88.5 %reduce-scatter.3.cloned.1.call-start = ((), (), s32[]{:S(2)}) async-start(), calls=%async_computation.4 | async-start | bytes 2621440 | tf_op jit(solution)/shard_map/reduce_scatter | solution.py:36
  65.7 37.7 %copy-start.3 = (bf16[128,4096]{1,0:T(8,128)(2,1)S(1)}, bf16[128,4096]{1,0:T(8,128)(2,1)}, u32[]{:S(2)}) copy-start(bf16[128,4096]{1,0:T(8,128)(2,1)} %param.11) | copy-start | bytes 3145732
  65.7 53.1 %copy-start.4 = (f32[128,8]{0,1:T(8,128)S(1)}, f32[128,8]{0,1:T(8,128)}, u32[]{:S(2)}) copy-start(f32[128,8]{0,1:T(8,128)} %param.17) | copy-start | bytes 12292
  65.7 53.1 %copy-start.5 = (s32[128,8]{0,1:T(8,128)S(1)}, s32[128,8]{0,1:T(8,128)}, u32[]{:S(2)}) copy-start(s32[128,8]{0,1:T(8,128)} %param.16) | copy-start | bytes 12292
  97.8 20.0 %all-to-all-start = ((f32[8,128,128]{1,2,0:T(8,128)}), f32[8,128,128]{1,2,0:T(8,128)S(1)}, u32[]{:S(2)}, u32[]{:S(2)}) async-start(f32[8,128,128]{1,2,0:T(8,128)} %copy.36), calls=%async_computation.1 | async-start | bytes 1048576 | tf_op jit(solution)/shard_map/all_to_all | solution.py:37
  103.3 30.5 %all-gather.14.cloned.1.call-start = ((), (), s32[]{:S(2)}) async-start(), calls=%async_computation.8 | async-start | bytes 1310720 | tf_op jit(solution)/shard_map/all_gather | solution.py:46
  118.8 102.9 %all-gather.16.cloned.1.call-start = ((), (), s32[]{:S(2)}) async-start(), calls=%async_computation.9 | async-start | bytes 9191424 | tf_op jit(solution)/shard_map/all_gather | solution.py:69
  141.9 142.4 %all-gather.12.cloned.1.call-start = ((), (), s32[]{:S(2)}) async-start(), calls=%async_computation.6 | async-start | bytes 3932160 | tf_op jit(solution)/shard_map/all_gather | solution.py:90
  230.0 21.5 %slice-start = ((s8[6291456]{0:T(1024)(128)(4,1)}), s8[2097152]{0:T(1024)(128)(4,1)S(1)}, s32[]{:S(2)}) async-start(s8[6291456]{0:T(1024)(128)(4,1)} %bitcast.98), calls=%async_computation.10 | async-start | bytes 4194304
  242.5 9.0 %copy-start.2 = (bf16[8,4,128,1024]{2,0,3,1:T(8,128)(2,1)S(1)}, bf16[8,4,128,1024]{2,0,3,1:T(8,128)(2,1)}, u32[]{:S(2)}) copy-start(bf16[8,4,128,1024]{2,0,3,1:T(8,128)(2,1)} %copy.44) | copy-start | bytes 25165828
  242.5 9.0 %slice-start.1 = ((s8[6291456]{0:T(1024)(128)(4,1)}), s8[4194304]{0:T(1024)(128)(4,1)S(1)}, s32[]{:S(2)}) async-start(s8[6291456]{0:T(1024)(128)(4,1)} %bitcast.98), calls=%async_computation.11 | async-start | bytes 8388608
  257.0 57.3 %all-gather.10.cloned.1.call-start = ((), (), s32[]{:S(2)}) async-start(), calls=%async_computation.5 | async-start | bytes 3932160 | tf_op jit(solution)/shard_map/all_gather | solution.py:90
  276.0 135.7 %reduce-scatter.5.cloned.1.call-start = ((), (), s32[]{:S(2)}) async-start(), calls=%async_computation.7 | async-start | bytes 4718592 | tf_op jit(solution)/shard_map/reduce_scatter | solution.py:96
  314.3 99.3 %copy-start.1 = (bf16[1024,512]{1,0:T(8,128)(2,1)S(1)}, bf16[1024,512]{1,0:T(8,128)(2,1)}, u32[]{:S(2)}) copy-start(bf16[1024,512]{1,0:T(8,128)(2,1)} %param.10) | copy-start | bytes 3145732
Sparse Core Ops, SparseCore 0:
  9.5 51.9 all-gather.7
  65.8 29.9 reduce-scatter.2
  118.9 14.8 all-gather.13
  142.0 79.6 all-gather.15
  257.2 27.0 all-gather.11
  285.8 28.4 all-gather.9
  323.5 88.0 reduce-scatter.4

commit v4 on v1

--- a/solution.py
+++ b/solution.py
@@ -30,8 +30,28 @@
     me_t = lax.axis_index("tensor")
     all_tok = groups * tok_count
 
-    heads_all = lax.all_gather(attn_heads, "expert", axis=0, tiled=True)
-    partial = jnp.dot(heads_all, out_proj, preferred_element_type=jnp.float32)
+    experts_all = groups * exp_local
+    hit_src = expert_ids[:, :, None] == jnp.arange(experts_all, dtype=jnp.int32)[None, None, :]
+    weights = gate_scores / jnp.sum(gate_scores, axis=1, keepdims=True)
+    w_src = jnp.sum(jnp.where(hit_src, weights[:, :, None], 0.0), axis=1)
+    hi = w_src.astype(jnp.bfloat16)
+    rest = w_src - hi.astype(jnp.float32)
+    mid = rest.astype(jnp.bfloat16)
+    lo = (rest - mid.astype(jnp.float32)).astype(jnp.bfloat16)
+    coded = jnp.stack([hi, mid, lo]).reshape(-1)
+    heads_w = attn_heads.shape[1]
+    extra = -(-coded.shape[0] // (heads_w * 8)) * 8
+    coded = jnp.pad(coded, (0, extra * heads_w - coded.shape[0])).reshape(extra, heads_w)
+    packet = jnp.concatenate([attn_heads, coded], axis=0)
+
+    got = lax.all_gather(packet, "expert", axis=0, tiled=False)
+    partial = jnp.einsum(
+        "enh,hc->enc", got[:, :tok_count], out_proj, preferred_element_type=jnp.float32
+    ).reshape(all_tok, cols_e)
+    parts = got[:, tok_count:].reshape(groups, -1)[:, : 3 * tok_count * experts_all]
+    parts = parts.reshape(groups, 3, tok_count, experts_all).astype(jnp.float32)
+    w_all = (parts[:, 0] + parts[:, 1] + parts[:, 2]).reshape(all_tok, experts_all)
+    w_mine = lax.dynamic_slice_in_dim(w_all, me_e * exp_local, exp_local, 1)
     summed = lax.psum_scatter(partial, "tensor", scatter_dimension=1, tiled=True)
     mine = lax.all_to_all(
         summed.reshape(groups, tok_count, cols_et), "expert", 0, 0, tiled=False
@@ -52,32 +72,33 @@
     gain_q = lax.dynamic_slice_in_dim(norm_gain, me_t * share, share, 0).astype(jnp.float32)
     normed_q = (state_q * scale * gain_q).astype(jnp.bfloat16)
 
-    rows_q = lax.all_gather(normed_q, "expert", axis=0, tiled=True)
-    rows = lax.all_gather(rows_q, "tensor", axis=0, tiled=False)
-
-    ids_all = lax.all_gather(expert_ids, "expert", axis=0, tiled=True)
-    scores_all = lax.all_gather(gate_scores, "expert", axis=0, tiled=True)
-    weights = scores_all / jnp.sum(scores_all, axis=1, keepdims=True)
+    slabs = lax.all_gather(normed_q, ("tensor", "expert"), axis=0, tiled=False).reshape(
+        tensor_ways, all_tok, share
+    )
 
     total = jnp.zeros((all_tok, share), jnp.float32)
     for loc in range(exp_local):
-        glob = me_e * exp_local + loc
-        hit = ids_all == glob
-        w_tok = jnp.sum(jnp.where(hit, weights, 0.0), axis=1)
-        chosen = jnp.any(hit, axis=1)
-        gmat = gate_proj[loc].reshape(hidden_local, tensor_ways, share)
-        umat = up_proj[loc].reshape(hidden_local, tensor_ways, share)
-        gate = jnp.einsum("ard,fad->rf", rows, gmat, preferred_element_type=jnp.float32)
-        upper = jnp.einsum("ard,fad->rf", rows, umat, preferred_element_type=jnp.float32)
+        gate = None
+        upper = None
+        for a in range(tensor_ways):
+            x = slabs[a]
+            gpart = jnp.dot(
+                x, gate_proj[loc, :, a * share : (a + 1) * share].T,
+                preferred_element_type=jnp.float32,
+            )
+            upart = jnp.dot(
+                x, up_proj[loc, :, a * share : (a + 1) * share].T,
+                preferred_element_type=jnp.float32,
+            )
+            gate = gpart if gate is None else gate + gpart
+            upper = upart if upper is None else upper + upart
         act = (jax.nn.silu(gate) * upper).astype(jnp.bfloat16)
-        act_all = lax.all_gather(act, "tensor", axis=0, tiled=False)
-        dmat = down_proj[loc].reshape(tensor_ways, hidden_local, share)
-        out = jnp.einsum(
-            "arf,afd->rd", act_all, dmat, preferred_element_type=jnp.float32
+        act_all = lax.all_gather(act, "tensor", axis=1, tiled=True)
+        out = jnp.dot(
+            act_all, down_proj[loc], preferred_element_type=jnp.float32
         ).astype(jnp.bfloat16)
-        total = total + jnp.where(
-            chosen[:, None], w_tok[:, None] * out.astype(jnp.float32), 0.0
-        )
+        w_tok = w_mine[:, loc][:, None]
+        total = total + jnp.where(w_tok > 0, w_tok * out.astype(jnp.float32), 0.0)
     mixture = lax.psum_scatter(total, "expert", scatter_dimension=0, tiled=True)
     state_out = lax.dynamic_slice_in_dim(state_f, me_t * share, share, 1)
     return (state_out + mixture).astype(jnp.bfloat16)

time: 467 us -> 407 us (0.87)
  blocking collectives: 61.1 us -> 0 us
  local copies, waits for them, and re-layouts: 41.9 us -> 9.31 us
  waiting for transfers between devices: 287 us -> 302 us
  matrix products: 49.4 us -> 64.1 us
    all_gather x2 -> x0, blocking collectives: 61.1 us -> none  [the longest x1 30.6 us: on_device(): scores_all = lax.all_gather(gate_scores, 'expert', axis=0, tiled=True)]
    slice x3 -> x1, local copies, waits for them, and re-layouts: 17.7 us -> 0.34 us  [on_device(): w_tok = w_mine[:, loc][:, None]]
    unnamed x23 -> x19, local copies, waits for them, and re-layouts: 18.1 us -> 2.06 us
    all_gather x5 -> x4, waiting for transfers between devices: 140 us -> 155 us  [the longest x1 77.3 us: on_device(): lax.all_gather(normed_q, ('tensor', 'expert'), axis=0, tiled=False)]
    dot_general x7 -> x19, matrix products: 49.4 us -> 64.1 us  [the longest x8 26.1 us: on_device(): jnp.dot(x, up_proj[loc, :, a * share:(a + 1) * share].T, preferred_elemen...]
  transfers between devices with their start and end apart: 9 -> 8, of which waited for: 7 -> 8; matrix products, arithmetic and copies ran while one was open for 13% -> 8% of each run, Pallas kernels for 0% -> 0%
where the time goes in v4:
time: 407 us; the launch traced here: 406 us
  waiting for transfers between devices  302 us (74%)
  matrix products  64.1 us (16%)
  between operations  13.7 us (3%)
  other arithmetic  10.3 us (3%)
  local copies, waits for them, and re-layouts  9.31 us (2%)
  starting transfers between devices  6.42 us (2%)
    reduce_scatter x1, waiting for transfers between devices, on_device(): mixture = lax.psum_scatter(total, 'expert', scatter_dimension=0, tiled=True)  88.2 us
    all_gather x1, waiting for transfers between devices, on_device(): lax.all_gather(normed_q, ('tensor', 'expert'), axis=0, tiled=False)  77.3 us
    all_gather x1, waiting for transfers between devices, on_device(): got = lax.all_gather(packet, 'expert', axis=0, tiled=False)  53.5 us
    reduce_scatter x1, waiting for transfers between devices, on_device(): lax.psum_scatter(partial, 'tensor', scatter_dimension=1, tiled=True)  30.1 us
    dot_general x8, matrix products, on_device(): jnp.dot(x, up_proj[loc, :, a * share:(a + 1) * share].T, preferred_elemen...  26.1 us
    all_gather x2, waiting for transfers between devices, on_device(): act_all = lax.all_gather(act, 'tensor', axis=1, tiled=True)  24.7 us
    dot_general x8, matrix products, on_device(): jnp.dot(x, gate_proj[loc, :, a * share:(a + 1) * share].T, preferred_elem...  19.2 us
    dot_general x2, matrix products, on_device(): jnp.dot(act_all, down_proj[loc], preferred_element_type=jnp.float32)  14.6 us
  transfers between devices with their start and end apart: 8, of which 8 were waited for; matrix products, arithmetic and copies ran while one was open for 8% of the time, Pallas kernels for 0%

profile of v4, /device:TPU:0, one launch (start us, length us, event | category | flops | bytes accessed | tf_op | source)
XLA Modules:
  0.0 405.9 jit_solution(17852189625332232553)
XLA Ops:
  9.1 1.7 pad_maximum_fusion
  10.8 53.5 %all-gather.13.cloned.1.call-done = bf16[1088,1024]{1,0:T(8,128)(2,1)} async-done(((bf16[136,1024]{1,0:T(8,128)(2,1)}), bf16[1088,1024]{1,0:T(8,128)(2,1)}) %all-gather.13.cloned.1.call-update) | async-done | bytes 2228240 | tf_op jit(solution)/shard_map/all_gather | solution.py:47
  64.3 4.2 %fusion.7 = f32[8,128,512]{2,1,0:T(8,128)} fusion(bf16[8,136,1024]{2,1,0:T(8,128)(2,1)} %bitcast.106, bf16[1024,512]{1,0:T(8,128)(2,1)S(1)} %copy-done), kind=kOutput, calls=%fused_computation.10 | convolution fusion | flops 1073741824 | bytes 5242880 | tf_op jit(solution)/shard_map/enh,hc->enc/dot_general | solution.py:48
  68.5 30.1 %reduce-scatter.3.cloned.1.call-done = f32[1024,128]{1,0:T(8,128)} async-done(((f32[1024,512]{1,0:T(8,128)}), f32[1024,128]{1,0:T(8,128)}) %reduce-scatter.3.cloned.1.call-update) | async-done | bytes 524304 | tf_op jit(solution)/shard_map/reduce_scatter | solution.py:55
  98.6 2.0 copy.40
  100.6 5.5 %all-to-all-start = ((f32[8,128,128]{1,2,0:T(8,128)}), f32[8,128,128]{1,2,0:T(8,128)S(1)}, u32[]{:S(2)}, u32[]{:S(2)}) async-start(f32[8,128,128]{1,2,0:T(8,128)} %copy.40), calls=%async_computation.1 | async-start | bytes 1048576 | tf_op jit(solution)/shard_map/all_to_all | solution.py:56
  106.8 13.8 %all-to-all-done = f32[8,128,128]{1,2,0:T(8,128)S(1)} async-done(((f32[8,128,128]{1,2,0:T(8,128)}), f32[8,128,128]{1,2,0:T(8,128)S(1)}, u32[]{:S(2)}, u32[]{:S(2)}) %all-to-all-start) | async-done | bytes 524320 | tf_op jit(solution)/shard_map/all_to_all | solution.py:56
  122.3 14.3 %all-gather.15.cloned.1.call-done = bf16[32,128,128]{2,1,0:T(8,128)(2,1)} async-done(((bf16[8,128,128]{2,1,0:T(8,128)(2,1)}), bf16[32,128,128]{2,1,0:T(8,128)(2,1)}) %all-gather.15.cloned.1.call-update) | async-done | bytes 1048592 | tf_op jit(solution)/shard_map/all_gather | solution.py:65
  139.4 1.9 reshape.92
  141.6 1.9 multiply_convert_fusion.2
  143.7 77.3 %all-gather.17.cloned.1.call-done = bf16[4096,1024]{1,0:T(8,128)(2,1)} async-done(((bf16[128,1024]{1,0:T(8,128)(2,1)}), bf16[4096,1024]{1,0:T(8,128)(2,1)}) %all-gather.17.cloned.1.call-update) | async-done | bytes 8388624 | tf_op jit(solution)/shard_map/all_gather | solution.py:75
  221.0 3.2 fusion.23
  224.2 3.1 fusion.39
  227.3 2.4 fusion.31
  229.7 2.4 fusion.11
  232.1 2.4 fusion.17
  234.5 2.4 fusion.33
  236.9 2.4 fusion.25
  239.4 3.8 multiply_convert_fusion
  243.5 3.2 fusion.19
  246.7 3.4 fusion.35
  250.1 3.2 fusion.27
  253.3 2.4 fusion.14
  255.7 2.4 fusion.21
  258.1 2.4 fusion.37
  260.5 2.4 fusion.29
  262.9 3.8 multiply_convert_fusion.1
  270.4 6.3 %fusion = bf16[1024,1024]{1,0:T(8,128)(2,1)S(1)} fusion(bf16[1024,1536]{1,0:T(8,128)(2,1)} %all-gather.11.cloned.1.call-done, bf16[2,1536,1024]{2,1,0:T(8,128)(2,1)} %param.15), kind=kOutput, calls=%fused_computation.1 | convolution fusion | flops 3221225472 | bytes 8388608 | tf_op jit(solution)/shard_map/dot_general | solution.py:97
  276.7 23.8 %all-gather.9.cloned.1.call-done = bf16[1024,1536]{1,0:T(8,128)(2,1)} async-done(((bf16[1024,384]{1,0:T(8,128)(2,1)}), bf16[1024,1536]{1,0:T(8,128)(2,1)}) %all-gather.9.cloned.1.call-update) | async-done | bytes 3145744 | tf_op jit(solution)/shard_map/all_gather | solution.py:96
  300.4 8.4 %select_add_fusion = f32[1024,1024]{1,0:T(8,128)} fusion(bf16[1024,1024]{1,0:T(8,128)(2,1)S(1)} %fusion, f32[1024]{0:T(1024)S(1)} %bitcast.104, f32[1024]{0:T(1024)S(1)} %bitcast.105, pred[1024]{0:T(1024)(128)(4,1)S(1)} %get-tuple-element.9, pred[1024]{0:T(1024)(128)(4,1)S(1)} %get-tuple-element.10, bf16[1024,1536]{1,0:T(8,128)(2,1)} %all-gather.9.cloned.1.call-done, ...), kind=kOutput, calls=%fused_computation | convolution fusion | flops 3229614080 | bytes 12593152 | tf_op jit(solution)/shard_map/dot_general | solution.py:97
  308.8 88.2 %reduce-scatter.5.cloned.1.call-done = f32[128,1024]{1,0:T(8,128)} async-done(((f32[1024,1024]{1,0:T(8,128)}), f32[128,1024]{1,0:T(8,128)}) %reduce-scatter.5.cloned.1.call-update) | async-done | bytes 524304 | tf_op jit(solution)/shard_map/reduce_scatter | solution.py:102
  397.1 2.0 add_convert_fusion
  (57 shorter events, 12.2 us)
Async XLA Ops:
  6.5 57.7 %copy-start = (bf16[1024,512]{1,0:T(8,128)(2,1)S(1)}, bf16[1024,512]{1,0:T(8,128)(2,1)}, u32[]{:S(2)}) copy-start(bf16[1024,512]{1,0:T(8,128)(2,1)} %param.10) | copy-start | bytes 3145732
  6.5 57.7 %all-gather.13.cloned.1.call-start = ((), (), s32[]{:S(2)}) async-start(), calls=%async_computation.7 | async-start | bytes 2506752 | tf_op jit(solution)/shard_map/all_gather | solution.py:47
  10.8 87.8 %reduce-scatter.3.cloned.1.call-start = ((), (), s32[]{:S(2)}) async-start(), calls=%async_computation.3 | async-start | bytes 2621440 | tf_op jit(solution)/shard_map/reduce_scatter | solution.py:55
  68.5 37.7 %copy-start.3 = (bf16[128,4096]{1,0:T(8,128)(2,1)S(1)}, bf16[128,4096]{1,0:T(8,128)(2,1)}, u32[]{:S(2)}) copy-start(bf16[128,4096]{1,0:T(8,128)(2,1)} %param.11) | copy-start | bytes 3145732
  100.6 20.0 %all-to-all-start = ((f32[8,128,128]{1,2,0:T(8,128)}), f32[8,128,128]{1,2,0:T(8,128)S(1)}, u32[]{:S(2)}, u32[]{:S(2)}) async-start(f32[8,128,128]{1,2,0:T(8,128)} %copy.40), calls=%async_computation.1 | async-start | bytes 1048576 | tf_op jit(solution)/shard_map/all_to_all | solution.py:56
  106.1 30.5 %all-gather.15.cloned.1.call-start = ((), (), s32[]{:S(2)}) async-start(), calls=%async_computation.8 | async-start | bytes 1310720 | tf_op jit(solution)/shard_map/all_gather | solution.py:65
  121.6 99.5 %all-gather.17.cloned.1.call-start = ((), (), s32[]{:S(2)}) async-start(), calls=%async_computation.9 | async-start | bytes 8650752 | tf_op jit(solution)/shard_map/all_gather | solution.py:75
  139.4 1.9 copy-start.2
  143.4 127.0 %all-gather.11.cloned.1.call-start = ((), (), s32[]{:S(2)}) async-start(), calls=%async_computation.5 | async-start | bytes 3932160 | tf_op jit(solution)/shard_map/all_gather | solution.py:96
  221.0 6.3 %copy-start.4 = (bf16[4096,1024]{1,0:T(8,128)(2,1)S(1)}, bf16[4096,1024]{1,0:T(8,128)(2,1)}, u32[]{:S(2)}) copy-start(bf16[4096,1024]{1,0:T(8,128)(2,1)} %all-gather.17.cloned.1.call-done) | copy-start | bytes 25165828
  243.2 57.3 %all-gather.9.cloned.1.call-start = ((), (), s32[]{:S(2)}) async-start(), calls=%async_computation.4 | async-start | bytes 3932160 | tf_op jit(solution)/shard_map/all_gather | solution.py:96
  243.4 9.8 %slice-start = ((s8[8388608]{0:T(1024)(128)(4,1)}), s8[4194304]{0:T(1024)(128)(4,1)S(1)}, s32[]{:S(2)}) async-start(s8[8388608]{0:T(1024)(128)(4,1)} %bitcast.108), calls=%async_computation.10 | async-start | bytes 8388608
  246.6 6.6 %slice-start.1 = ((s8[8388608]{0:T(1024)(128)(4,1)}), s8[4194304]{0:T(1024)(128)(4,1)S(1)}, s32[]{:S(2)}) async-start(s8[8388608]{0:T(1024)(128)(4,1)} %bitcast.108), calls=%async_computation.11 | async-start | bytes 8388608
  266.7 130.3 %reduce-scatter.5.cloned.1.call-start = ((), (), s32[]{:S(2)}) async-start(), calls=%async_computation.6 | async-start | bytes 4718592 | tf_op jit(solution)/shard_map/reduce_scatter | solution.py:102
  308.8 90.2 %copy-start.1 = (bf16[1024,512]{1,0:T(8,128)(2,1)S(1)}, bf16[1024,512]{1,0:T(8,128)(2,1)}, u32[]{:S(2)}) copy-start(bf16[1024,512]{1,0:T(8,128)(2,1)} %param.10) | copy-start | bytes 3145732
Sparse Core Ops, SparseCore 0:
  10.9 53.3 all-gather.12
  68.6 29.9 reduce-scatter.2
  121.7 14.8 all-gather.14
  143.6 77.4 all-gather.16
  243.3 27.0 all-gather.10
  271.9 28.4 all-gather.8
  309.0 88.0 reduce-scatter.4

commit v5 on v4

--- a/solution.py
+++ b/solution.py
@@ -99,7 +99,9 @@
         ).astype(jnp.bfloat16)
         w_tok = w_mine[:, loc][:, None]
         total = total + jnp.where(w_tok > 0, w_tok * out.astype(jnp.float32), 0.0)
-    mixture = lax.psum_scatter(total, "expert", scatter_dimension=0, tiled=True)
+    mixture = lax.psum_scatter(
+        total.astype(jnp.bfloat16), "expert", scatter_dimension=0, tiled=True
+    ).astype(jnp.float32)
     state_out = lax.dynamic_slice_in_dim(state_f, me_t * share, share, 1)
     return (state_out + mixture).astype(jnp.bfloat16)
 

time: 407 us -> 387 us (0.951)
  waiting for transfers between devices: 302 us -> 280 us
    reduce_scatter x1, waiting for transfers between devices: 88.2 us -> 68.1 us  [on_device(): lax.psum_scatter(total.astype(jnp.bfloat16), 'expert', scatter_dimension=...]
  transfers between devices with their start and end apart: 8 -> 8, of which waited for: 8 -> 8; matrix products, arithmetic and copies ran while one was open for 8% -> 9% of each run, Pallas kernels for 0% -> 0%
where the time goes in v5:
time: 387 us; the launch traced here: 386 us
  waiting for transfers between devices  280 us (72%)
  matrix products  65.8 us (17%)
  between operations  13.7 us (4%)
  other arithmetic  10.3 us (3%)
  local copies, waits for them, and re-layouts  9.31 us (2%)
  starting transfers between devices  6.42 us (2%)
    all_gather x1, waiting for transfers between devices, on_device(): lax.all_gather(normed_q, ('tensor', 'expert'), axis=0, tiled=False)  77.3 us
    reduce_scatter x1, waiting for transfers between devices, on_device(): lax.psum_scatter(total.astype(jnp.bfloat16), 'expert', scatter_dimension=...  68.1 us
    all_gather x1, waiting for transfers between devices, on_device(): got = lax.all_gather(packet, 'expert', axis=0, tiled=False)  53.5 us
    reduce_scatter x1, waiting for transfers between devices, on_device(): lax.psum_scatter(partial, 'tensor', scatter_dimension=1, tiled=True)  30.1 us
    dot_general x8, matrix products, on_device(): jnp.dot(x, up_proj[loc, :, a * share:(a + 1) * share].T, preferred_elemen...  26.1 us
    all_gather x2, waiting for transfers between devices, on_device(): act_all = lax.all_gather(act, 'tensor', axis=1, tiled=True)  23.2 us
    dot_general x8, matrix products, on_device(): jnp.dot(x, gate_proj[loc, :, a * share:(a + 1) * share].T, preferred_elem...  19.2 us
    dot_general x2, matrix products, on_device(): jnp.dot(act_all, down_proj[loc], preferred_element_type=jnp.float32)  16.3 us
  transfers between devices with their start and end apart: 8, of which 8 were waited for; matrix products, arithmetic and copies ran while one was open for 9% of the time, Pallas kernels for 0%

profile of v5, /device:TPU:0, one launch (start us, length us, event | category | flops | bytes accessed | tf_op | source)
XLA Modules:
  0.0 385.9 jit_solution(10271021394509519939)
XLA Ops:
  9.1 1.7 pad_maximum_fusion
  10.8 53.5 %all-gather.13.cloned.1.call-done = bf16[1088,1024]{1,0:T(8,128)(2,1)} async-done(((bf16[136,1024]{1,0:T(8,128)(2,1)}), bf16[1088,1024]{1,0:T(8,128)(2,1)}) %all-gather.13.cloned.1.call-update) | async-done | bytes 2228240 | tf_op jit(solution)/shard_map/all_gather | solution.py:47
  64.3 4.2 %fusion.7 = f32[8,128,512]{2,1,0:T(8,128)} fusion(bf16[8,136,1024]{2,1,0:T(8,128)(2,1)} %bitcast.106, bf16[1024,512]{1,0:T(8,128)(2,1)S(1)} %copy-done), kind=kOutput, calls=%fused_computation.10 | convolution fusion | flops 1073741824 | bytes 5242880 | tf_op jit(solution)/shard_map/enh,hc->enc/dot_general | solution.py:48
  68.5 30.1 %reduce-scatter.3.cloned.1.call-done = f32[1024,128]{1,0:T(8,128)} async-done(((f32[1024,512]{1,0:T(8,128)}), f32[1024,128]{1,0:T(8,128)}) %reduce-scatter.3.cloned.1.call-update) | async-done | bytes 524304 | tf_op jit(solution)/shard_map/reduce_scatter | solution.py:55
  98.6 2.0 copy.40
  100.6 5.5 %all-to-all-start = ((f32[8,128,128]{1,2,0:T(8,128)}), f32[8,128,128]{1,2,0:T(8,128)S(1)}, u32[]{:S(2)}, u32[]{:S(2)}) async-start(f32[8,128,128]{1,2,0:T(8,128)} %copy.40), calls=%async_computation.1 | async-start | bytes 1048576 | tf_op jit(solution)/shard_map/all_to_all | solution.py:56
  106.8 13.8 %all-to-all-done = f32[8,128,128]{1,2,0:T(8,128)S(1)} async-done(((f32[8,128,128]{1,2,0:T(8,128)}), f32[8,128,128]{1,2,0:T(8,128)S(1)}, u32[]{:S(2)}, u32[]{:S(2)}) %all-to-all-start) | async-done | bytes 524320 | tf_op jit(solution)/shard_map/all_to_all | solution.py:56
  122.3 14.3 %all-gather.15.cloned.1.call-done = bf16[32,128,128]{2,1,0:T(8,128)(2,1)} async-done(((bf16[8,128,128]{2,1,0:T(8,128)(2,1)}), bf16[32,128,128]{2,1,0:T(8,128)(2,1)}) %all-gather.15.cloned.1.call-update) | async-done | bytes 1048592 | tf_op jit(solution)/shard_map/all_gather | solution.py:65
  139.4 1.9 reshape.92
  141.6 1.9 multiply_convert_fusion.2
  143.7 77.3 %all-gather.17.cloned.1.call-done = bf16[4096,1024]{1,0:T(8,128)(2,1)} async-done(((bf16[128,1024]{1,0:T(8,128)(2,1)}), bf16[4096,1024]{1,0:T(8,128)(2,1)}) %all-gather.17.cloned.1.call-update) | async-done | bytes 8388624 | tf_op jit(solution)/shard_map/all_gather | solution.py:75
  221.0 3.2 fusion.23
  224.2 3.1 fusion.39
  227.3 2.4 fusion.31
  229.7 2.4 fusion.11
  232.1 2.4 fusion.17
  234.5 2.4 fusion.33
  236.9 2.4 fusion.25
  239.4 3.8 multiply_convert_fusion
  243.5 3.2 fusion.19
  246.7 3.4 fusion.35
  250.1 3.2 fusion.27
  253.3 2.4 fusion.14
  255.7 2.4 fusion.21
  258.1 2.4 fusion.37
  260.5 2.4 fusion.29
  262.9 3.8 multiply_convert_fusion.1
  270.4 7.7 %fusion = bf16[1024,1024]{1,0:T(8,128)(2,1)} fusion(bf16[1024,1536]{1,0:T(8,128)(2,1)} %all-gather.11.cloned.1.call-done, bf16[2,1536,1024]{2,1,0:T(8,128)(2,1)} %param.15), kind=kOutput, calls=%fused_computation.1 | convolution fusion | flops 3221225472 | bytes 8388608 | tf_op jit(solution)/shard_map/dot_general | solution.py:97
  278.1 22.3 %all-gather.9.cloned.1.call-done = bf16[1024,1536]{1,0:T(8,128)(2,1)} async-done(((bf16[1024,384]{1,0:T(8,128)(2,1)}), bf16[1024,1536]{1,0:T(8,128)(2,1)}) %all-gather.9.cloned.1.call-update) | async-done | bytes 3145744 | tf_op jit(solution)/shard_map/all_gather | solution.py:96
  300.4 8.6 %add_convert_fusion = bf16[1024,1024]{1,0:T(8,128)(2,1)} fusion(bf16[1024,1024]{1,0:T(8,128)(2,1)} %fusion, f32[1024]{0:T(1024)S(1)} %bitcast.104, f32[1024]{0:T(1024)S(1)} %bitcast.105, pred[1024]{0:T(1024)(128)(4,1)S(1)} %get-tuple-element.9, pred[1024]{0:T(1024)(128)(4,1)S(1)} %get-tuple-element.10, bf16[1024,1536]{1,0:T(8,128)(2,1)} %all-gather.9.cloned.1.call-done, ...), kind=kOutput, calls=%fused_computation | convolution fusion | flops 3230662656 | bytes 10496000 | tf_op jit(solution)/shard_map/dot_general | solution.py:97
  309.1 68.1 %reduce-scatter.5.cloned.1.call-done = bf16[128,1024]{1,0:T(8,128)(2,1)} async-done(((bf16[1024,1024]{1,0:T(8,128)(2,1)}), bf16[128,1024]{1,0:T(8,128)(2,1)}) %reduce-scatter.5.cloned.1.call-update) | async-done | bytes 262160 | tf_op jit(solution)/shard_map/reduce_scatter | solution.py:102
  377.1 1.9 add_convert_fusion.1
  (57 shorter events, 12.2 us)
Async XLA Ops:
  6.5 57.7 %copy-start = (bf16[1024,512]{1,0:T(8,128)(2,1)S(1)}, bf16[1024,512]{1,0:T(8,128)(2,1)}, u32[]{:S(2)}) copy-start(bf16[1024,512]{1,0:T(8,128)(2,1)} %param.10) | copy-start | bytes 3145732
  6.5 57.7 %all-gather.13.cloned.1.call-start = ((), (), s32[]{:S(2)}) async-start(), calls=%async_computation.7 | async-start | bytes 2506752 | tf_op jit(solution)/shard_map/all_gather | solution.py:47
  10.8 87.8 %reduce-scatter.3.cloned.1.call-start = ((), (), s32[]{:S(2)}) async-start(), calls=%async_computation.3 | async-start | bytes 2621440 | tf_op jit(solution)/shard_map/reduce_scatter | solution.py:55
  68.5 37.7 %copy-start.3 = (bf16[128,4096]{1,0:T(8,128)(2,1)S(1)}, bf16[128,4096]{1,0:T(8,128)(2,1)}, u32[]{:S(2)}) copy-start(bf16[128,4096]{1,0:T(8,128)(2,1)} %param.11) | copy-start | bytes 3145732
  100.6 20.0 %all-to-all-start = ((f32[8,128,128]{1,2,0:T(8,128)}), f32[8,128,128]{1,2,0:T(8,128)S(1)}, u32[]{:S(2)}, u32[]{:S(2)}) async-start(f32[8,128,128]{1,2,0:T(8,128)} %copy.40), calls=%async_computation.1 | async-start | bytes 1048576 | tf_op jit(solution)/shard_map/all_to_all | solution.py:56
  106.1 30.5 %all-gather.15.cloned.1.call-start = ((), (), s32[]{:S(2)}) async-start(), calls=%async_computation.8 | async-start | bytes 1310720 | tf_op jit(solution)/shard_map/all_gather | solution.py:65
  121.6 99.5 %all-gather.17.cloned.1.call-start = ((), (), s32[]{:S(2)}) async-start(), calls=%async_computation.9 | async-start | bytes 8650752 | tf_op jit(solution)/shard_map/all_gather | solution.py:75
  139.4 1.9 copy-start.2
  143.4 127.0 %all-gather.11.cloned.1.call-start = ((), (), s32[]{:S(2)}) async-start(), calls=%async_computation.5 | async-start | bytes 3932160 | tf_op jit(solution)/shard_map/all_gather | solution.py:96
  221.0 6.3 %copy-start.4 = (bf16[4096,1024]{1,0:T(8,128)(2,1)S(1)}, bf16[4096,1024]{1,0:T(8,128)(2,1)}, u32[]{:S(2)}) copy-start(bf16[4096,1024]{1,0:T(8,128)(2,1)} %all-gather.17.cloned.1.call-done) | copy-start | bytes 25165828
  243.2 57.3 %all-gather.9.cloned.1.call-start = ((), (), s32[]{:S(2)}) async-start(), calls=%async_computation.4 | async-start | bytes 3932160 | tf_op jit(solution)/shard_map/all_gather | solution.py:96
  243.4 9.8 %slice-start = ((s8[8388608]{0:T(1024)(128)(4,1)}), s8[4194304]{0:T(1024)(128)(4,1)S(1)}, s32[]{:S(2)}) async-start(s8[8388608]{0:T(1024)(128)(4,1)} %bitcast.108), calls=%async_computation.10 | async-start | bytes 8388608
  246.6 6.6 %slice-start.1 = ((s8[8388608]{0:T(1024)(128)(4,1)}), s8[4194304]{0:T(1024)(128)(4,1)S(1)}, s32[]{:S(2)}) async-start(s8[8388608]{0:T(1024)(128)(4,1)} %bitcast.108), calls=%async_computation.11 | async-start | bytes 8388608
  266.8 110.4 %reduce-scatter.5.cloned.1.call-start = ((), (), s32[]{:S(2)}) async-start(), calls=%async_computation.6 | async-start | bytes 2359296 | tf_op jit(solution)/shard_map/reduce_scatter | solution.py:102
  300.4 78.6 %copy-start.1 = (bf16[1024,512]{1,0:T(8,128)(2,1)S(1)}, bf16[1024,512]{1,0:T(8,128)(2,1)}, u32[]{:S(2)}) copy-start(bf16[1024,512]{1,0:T(8,128)(2,1)} %param.10) | copy-start | bytes 3145732
Sparse Core Ops, SparseCore 0:
  10.9 53.3 all-gather.12
  68.6 29.9 reduce-scatter.2
  121.7 14.8 all-gather.14
  143.6 77.4 all-gather.16
  243.3 27.0 all-gather.10
  271.9 28.4 all-gather.8
  309.2 67.9 reduce-scatter.4

commit v6 on v4

--- a/solution.py
+++ b/solution.py
@@ -99,7 +99,13 @@
         ).astype(jnp.bfloat16)
         w_tok = w_mine[:, loc][:, None]
         total = total + jnp.where(w_tok > 0, w_tok * out.astype(jnp.float32), 0.0)
-    mixture = lax.psum_scatter(total, "expert", scatter_dimension=0, tiled=True)
+    blocks = total.reshape(groups, tok_count, share)
+    mixture = lax.dynamic_index_in_dim(blocks, me_e, 0, keepdims=False)
+    for s in range(1, groups):
+        dest = lax.rem(me_e + s, groups)
+        sent = lax.dynamic_index_in_dim(blocks, dest, 0, keepdims=False)
+        perm = [(i, (i + s) % groups) for i in range(groups)]
+        mixture = mixture + lax.ppermute(sent, "expert", perm)
     state_out = lax.dynamic_slice_in_dim(state_f, me_t * share, share, 1)
     return (state_out + mixture).astype(jnp.bfloat16)
 

time: 407 us -> 428 us (1.052)
  waiting for transfers between devices: 302 us -> 315 us
  local copies, waits for them, and re-layouts: 9.31 us -> 20.9 us
  matrix products: 64.1 us -> 53.3 us
  starting transfers between devices: 6.42 us -> 13.8 us
    reduce_scatter x1 -> x0, waiting for transfers between devices: 88.2 us -> none  [on_device(): mixture = lax.psum_scatter(total, 'expert', scatter_dimension=0, tiled=True)]
    ppermute x0 -> x7, waiting for transfers between devices: none -> 82.2 us  [on_device(): mixture = mixture + lax.ppermute(sent, 'expert', perm)]
    all_gather x1, waiting for transfers between devices: 77.3 us -> 92.2 us  [on_device(): lax.all_gather(normed_q, ('tensor', 'expert'), axis=0, tiled=False)]
    dynamic_slice x0 -> x9, local copies, waits for them, and re-layouts: none -> 10.8 us  [the longest x7 9.15 us: on_device(): sent = lax.dynamic_index_in_dim(blocks, dest, 0, keepdims=False)]
    dot_general x8, matrix products: 19.2 us -> 10.4 us  [on_device(): jnp.dot(x, gate_proj[loc, :, a * share:(a + 1) * share].T, preferred_elem...]
    ppermute x0 -> x7, starting transfers between devices: none -> 7.72 us  [on_device(): mixture = mixture + lax.ppermute(sent, 'expert', perm)]
  transfers between devices with their start and end apart: 8 -> 14, of which waited for: 8 -> 12; matrix products, arithmetic and copies ran while one was open for 8% -> 9% of each run, Pallas kernels for 0% -> 0%
where the time goes in v6:
time: 428 us; the launch traced here: 427 us
  waiting for transfers between devices  315 us (74%)
  matrix products  53.3 us (12%)
  local copies, waits for them, and re-layouts  20.9 us (5%)
  starting transfers between devices  13.8 us (3%)
  between operations  13.8 us (3%)
  other arithmetic  10.5 us (2%)
    all_gather x1, waiting for transfers between devices, on_device(): lax.all_gather(normed_q, ('tensor', 'expert'), axis=0, tiled=False)  92.2 us
    ppermute x7, waiting for transfers between devices, on_device(): mixture = mixture + lax.ppermute(sent, 'expert', perm)  82.2 us
    all_gather x1, waiting for transfers between devices, on_device(): got = lax.all_gather(packet, 'expert', axis=0, tiled=False)  53.5 us
    reduce_scatter x1, waiting for transfers between devices, on_device(): lax.psum_scatter(partial, 'tensor', scatter_dimension=1, tiled=True)  30.1 us
    all_gather x2, waiting for transfers between devices, on_device(): act_all = lax.all_gather(act, 'tensor', axis=1, tiled=True)  28.5 us
    dot_general x8, matrix products, on_device(): jnp.dot(x, up_proj[loc, :, a * share:(a + 1) * share].T, preferred_elemen...  25.8 us
    all_gather x1, waiting for transfers between devices, on_device(): state_all = lax.all_gather(state_ct, 'tensor', axis=0, tiled=False)  14.3 us
    all_to_all x1, waiting for transfers between devices, on_device(): lax.all_to_all(summed.reshape(groups, tok_count, cols_et), 'expert', 0, 0...  13.8 us
  transfers between devices with their start and end apart: 14, of which 12 were waited for; matrix products, arithmetic and copies ran while one was open for 9% of the time, Pallas kernels for 0%

profile of v6, /device:TPU:0, one launch (start us, length us, event | category | flops | bytes accessed | tf_op | source)
XLA Modules:
  0.0 426.9 jit_solution(609521266359278580)
XLA Ops:
  10.8 53.5 %all-gather.13.cloned.1.call-done = bf16[1088,1024]{1,0:T(8,128)(2,1)} async-done(((bf16[136,1024]{1,0:T(8,128)(2,1)}), bf16[1088,1024]{1,0:T(8,128)(2,1)}) %all-gather.13.cloned.1.call-update) | async-done | bytes 2228240 | tf_op jit(solution)/shard_map/all_gather | solution.py:47
  64.3 4.2 fusion.7
  68.5 30.1 %reduce-scatter.2.cloned.1.call-done = f32[1024,128]{1,0:T(8,128)} async-done(((f32[1024,512]{1,0:T(8,128)}), f32[1024,128]{1,0:T(8,128)}) %reduce-scatter.2.cloned.1.call-update) | async-done | bytes 524304 | tf_op jit(solution)/shard_map/reduce_scatter | solution.py:55
  98.6 2.1 copy.66
  100.7 5.5 %all-to-all-start = ((f32[8,128,128]{1,2,0:T(8,128)}), f32[8,128,128]{1,2,0:T(8,128)S(1)}, u32[]{:S(2)}, u32[]{:S(2)}) async-start(f32[8,128,128]{1,2,0:T(8,128)} %copy.66), calls=%async_computation.1 | async-start | bytes 1048576 | tf_op jit(solution)/shard_map/all_to_all | solution.py:56
  106.9 13.8 %all-to-all-done = f32[8,128,128]{1,2,0:T(8,128)S(1)} async-done(((f32[8,128,128]{1,2,0:T(8,128)}), f32[8,128,128]{1,2,0:T(8,128)S(1)}, u32[]{:S(2)}, u32[]{:S(2)}) %all-to-all-start) | async-done | bytes 524320 | tf_op jit(solution)/shard_map/all_to_all | solution.py:56
  122.3 14.3 %all-gather.15.cloned.1.call-done = bf16[32,128,128]{2,1,0:T(8,128)(2,1)} async-done(((bf16[8,128,128]{2,1,0:T(8,128)(2,1)}), bf16[32,128,128]{2,1,0:T(8,128)(2,1)}) %all-gather.15.cloned.1.call-update) | async-done | bytes 1048592 | tf_op jit(solution)/shard_map/all_gather | solution.py:65
  138.1 1.8 copy.68
  140.2 2.0 multiply_convert_fusion.2
  142.4 92.2 %all-gather.17.cloned.1.call-done = bf16[4096,1024]{0,1:T(8,128)(2,1)} async-done(((bf16[128,1024]{0,1:T(8,128)(2,1)}), bf16[4096,1024]{0,1:T(8,128)(2,1)}) %all-gather.17.cloned.1.call-update) | async-done | bytes 8388624 | tf_op jit(solution)/shard_map/all_gather | solution.py:75
  234.6 3.2 fusion.23
  238.9 2.6 fusion.39
  241.5 2.6 fusion.31
  249.3 3.8 multiply_convert_fusion
  253.5 3.2 fusion.19
  256.7 3.4 fusion.35
  260.4 3.0 fusion.27
  268.7 3.9 multiply_convert_fusion.1
  275.0 5.0 %all-gather.11.cloned.1.call-done = bf16[1024,1536]{1,0:T(8,128)(2,1)} async-done(((bf16[1024,384]{1,0:T(8,128)(2,1)}), bf16[1024,1536]{1,0:T(8,128)(2,1)}) %all-gather.11.cloned.1.call-update) | async-done | bytes 3145744 | tf_op jit(solution)/shard_map/all_gather | solution.py:96
  280.0 6.5 %fusion = bf16[1024,1024]{1,0:T(8,128)(2,1)S(1)} fusion(bf16[1024,1536]{1,0:T(8,128)(2,1)} %all-gather.11.cloned.1.call-done, bf16[2,1536,1024]{2,1,0:T(8,128)(2,1)} %param.15), kind=kOutput, calls=%fused_computation.1 | convolution fusion | flops 3221225472 | bytes 8388608 | tf_op jit(solution)/shard_map/dot_general | solution.py:97
  286.5 23.5 %all-gather.9.cloned.1.call-done = bf16[1024,1536]{1,0:T(8,128)(2,1)} async-done(((bf16[1024,384]{1,0:T(8,128)(2,1)}), bf16[1024,1536]{1,0:T(8,128)(2,1)}) %all-gather.9.cloned.1.call-update) | async-done | bytes 3145744 | tf_op jit(solution)/shard_map/all_gather | solution.py:96
  310.0 6.4 %select_add_fusion = f32[1024,1024]{1,0:T(8,128)S(1)} fusion(bf16[1024,1024]{1,0:T(8,128)(2,1)S(1)} %fusion, f32[1024]{0:T(1024)S(1)} %bitcast.139, f32[1024]{0:T(1024)S(1)} %bitcast.140, pred[1024]{0:T(1024)(128)(4,1)S(1)} %get-tuple-element.17, pred[1024]{0:T(1024)(128)(4,1)S(1)} %get-tuple-element.18, bf16[1024,1536]{1,0:T(8,128)(2,1)} %all-gather.9.cloned.1.call-done, ...), kind=kOutput, calls=%fused_computation | convolution fusion | flops 3229614080 | bytes 12593152 | tf_op jit(solution)/shard_map/dot_general | solution.py:97
  317.9 2.0 copy.77
  320.0 4.2 collective-permute-start.6
  324.2 2.1 copy.76
  328.8 2.9 collective-permute-start.3
  334.8 2.1 collective-permute-done.6
  336.9 11.2 %collective-permute-done.5 = f32[128,1024]{0,1:T(8,128)} collective-permute-done((f32[128,1024]{0,1:T(8,128)}, f32[128,1024]{0,1:T(8,128)}, u32[]{:S(2)}, u32[]{:S(2)}) %collective-permute-start.5) | collective-permute-done | bytes 524320 | tf_op jit(solution)/shard_map/ppermute | solution.py:108
  348.3 11.1 %collective-permute-done.4 = f32[128,1024]{0,1:T(8,128)S(1)} collective-permute-done((f32[128,1024]{0,1:T(8,128)}, f32[128,1024]{0,1:T(8,128)S(1)}, u32[]{:S(2)}, u32[]{:S(2)}) %collective-permute-start.4) | collective-permute-done | bytes 524320 | tf_op jit(solution)/shard_map/ppermute | solution.py:108
  359.4 55.3 %collective-permute-done.3 = f32[128,1024]{0,1:T(8,128)S(1)} collective-permute-done((f32[128,1024]{0,1:T(8,128)}, f32[128,1024]{0,1:T(8,128)S(1)}, u32[]{:S(2)}, u32[]{:S(2)}) %collective-permute-start.3) | collective-permute-done | bytes 524320 | tf_op jit(solution)/shard_map/ppermute | solution.py:108
  414.7 2.4 collective-permute-done.2
  417.2 2.0 fusion.83
  (87 shorter events, 31.1 us)
Async XLA Ops:
  6.5 57.7 %copy-start = (bf16[1024,512]{1,0:T(8,128)(2,1)S(1)}, bf16[1024,512]{1,0:T(8,128)(2,1)}, u32[]{:S(2)}) copy-start(bf16[1024,512]{1,0:T(8,128)(2,1)} %param.10) | copy-start | bytes 3145732
  6.5 57.7 %all-gather.13.cloned.1.call-start = ((), (), s32[]{:S(2)}) async-start(), calls=%async_computation.5 | async-start | bytes 2506752 | tf_op jit(solution)/shard_map/all_gather | solution.py:47
  10.8 87.8 %reduce-scatter.2.cloned.1.call-start = ((), (), s32[]{:S(2)}) async-start(), calls=%async_computation.2 | async-start | bytes 2621440 | tf_op jit(solution)/shard_map/reduce_scatter | solution.py:55
  68.5 37.7 %copy-start.3 = (bf16[128,4096]{1,0:T(8,128)(2,1)S(1)}, bf16[128,4096]{1,0:T(8,128)(2,1)}, u32[]{:S(2)}) copy-start(bf16[128,4096]{1,0:T(8,128)(2,1)} %param.11) | copy-start | bytes 3145732
  100.7 20.0 %all-to-all-start = ((f32[8,128,128]{1,2,0:T(8,128)}), f32[8,128,128]{1,2,0:T(8,128)S(1)}, u32[]{:S(2)}, u32[]{:S(2)}) async-start(f32[8,128,128]{1,2,0:T(8,128)} %copy.66), calls=%async_computation.1 | async-start | bytes 1048576 | tf_op jit(solution)/shard_map/all_to_all | solution.py:56
  106.2 30.5 %all-gather.15.cloned.1.call-start = ((), (), s32[]{:S(2)}) async-start(), calls=%async_computation.6 | async-start | bytes 1310720 | tf_op jit(solution)/shard_map/all_gather | solution.py:65
  121.6 113.0 %all-gather.17.cloned.1.call-start = ((), (), s32[]{:S(2)}) async-start(), calls=%async_computation.7 | async-start | bytes 8650752 | tf_op jit(solution)/shard_map/all_gather | solution.py:75
  138.1 1.8 copy-start.2
  142.2 137.8 %all-gather.11.cloned.1.call-start = ((), (), s32[]{:S(2)}) async-start(), calls=%async_computation.4 | async-start | bytes 3932160 | tf_op jit(solution)/shard_map/all_gather | solution.py:96
  234.6 4.3 copy-start.4
  238.9 5.2 %slice-start.2 = ((s8[6291456]{0:T(1024)(128)(4,1)}), s8[4194304]{0:T(1024)(128)(4,1)S(1)}, s32[]{:S(2)}) async-start(s8[6291456]{0:T(1024)(128)(4,1)} %bitcast.145), calls=%async_computation.10 | async-start | bytes 8388608
  241.5 2.6 slice-start.3
  253.2 56.8 %all-gather.9.cloned.1.call-start = ((), (), s32[]{:S(2)}) async-start(), calls=%async_computation.3 | async-start | bytes 3932160 | tf_op jit(solution)/shard_map/all_gather | solution.py:96
  253.4 6.7 %slice-start = ((s8[8388608]{0:T(1024)(128)(4,1)}), s8[4194304]{0:T(1024)(128)(4,1)S(1)}, s32[]{:S(2)}) async-start(s8[8388608]{0:T(1024)(128)(4,1)} %bitcast.143), calls=%async_computation.8 | async-start | bytes 8388608
  256.7 3.7 slice-start.1
  256.7 6.8 %slice-start.4 = ((s8[6291456]{0:T(1024)(128)(4,1)}), s8[4194304]{0:T(1024)(128)(4,1)S(1)}, s32[]{:S(2)}) async-start(s8[6291456]{0:T(1024)(128)(4,1)} %bitcast.147), calls=%async_computation.12 | async-start | bytes 8388608
  260.4 3.0 slice-start.5
  320.0 16.9 %collective-permute-start.6 = (f32[128,1024]{0,1:T(8,128)}, f32[128,1024]{0,1:T(8,128)}, u32[]{:S(2)}, u32[]{:S(2)}) collective-permute-start(f32[128,1024]{0,1:T(8,128)} %bitcast.136), channel_id=1, source_target_pairs={{0,28},{4,0},{8,4},{12,8},{16,12},{20,16},{24,20},{28,24},{1,29},{... | collective-permute-start | bytes 1572872 | tf_op jit(solution)/shard_map/ppermute | solution.py:108
  326.3 21.9 %collective-permute-start.5 = (f32[128,1024]{0,1:T(8,128)}, f32[128,1024]{0,1:T(8,128)}, u32[]{:S(2)}, u32[]{:S(2)}) collective-permute-start(f32[128,1024]{0,1:T(8,128)} %bitcast.135), channel_id=1, source_target_pairs={{0,24},{4,28},{8,0},{12,4},{16,8},{20,12},{24,16},{28,20},{1,25},{... | collective-permute-start | bytes 1572872 | tf_op jit(solution)/shard_map/ppermute | solution.py:108
  327.8 31.6 %collective-permute-start.4 = (f32[128,1024]{0,1:T(8,128)}, f32[128,1024]{0,1:T(8,128)S(1)}, u32[]{:S(2)}, u32[]{:S(2)}) collective-permute-start(f32[128,1024]{0,1:T(8,128)} %bitcast.132), channel_id=1, source_target_pairs={{0,20},{4,24},{8,28},{12,0},{16,4},{20,8},{24,12},{28,16},{1,21},{... | collective-permute-start | bytes 1572872 | tf_op jit(solution)/shard_map/ppermute | solution.py:108
  328.8 85.9 %collective-permute-start.3 = (f32[128,1024]{0,1:T(8,128)}, f32[128,1024]{0,1:T(8,128)S(1)}, u32[]{:S(2)}, u32[]{:S(2)}) collective-permute-start(f32[128,1024]{0,1:T(8,128)} %bitcast.133), channel_id=1, source_target_pairs={{0,16},{4,20},{8,24},{12,28},{16,0},{20,4},{24,8},{28,12},{1,17},{... | collective-permute-start | bytes 1572872 | tf_op jit(solution)/shard_map/ppermute | solution.py:108
  332.7 84.4 %collective-permute-start.2 = (f32[128,1024]{0,1:T(8,128)}, f32[128,1024]{0,1:T(8,128)}, u32[]{:S(2)}, u32[]{:S(2)}) collective-permute-start(f32[128,1024]{0,1:T(8,128)} %bitcast.134), channel_id=1, source_target_pairs={{0,12},{4,16},{8,20},{12,24},{16,28},{20,0},{24,4},{28,8},{1,13},{... | collective-permute-start | bytes 1572872 | tf_op jit(solution)/shard_map/ppermute | solution.py:108
  336.9 80.3 %collective-permute-start.1 = (f32[128,1024]{0,1:T(8,128)}, f32[128,1024]{0,1:T(8,128)}, u32[]{:S(2)}, u32[]{:S(2)}) collective-permute-start(f32[128,1024]{0,1:T(8,128)} %bitcast.36), channel_id=1, source_target_pairs={{0,8},{4,12},{8,16},{12,20},{16,24},{20,28},{24,0},{28,4},{1,9},{5... | collective-permute-start | bytes 1572872 | tf_op jit(solution)/shard_map/ppermute | solution.py:108
  348.1 69.0 %collective-permute-start = (f32[128,1024]{0,1:T(8,128)}, f32[128,1024]{0,1:T(8,128)}, u32[]{:S(2)}, u32[]{:S(2)}) collective-permute-start(f32[128,1024]{0,1:T(8,128)} %bitcast.35), channel_id=1, source_target_pairs={{0,4},{4,8},{8,12},{12,16},{16,20},{20,24},{24,28},{28,0},{1,5},{5... | collective-permute-start | bytes 1572872 | tf_op jit(solution)/shard_map/ppermute | solution.py:108
  348.1 71.9 %copy-start.1 = (bf16[1024,512]{1,0:T(8,128)(2,1)S(1)}, bf16[1024,512]{1,0:T(8,128)(2,1)}, u32[]{:S(2)}) copy-start(bf16[1024,512]{1,0:T(8,128)(2,1)} %param.10) | copy-start | bytes 3145732
Sparse Core Ops, SparseCore 0:
  10.9 53.3 all-gather.12
  68.6 29.9 reduce-scatter.1
  121.7 14.8 all-gather.14
  142.3 92.2 all-gather.16
  253.3 26.6 all-gather.10
  281.5 28.4 all-gather.8

commit v7 on v5

--- a/solution.py
+++ b/solution.py
@@ -4,6 +4,7 @@
 from jax.sharding import PartitionSpec as P
 
 EPS = 1e-06
+EXPERT = ("ez", "ex")
 
 
 def on_device(
@@ -19,14 +20,14 @@
 ):
     tok_count = residual.shape[0]
     width = residual.shape[1]
-    groups = lax.axis_size("expert")
+    groups = lax.axis_size(EXPERT)
     tensor_ways = lax.axis_size("tensor")
     exp_local = gate_proj.shape[0]
     hidden_local = gate_proj.shape[1]
     share = width // tensor_ways
     cols_e = out_proj.shape[1]
     cols_et = cols_e // tensor_ways
-    me_e = lax.axis_index("expert")
+    me_e = lax.axis_index(EXPERT)
     me_t = lax.axis_index("tensor")
     all_tok = groups * tok_count
 
@@ -44,7 +45,10 @@
     coded = jnp.pad(coded, (0, extra * heads_w - coded.shape[0])).reshape(extra, heads_w)
     packet = jnp.concatenate([attn_heads, coded], axis=0)
 
-    got = lax.all_gather(packet, "expert", axis=0, tiled=False)
+    pair = lax.all_gather(packet, "ex", axis=0, tiled=False)
+    got = lax.all_gather(pair, "ez", axis=0, tiled=False).reshape(
+        (groups,) + packet.shape
+    )
     partial = jnp.einsum(
         "enh,hc->enc", got[:, :tok_count], out_proj, preferred_element_type=jnp.float32
     ).reshape(all_tok, cols_e)
@@ -54,7 +58,7 @@
     w_mine = lax.dynamic_slice_in_dim(w_all, me_e * exp_local, exp_local, 1)
     summed = lax.psum_scatter(partial, "tensor", scatter_dimension=1, tiled=True)
     mine = lax.all_to_all(
-        summed.reshape(groups, tok_count, cols_et), "expert", 0, 0, tiled=False
+        summed.reshape(groups, tok_count, cols_et), EXPERT, 0, 0, tiled=False
     )
     res_cols = lax.dynamic_index_in_dim(
         residual.reshape(tok_count, groups, tensor_ways, cols_et), me_t, 2, keepdims=False
@@ -72,7 +76,7 @@
     gain_q = lax.dynamic_slice_in_dim(norm_gain, me_t * share, share, 0).astype(jnp.float32)
     normed_q = (state_q * scale * gain_q).astype(jnp.bfloat16)
 
-    slabs = lax.all_gather(normed_q, ("tensor", "expert"), axis=0, tiled=False).reshape(
+    slabs = lax.all_gather(normed_q, ("tensor",) + EXPERT, axis=0, tiled=False).reshape(
         tensor_ways, all_tok, share
     )
 
@@ -99,26 +103,39 @@
         ).astype(jnp.bfloat16)
         w_tok = w_mine[:, loc][:, None]
         total = total + jnp.where(w_tok > 0, w_tok * out.astype(jnp.float32), 0.0)
+    near = lax.axis_size("ex")
+    far = groups // near
+    by_x = jnp.transpose(
+        total.astype(jnp.bfloat16).reshape(far, near, tok_count, share), (1, 0, 2, 3)
+    )
+    halves = lax.psum_scatter(by_x, "ex", scatter_dimension=0, tiled=True)
     mixture = lax.psum_scatter(
-        total.astype(jnp.bfloat16), "expert", scatter_dimension=0, tiled=True
-    ).astype(jnp.float32)
+        halves.reshape(far, tok_count, share), "ez", scatter_dimension=0, tiled=True
+    )
+    mixture = mixture.reshape(tok_count, share).astype(jnp.float32)
     state_out = lax.dynamic_slice_in_dim(state_f, me_t * share, share, 1)
     return (state_out + mixture).astype(jnp.bfloat16)
 
 
 def solution(mesh):
     in_specs = (
-        P("expert", "tensor"),
-        P("tensor", "expert"),
-        P("expert", None),
+        P(EXPERT, "tensor"),
+        P("tensor", EXPERT),
+        P(EXPERT, None),
         P(),
-        P("expert", "tensor", None),
-        P("expert", "tensor", None),
-        P("expert", None, "tensor"),
-        P("expert", None),
-        P("expert", None),
+        P(EXPERT, "tensor", None),
+        P(EXPERT, "tensor", None),
+        P(EXPERT, None, "tensor"),
+        P(EXPERT, None),
+        P(EXPERT, None),
     )
-    out_specs = P("expert", "tensor")
+    out_specs = P(EXPERT, "tensor")
+    devices = mesh.devices
+    near = 2 if devices.shape[0] % 2 == 0 else 1
+    split = jax.sharding.Mesh(
+        devices.reshape(devices.shape[0] // near, near, devices.shape[1]),
+        ("ez", "ex", "tensor"),
+    )
     return jax.shard_map(
-        on_device, mesh=mesh, in_specs=in_specs, out_specs=out_specs, check_vma=False
+        on_device, mesh=split, in_specs=in_specs, out_specs=out_specs, check_vma=False
     )

time: 387 us -> 397 us (1.026)
  matrix products: 65.8 us -> 55.2 us
  blocking collectives: 0 us -> 10.4 us
  waiting for transfers between devices: 280 us -> 289 us
    all_gather x2, waiting for transfers between devices: 131 us -> 142 us  [the longest x1 92.2 us: on_device(): lax.all_gather(normed_q, ('tensor',) + EXPERT, axis=0, tiled=False)]
    all_gather x0 -> x1, blocking collectives: none -> 10.4 us  [on_device(): pair = lax.all_gather(packet, 'ex', axis=0, tiled=False)]
    dot_general x8, matrix products: 19.2 us -> 10.4 us  [on_device(): jnp.dot(x, gate_proj[loc, :, a * share:(a + 1) * share].T, preferred_elem...]
    reduce_scatter x1 -> x2, waiting for transfers between devices: 68.1 us -> 61.4 us  [the longest x1 31.9 us: on_device(): halves = lax.psum_scatter(by_x, 'ex', scatter_dimension=0, tiled=True)]
  transfers between devices with their start and end apart: 8 -> 9, of which waited for: 8 -> 9; matrix products, arithmetic and copies ran while one was open for 9% -> 8% of each run, Pallas kernels for 0% -> 0%
where the time goes in v7:
time: 397 us
  waiting for transfers between devices  289 us (73%)
  matrix products  55.2 us (14%)
  between operations  13.8 us (3%)
  local copies, waits for them, and re-layouts  12.8 us (3%)
  blocking collectives  10.4 us (3%)
  other arithmetic  8.94 us (2%)
  starting transfers between devices  6.47 us (2%)
    all_gather x1, waiting for transfers between devices, on_device(): lax.all_gather(normed_q, ('tensor',) + EXPERT, axis=0, tiled=False)  92.2 us
    all_gather x1, waiting for transfers between devices, on_device(): lax.all_gather(pair, 'ez', axis=0, tiled=False)  50 us
    reduce_scatter x1, waiting for transfers between devices, on_device(): halves = lax.psum_scatter(by_x, 'ex', scatter_dimension=0, tiled=True)  31.9 us
    reduce_scatter x1, waiting for transfers between devices, on_device(): lax.psum_scatter(partial, 'tensor', scatter_dimension=1, tiled=True)  30.4 us
    reduce_scatter x1, waiting for transfers between devices, on_device(): lax.psum_scatter(halves.reshape(far, tok_count, share), 'ez', scatter_dim...  29.4 us
    all_gather x2, waiting for transfers between devices, on_device(): act_all = lax.all_gather(act, 'tensor', axis=1, tiled=True)  27 us
    dot_general x8, matrix products, on_device(): jnp.dot(x, up_proj[loc, :, a * share:(a + 1) * share].T, preferred_elemen...  25.8 us
    dot_general x2, matrix products, on_device(): jnp.dot(act_all, down_proj[loc], preferred_element_type=jnp.float32)  14.8 us
  transfers between devices with their start and end apart: 9, of which 9 were waited for; matrix products, arithmetic and copies ran while one was open for 8% of the time, Pallas kernels for 0%

profile of v7, /device:TPU:0, one launch (start us, length us, event | category | flops | bytes accessed | tf_op | source)
XLA Modules:
  0.0 396.6 jit_solution(3140384282111117014)
XLA Ops:
  10.0 10.4 %all-gather = bf16[272,1024]{1,0:T(8,128)(2,1)} all-gather(bf16[136,1024]{1,0:T(8,128)(2,1)S(1)} %pad_maximum_fusion), channel_id=2, replica_groups=mesh['ez'=4,'ex'=2,'tensor'=4] {'ex'}, dimensions={0}, use_global_device_ids=true | all-gather | bytes 835584 | tf_op jit(solution)/shard_map/all_gather | solution.py:48
  20.5 50.0 %all-gather.14.cloned.1.call-done = bf16[8,136,1024]{2,1,0:T(8,128)(2,1)} async-done(((bf16[2,136,1024]{2,1,0:T(8,128)(2,1)}), bf16[8,136,1024]{2,1,0:T(8,128)(2,1)}) %all-gather.14.cloned.1.call-update) | async-done | bytes 2228240 | tf_op jit(solution)/shard_map/all_gather | solution.py:49
  70.4 4.2 %fusion.7 = f32[8,128,512]{2,1,0:T(8,128)} fusion(bf16[8,136,1024]{2,1,0:T(8,128)(2,1)} %all-gather.14.cloned.1.call-done, bf16[1024,512]{1,0:T(8,128)(2,1)S(1)} %copy-done), kind=kOutput, calls=%fused_computation.10 | convolution fusion | flops 1073741824 | bytes 5242880 | tf_op jit(solution)/shard_map/enh,hc->enc/dot_general | solution.py:52
  74.6 30.4 %reduce-scatter.4.cloned.1.call-done = f32[1024,128]{1,0:T(8,128)} async-done(((f32[1024,512]{1,0:T(8,128)}), f32[1024,128]{1,0:T(8,128)}) %reduce-scatter.4.cloned.1.call-update) | async-done | bytes 524304 | tf_op jit(solution)/shard_map/reduce_scatter | solution.py:59
  105.0 2.0 copy.47
  107.1 5.5 %all-to-all-start = ((f32[8,128,128]{1,2,0:T(8,128)}), f32[8,128,128]{1,2,0:T(8,128)S(1)}, u32[]{:S(2)}, u32[]{:S(2)}) async-start(f32[8,128,128]{1,2,0:T(8,128)} %copy.47), calls=%async_computation.1 | async-start | bytes 1048576 | tf_op jit(solution)/shard_map/all_to_all | solution.py:60
  113.3 13.8 %all-to-all-done = f32[8,128,128]{1,2,0:T(8,128)S(1)} async-done(((f32[8,128,128]{1,2,0:T(8,128)}), f32[8,128,128]{1,2,0:T(8,128)S(1)}, u32[]{:S(2)}, u32[]{:S(2)}) %all-to-all-start) | async-done | bytes 524320 | tf_op jit(solution)/shard_map/all_to_all | solution.py:60
  128.8 14.3 %all-gather.16.cloned.1.call-done = bf16[32,128,128]{2,1,0:T(8,128)(2,1)} async-done(((bf16[8,128,128]{2,1,0:T(8,128)(2,1)}), bf16[32,128,128]{2,1,0:T(8,128)(2,1)}) %all-gather.16.cloned.1.call-update) | async-done | bytes 1048592 | tf_op jit(solution)/shard_map/all_gather | solution.py:69
  143.0 1.5 convert_bitcast_fusion
  144.5 1.9 copy.49
  146.7 2.0 multiply_convert_fusion.2
  148.9 92.2 %all-gather.18.cloned.1.call-done = bf16[4096,1024]{0,1:T(8,128)(2,1)} async-done(((bf16[128,1024]{0,1:T(8,128)(2,1)}), bf16[4096,1024]{0,1:T(8,128)(2,1)}) %all-gather.18.cloned.1.call-update) | async-done | bytes 8388624 | tf_op jit(solution)/shard_map/all_gather | solution.py:79
  241.1 3.2 fusion.23
  245.3 2.6 fusion.39
  247.9 2.6 fusion.31
  253.1 1.3 fusion.33
  254.4 1.3 fusion.25
  255.7 3.9 multiply_convert_fusion
  259.9 3.2 fusion.19
  263.2 3.5 fusion.35
  266.9 3.0 fusion.27
  269.9 1.3 fusion.14
  271.2 1.3 fusion.21
  272.5 1.3 fusion.37
  275.1 3.9 multiply_convert_fusion.1
  281.8 4.7 %all-gather.12.cloned.1.call-done = bf16[1024,1536]{1,0:T(8,128)(2,1)} async-done(((bf16[1024,384]{1,0:T(8,128)(2,1)}), bf16[1024,1536]{1,0:T(8,128)(2,1)}) %all-gather.12.cloned.1.call-update) | async-done | bytes 3145744 | tf_op jit(solution)/shard_map/all_gather | solution.py:100
  286.5 7.7 %fusion = bf16[1024,1024]{1,0:T(8,128)(2,1)} fusion(bf16[1024,1536]{1,0:T(8,128)(2,1)} %all-gather.12.cloned.1.call-done, bf16[2,1536,1024]{2,1,0:T(8,128)(2,1)} %param.15), kind=kOutput, calls=%fused_computation.1 | convolution fusion | flops 3221225472 | bytes 8388608 | tf_op jit(solution)/shard_map/dot_general | solution.py:101
  294.2 22.3 %all-gather.10.cloned.1.call-done = bf16[1024,1536]{1,0:T(8,128)(2,1)} async-done(((bf16[1024,384]{1,0:T(8,128)(2,1)}), bf16[1024,1536]{1,0:T(8,128)(2,1)}) %all-gather.10.cloned.1.call-update) | async-done | bytes 3145744 | tf_op jit(solution)/shard_map/all_gather | solution.py:100
  316.5 7.1 %add_convert_fusion = bf16[1024,1024]{1,0:T(8,128)(2,1)S(1)} fusion(bf16[1024,1024]{1,0:T(8,128)(2,1)} %fusion, f32[1024]{0:T(1024)S(1)} %bitcast.117, f32[1024]{0:T(1024)S(1)} %bitcast.118, pred[1024]{0:T(1024)(128)(4,1)S(1)} %get-tuple-element.9, pred[1024]{0:T(1024)(128)(4,1)S(1)} %get-tuple-element.10, ...), kind=kOutput, calls=%fused_computation | convolution fusion | flops 3230662656 | bytes 10496000 | tf_op jit(solution)/shard_map/dot_general | solution.py:101
  323.6 2.6 copy.51
  326.3 31.9 %reduce-scatter.6.cloned.1.call-done = bf16[1,4,128,1024]{2,3,1,0:T(8,128)(2,1)} async-done(((bf16[2,4,128,1024]{2,3,1,0:T(8,128)(2,1)}), bf16[1,4,128,1024]{2,3,1,0:T(8,128)(2,1)}) %reduce-scatter.6.cloned.1.call-update) | async-done | bytes 1048592 | tf_op jit(solution)/shard_map/reduce_scatter | solution.py:111
  358.3 29.4 %reduce-scatter.8.cloned.1.call-done = bf16[1,128,1024]{1,2,0:T(8,128)(2,1)} async-done(((bf16[4,128,1024]{1,2,0:T(8,128)(2,1)}), bf16[1,128,1024]{1,2,0:T(8,128)(2,1)}) %reduce-scatter.8.cloned.1.call-update) | async-done | bytes 262160 | tf_op jit(solution)/shard_map/reduce_scatter | solution.py:112
  (72 shorter events, 16.7 us)
Async XLA Ops:
  6.5 63.9 %copy-start = (bf16[1024,512]{1,0:T(8,128)(2,1)S(1)}, bf16[1024,512]{1,0:T(8,128)(2,1)}, u32[]{:S(2)}) copy-start(bf16[1024,512]{1,0:T(8,128)(2,1)} %param.10) | copy-start | bytes 3145732
  6.5 63.9 %all-gather.14.cloned.1.call-start = ((), (), s32[]{:S(2)}) async-start(), calls=%async_computation.9 | async-start | bytes 2785280 | tf_op jit(solution)/shard_map/all_gather | solution.py:49
  20.4 84.6 %reduce-scatter.4.cloned.1.call-start = ((), (), s32[]{:S(2)}) async-start(), calls=%async_computation.4 | async-start | bytes 2621440 | tf_op jit(solution)/shard_map/reduce_scatter | solution.py:59
  74.6 38.0 %copy-start.3 = (bf16[128,4096]{1,0:T(8,128)(2,1)S(1)}, bf16[128,4096]{1,0:T(8,128)(2,1)}, u32[]{:S(2)}) copy-start(bf16[128,4096]{1,0:T(8,128)(2,1)} %param.11) | copy-start | bytes 3145732
  107.1 20.0 %all-to-all-start = ((f32[8,128,128]{1,2,0:T(8,128)}), f32[8,128,128]{1,2,0:T(8,128)S(1)}, u32[]{:S(2)}, u32[]{:S(2)}) async-start(f32[8,128,128]{1,2,0:T(8,128)} %copy.47), calls=%async_computation.1 | async-start | bytes 1048576 | tf_op jit(solution)/shard_map/all_to_all | solution.py:60
  112.6 30.4 %all-gather.16.cloned.1.call-start = ((), (), s32[]{:S(2)}) async-start(), calls=%async_computation.10 | async-start | bytes 1310720 | tf_op jit(solution)/shard_map/all_gather | solution.py:69
  128.0 113.0 %all-gather.18.cloned.1.call-start = ((), (), s32[]{:S(2)}) async-start(), calls=%async_computation.11 | async-start | bytes 8650752 | tf_op jit(solution)/shard_map/all_gather | solution.py:79
  144.5 1.9 copy-start.2
  148.6 137.8 %all-gather.12.cloned.1.call-start = ((), (), s32[]{:S(2)}) async-start(), calls=%async_computation.6 | async-start | bytes 3932160 | tf_op jit(solution)/shard_map/all_gather | solution.py:100
  241.1 4.3 %copy-start.4 = (bf16[4096,1024]{0,1:T(8,128)(2,1)S(1)}, bf16[4096,1024]{0,1:T(8,128)(2,1)}, u32[]{:S(2)}) copy-start(bf16[4096,1024]{0,1:T(8,128)(2,1)} %all-gather.18.cloned.1.call-done) | copy-start | bytes 25165828
  245.3 5.2 %slice-start.2 = ((s8[6291456]{0:T(1024)(128)(4,1)}), s8[4194304]{0:T(1024)(128)(4,1)S(1)}, s32[]{:S(2)}) async-start(s8[6291456]{0:T(1024)(128)(4,1)} %bitcast.121), calls=%async_computation.14 | async-start | bytes 8388608
  247.9 2.6 slice-start.3
  259.6 56.8 %all-gather.10.cloned.1.call-start = ((), (), s32[]{:S(2)}) async-start(), calls=%async_computation.5 | async-start | bytes 3932160 | tf_op jit(solution)/shard_map/all_gather | solution.py:100
  259.9 6.7 %slice-start = ((s8[8388608]{0:T(1024)(128)(4,1)}), s8[4194304]{0:T(1024)(128)(4,1)S(1)}, s32[]{:S(2)}) async-start(s8[8388608]{0:T(1024)(128)(4,1)} %bitcast.119), calls=%async_computation.12 | async-start | bytes 8388608
  263.1 3.7 slice-start.1
  263.1 6.8 %slice-start.4 = ((s8[6291456]{0:T(1024)(128)(4,1)}), s8[4194304]{0:T(1024)(128)(4,1)S(1)}, s32[]{:S(2)}) async-start(s8[6291456]{0:T(1024)(128)(4,1)} %bitcast.123), calls=%async_computation.16 | async-start | bytes 8388608
  266.9 3.0 slice-start.5
  279.0 79.2 %reduce-scatter.6.cloned.1.call-start = ((), (), s32[]{:S(2)}) async-start(), calls=%async_computation.7 | async-start | bytes 3145728 | tf_op jit(solution)/shard_map/reduce_scatter | solution.py:111
  326.2 63.5 %copy-start.1 = (bf16[1024,512]{1,0:T(8,128)(2,1)S(1)}, bf16[1024,512]{1,0:T(8,128)(2,1)}, u32[]{:S(2)}) copy-start(bf16[1024,512]{1,0:T(8,128)(2,1)} %param.10) | copy-start | bytes 3145732
  326.3 61.4 %reduce-scatter.8.cloned.1.call-start = ((), (), s32[]{:S(2)}) async-start(), calls=%async_computation.8 | async-start | bytes 1310720 | tf_op jit(solution)/shard_map/reduce_scatter | solution.py:112
Sparse Core Ops, SparseCore 0:
  20.5 49.8 all-gather.13
  74.7 30.2 reduce-scatter.3
  128.1 14.8 all-gather.15
  148.8 92.2 all-gather.17
  259.8 26.6 all-gather.11
  287.9 28.4 all-gather.9
  326.4 31.8 reduce-scatter.5
  360.5 27.1 reduce-scatter.7

commit v8 on v5

--- a/solution.py
+++ b/solution.py
@@ -99,9 +99,19 @@
         ).astype(jnp.bfloat16)
         w_tok = w_mine[:, loc][:, None]
         total = total + jnp.where(w_tok > 0, w_tok * out.astype(jnp.float32), 0.0)
+    near = 2 if groups % 2 == 0 else 1
+    far = groups // near
+    pairs = [[z * near + x for x in range(near)] for z in range(far)]
+    lines = [[z * near + x for z in range(far)] for x in range(near)]
+    halves = lax.psum_scatter(
+        total.astype(jnp.bfloat16).reshape(far, near * tok_count, share), "expert",
+        scatter_dimension=0, tiled=True, axis_index_groups=lines,
+    )
     mixture = lax.psum_scatter(
-        total.astype(jnp.bfloat16), "expert", scatter_dimension=0, tiled=True
-    ).astype(jnp.float32)
+        halves.reshape(near * tok_count, share), "expert", scatter_dimension=0,
+        tiled=True, axis_index_groups=pairs,
+    )
+    mixture = mixture.astype(jnp.float32)
     state_out = lax.dynamic_slice_in_dim(state_f, me_t * share, share, 1)
     return (state_out + mixture).astype(jnp.bfloat16)
 

time: 387 us -> 391 us (1.010)
  matrix products: 65.8 us -> 55.2 us
  waiting for transfers between devices: 280 us -> 289 us
  local copies, waits for them, and re-layouts: 9.31 us -> 15.9 us
    reduce_scatter x1, waiting for transfers between devices: 68.1 us -> 44 us  [on_device(): lax.psum_scatter(total.astype(jnp.bfloat16).reshape(far, near * tok_count...]
    all_gather x1, waiting for transfers between devices: 77.3 us -> 92.2 us  [on_device(): lax.all_gather(normed_q, ('tensor', 'expert'), axis=0, tiled=False)]
    unnamed x7 -> x9, waiting for transfers between devices: 0.11 us -> 14.2 us
    dot_general x8, matrix products: 19.2 us -> 10.4 us  [on_device(): jnp.dot(x, gate_proj[loc, :, a * share:(a + 1) * share].T, preferred_elem...]
    unnamed x19 -> x29, local copies, waits for them, and re-layouts: 2.06 us -> 6.53 us
  transfers between devices with their start and end apart: 8 -> 9, of which waited for: 8 -> 9; matrix products, arithmetic and copies ran while one was open for 9% -> 8% of each run, Pallas kernels for 0% -> 0%
where the time goes in v8:
time: 391 us; the launch traced here: 390 us
  waiting for transfers between devices  289 us (74%)
  matrix products  55.2 us (14%)
  local copies, waits for them, and re-layouts  15.9 us (4%)
  between operations  13.8 us (4%)
  other arithmetic  9.58 us (2%)
  starting transfers between devices  6.46 us (2%)
    all_gather x1, waiting for transfers between devices, on_device(): lax.all_gather(normed_q, ('tensor', 'expert'), axis=0, tiled=False)  92.2 us
    all_gather x1, waiting for transfers between devices, on_device(): got = lax.all_gather(packet, 'expert', axis=0, tiled=False)  53.5 us
    reduce_scatter x1, waiting for transfers between devices, on_device(): lax.psum_scatter(total.astype(jnp.bfloat16).reshape(far, near * tok_count...  44 us
    reduce_scatter x1, waiting for transfers between devices, on_device(): lax.psum_scatter(partial, 'tensor', scatter_dimension=1, tiled=True)  30.1 us
    all_gather x2, waiting for transfers between devices, on_device(): act_all = lax.all_gather(act, 'tensor', axis=1, tiled=True)  27 us
    dot_general x8, matrix products, on_device(): jnp.dot(x, up_proj[loc, :, a * share:(a + 1) * share].T, preferred_elemen...  25.8 us
    dot_general x2, matrix products, on_device(): jnp.dot(act_all, down_proj[loc], preferred_element_type=jnp.float32)  14.8 us
    all_gather x1, waiting for transfers between devices, on_device(): state_all = lax.all_gather(state_ct, 'tensor', axis=0, tiled=False)  14.3 us
  transfers between devices with their start and end apart: 9, of which 9 were waited for; matrix products, arithmetic and copies ran while one was open for 8% of the time, Pallas kernels for 0%

profile of v8, /device:TPU:0, one launch (start us, length us, event | category | flops | bytes accessed | tf_op | source)
XLA Modules:
  0.0 389.9 jit_solution(14523322449023901068)
XLA Ops:
  9.1 1.7 pad_maximum_fusion
  10.8 53.5 %all-gather.13.cloned.1.call-done = bf16[1088,1024]{1,0:T(8,128)(2,1)} async-done(((bf16[136,1024]{1,0:T(8,128)(2,1)}), bf16[1088,1024]{1,0:T(8,128)(2,1)}) %all-gather.13.cloned.1.call-update) | async-done | bytes 2228240 | tf_op jit(solution)/shard_map/all_gather | solution.py:47
  64.3 4.2 %fusion.7 = f32[8,128,512]{2,1,0:T(8,128)} fusion(bf16[8,136,1024]{2,1,0:T(8,128)(2,1)} %bitcast.114, bf16[1024,512]{1,0:T(8,128)(2,1)S(1)} %copy-done), kind=kOutput, calls=%fused_computation.10 | convolution fusion | flops 1073741824 | bytes 5242880 | tf_op jit(solution)/shard_map/enh,hc->enc/dot_general | solution.py:48
  68.5 30.1 %reduce-scatter.6.cloned.1.call-done = f32[1024,128]{1,0:T(8,128)} async-done(((f32[1024,512]{1,0:T(8,128)}), f32[1024,128]{1,0:T(8,128)}) %reduce-scatter.6.cloned.1.call-update) | async-done | bytes 524304 | tf_op jit(solution)/shard_map/reduce_scatter | solution.py:55
  98.6 2.0 copy.45
  100.6 5.5 %all-to-all-start = ((f32[8,128,128]{1,2,0:T(8,128)}), f32[8,128,128]{1,2,0:T(8,128)S(1)}, u32[]{:S(2)}, u32[]{:S(2)}) async-start(f32[8,128,128]{1,2,0:T(8,128)} %copy.45), calls=%async_computation.1 | async-start | bytes 1048576 | tf_op jit(solution)/shard_map/all_to_all | solution.py:56
  106.9 13.8 %all-to-all-done = f32[8,128,128]{1,2,0:T(8,128)S(1)} async-done(((f32[8,128,128]{1,2,0:T(8,128)}), f32[8,128,128]{1,2,0:T(8,128)S(1)}, u32[]{:S(2)}, u32[]{:S(2)}) %all-to-all-start) | async-done | bytes 524320 | tf_op jit(solution)/shard_map/all_to_all | solution.py:56
  122.3 14.3 %all-gather.15.cloned.1.call-done = bf16[32,128,128]{2,1,0:T(8,128)(2,1)} async-done(((bf16[8,128,128]{2,1,0:T(8,128)(2,1)}), bf16[32,128,128]{2,1,0:T(8,128)(2,1)}) %all-gather.15.cloned.1.call-update) | async-done | bytes 1048592 | tf_op jit(solution)/shard_map/all_gather | solution.py:65
  136.6 1.5 convert_bitcast_fusion
  138.0 1.9 copy.47
  140.2 2.0 multiply_convert_fusion.2
  142.4 92.2 %all-gather.17.cloned.1.call-done = bf16[4096,1024]{0,1:T(8,128)(2,1)} async-done(((bf16[128,1024]{0,1:T(8,128)(2,1)}), bf16[4096,1024]{0,1:T(8,128)(2,1)}) %all-gather.17.cloned.1.call-update) | async-done | bytes 8388624 | tf_op jit(solution)/shard_map/all_gather | solution.py:75
  234.6 3.2 fusion.23
  238.9 2.6 fusion.39
  241.5 2.6 fusion.31
  245.4 1.3 fusion.17
  246.7 1.3 fusion.33
  248.0 1.3 fusion.25
  249.3 3.9 multiply_convert_fusion
  253.5 3.2 fusion.19
  256.7 3.5 fusion.35
  260.4 3.0 fusion.27
  264.8 1.3 fusion.21
  268.7 3.9 multiply_convert_fusion.1
  275.3 4.7 %all-gather.11.cloned.1.call-done = bf16[1024,1536]{1,0:T(8,128)(2,1)} async-done(((bf16[1024,384]{1,0:T(8,128)(2,1)}), bf16[1024,1536]{1,0:T(8,128)(2,1)}) %all-gather.11.cloned.1.call-update) | async-done | bytes 3145744 | tf_op jit(solution)/shard_map/all_gather | solution.py:96
  280.0 7.7 %fusion = bf16[1024,1024]{1,0:T(8,128)(2,1)} fusion(bf16[1024,1536]{1,0:T(8,128)(2,1)} %all-gather.11.cloned.1.call-done, bf16[2,1536,1024]{2,1,0:T(8,128)(2,1)} %param.15), kind=kOutput, calls=%fused_computation.1 | convolution fusion | flops 3221225472 | bytes 8388608 | tf_op jit(solution)/shard_map/dot_general | solution.py:97
  287.7 22.3 %all-gather.9.cloned.1.call-done = bf16[1024,1536]{1,0:T(8,128)(2,1)} async-done(((bf16[1024,384]{1,0:T(8,128)(2,1)}), bf16[1024,1536]{1,0:T(8,128)(2,1)}) %all-gather.9.cloned.1.call-update) | async-done | bytes 3145744 | tf_op jit(solution)/shard_map/all_gather | solution.py:96
  310.0 7.1 %add_convert_fusion = bf16[1024,1024]{1,0:T(8,128)(2,1)S(1)} fusion(bf16[1024,1024]{1,0:T(8,128)(2,1)} %fusion, f32[1024]{0:T(1024)S(1)} %bitcast.112, f32[1024]{0:T(1024)S(1)} %bitcast.113, pred[1024]{0:T(1024)(128)(4,1)S(1)} %get-tuple-element.9, pred[1024]{0:T(1024)(128)(4,1)S(1)} %get-tuple-element.10, ...), kind=kOutput, calls=%fused_computation | convolution fusion | flops 3230662656 | bytes 10496000 | tf_op jit(solution)/shard_map/dot_general | solution.py:97
  317.2 2.6 copy.49
  319.8 44.0 %reduce-scatter.8.cloned.1.call-done = bf16[1,256,1024]{1,2,0:T(8,128)(2,1)} async-done(((bf16[4,256,1024]{1,2,0:T(8,128)(2,1)}), bf16[1,256,1024]{1,2,0:T(8,128)(2,1)}) %reduce-scatter.8.cloned.1.call-update) | async-done | bytes 524304 | tf_op jit(solution)/shard_map/reduce_scatter | solution.py:106
  363.8 2.1 copy.51
  365.9 14.1 %reduce-scatter.10.cloned.1.call-done = bf16[128,1024]{1,0:T(8,128)(2,1)} async-done(((bf16[256,1024]{1,0:T(8,128)(2,1)}), bf16[128,1024]{1,0:T(8,128)(2,1)}) %reduce-scatter.10.cloned.1.call-update) | async-done | bytes 262160
  (73 shorter events, 18.1 us)
Async XLA Ops:
  6.5 57.7 %copy-start = (bf16[1024,512]{1,0:T(8,128)(2,1)S(1)}, bf16[1024,512]{1,0:T(8,128)(2,1)}, u32[]{:S(2)}) copy-start(bf16[1024,512]{1,0:T(8,128)(2,1)} %param.10) | copy-start | bytes 3145732
  6.5 57.7 %all-gather.13.cloned.1.call-start = ((), (), s32[]{:S(2)}) async-start(), calls=%async_computation.8 | async-start | bytes 2506752 | tf_op jit(solution)/shard_map/all_gather | solution.py:47
  10.8 87.8 %reduce-scatter.6.cloned.1.call-start = ((), (), s32[]{:S(2)}) async-start(), calls=%async_computation.4 | async-start | bytes 2621440 | tf_op jit(solution)/shard_map/reduce_scatter | solution.py:55
  68.5 37.7 %copy-start.3 = (bf16[128,4096]{1,0:T(8,128)(2,1)S(1)}, bf16[128,4096]{1,0:T(8,128)(2,1)}, u32[]{:S(2)}) copy-start(bf16[128,4096]{1,0:T(8,128)(2,1)} %param.11) | copy-start | bytes 3145732
  100.6 20.0 %all-to-all-start = ((f32[8,128,128]{1,2,0:T(8,128)}), f32[8,128,128]{1,2,0:T(8,128)S(1)}, u32[]{:S(2)}, u32[]{:S(2)}) async-start(f32[8,128,128]{1,2,0:T(8,128)} %copy.45), calls=%async_computation.1 | async-start | bytes 1048576 | tf_op jit(solution)/shard_map/all_to_all | solution.py:56
  106.1 30.4 %all-gather.15.cloned.1.call-start = ((), (), s32[]{:S(2)}) async-start(), calls=%async_computation.9 | async-start | bytes 1310720 | tf_op jit(solution)/shard_map/all_gather | solution.py:65
  121.6 113.0 %all-gather.17.cloned.1.call-start = ((), (), s32[]{:S(2)}) async-start(), calls=%async_computation.10 | async-start | bytes 8650752 | tf_op jit(solution)/shard_map/all_gather | solution.py:75
  138.0 1.9 copy-start.2
  142.2 137.8 %all-gather.11.cloned.1.call-start = ((), (), s32[]{:S(2)}) async-start(), calls=%async_computation.6 | async-start | bytes 3932160 | tf_op jit(solution)/shard_map/all_gather | solution.py:96
  234.6 4.3 %copy-start.4 = (bf16[4096,1024]{0,1:T(8,128)(2,1)S(1)}, bf16[4096,1024]{0,1:T(8,128)(2,1)}, u32[]{:S(2)}) copy-start(bf16[4096,1024]{0,1:T(8,128)(2,1)} %all-gather.17.cloned.1.call-done) | copy-start | bytes 25165828
  238.9 5.2 %slice-start.2 = ((s8[6291456]{0:T(1024)(128)(4,1)}), s8[4194304]{0:T(1024)(128)(4,1)S(1)}, s32[]{:S(2)}) async-start(s8[6291456]{0:T(1024)(128)(4,1)} %bitcast.118), calls=%async_computation.14 | async-start | bytes 8388608
  241.5 2.6 slice-start.3
  253.2 56.8 %all-gather.9.cloned.1.call-start = ((), (), s32[]{:S(2)}) async-start(), calls=%async_computation.5 | async-start | bytes 3932160 | tf_op jit(solution)/shard_map/all_gather | solution.py:96
  253.5 6.7 %slice-start = ((s8[8388608]{0:T(1024)(128)(4,1)}), s8[4194304]{0:T(1024)(128)(4,1)S(1)}, s32[]{:S(2)}) async-start(s8[8388608]{0:T(1024)(128)(4,1)} %bitcast.116), calls=%async_computation.12 | async-start | bytes 8388608
  256.7 3.7 slice-start.1
  256.7 6.8 %slice-start.4 = ((s8[6291456]{0:T(1024)(128)(4,1)}), s8[4194304]{0:T(1024)(128)(4,1)S(1)}, s32[]{:S(2)}) async-start(s8[6291456]{0:T(1024)(128)(4,1)} %bitcast.120), calls=%async_computation.16 | async-start | bytes 8388608
  260.4 3.0 slice-start.5
  272.6 91.2 %reduce-scatter.8.cloned.1.call-start = ((), (), s32[]{:S(2)}) async-start(), calls=%async_computation.7 | async-start | bytes 2621440 | tf_op jit(solution)/shard_map/reduce_scatter | solution.py:106
  319.8 63.2 %copy-start.1 = (bf16[1024,512]{1,0:T(8,128)(2,1)S(1)}, bf16[1024,512]{1,0:T(8,128)(2,1)}, u32[]{:S(2)}) copy-start(bf16[1024,512]{1,0:T(8,128)(2,1)} %param.10) | copy-start | bytes 3145732
  319.8 60.1 %reduce-scatter.10.cloned.1.call-start = ((), (), s32[]{:S(2)}) async-start(), calls=%async_computation.11 | async-start | bytes 786432
Sparse Core Ops, SparseCore 0:
  10.9 53.3 all-gather.12
  68.6 29.9 reduce-scatter.5
  121.7 14.8 all-gather.14
  142.3 92.2 all-gather.16
  253.3 26.6 all-gather.10
  281.5 28.4 all-gather.8
  319.9 43.8 reduce-scatter.7
  366.0 13.8 reduce-scatter.9

commit v9 on v8

--- a/solution.py
+++ b/solution.py
@@ -2,6 +2,7 @@
 import jax.numpy as jnp
 from jax import lax
 from jax.sharding import PartitionSpec as P
+from jax.experimental.layout import Layout, with_layout_constraint
 
 EPS = 1e-06
 
@@ -72,9 +73,9 @@
     gain_q = lax.dynamic_slice_in_dim(norm_gain, me_t * share, share, 0).astype(jnp.float32)
     normed_q = (state_q * scale * gain_q).astype(jnp.bfloat16)
 
-    slabs = lax.all_gather(normed_q, ("tensor", "expert"), axis=0, tiled=False).reshape(
-        tensor_ways, all_tok, share
-    )
+    normed_q = with_layout_constraint(normed_q, Layout(major_to_minor=(0, 1)))
+    slabs = lax.all_gather(normed_q, ("tensor", "expert"), axis=0, tiled=False)
+    slabs = slabs.reshape(tensor_ways, all_tok, share)
 
     total = jnp.zeros((all_tok, share), jnp.float32)
     for loc in range(exp_local):

time: 391 us -> 379 us (0.969)
  waiting for transfers between devices: 289 us -> 272 us
  matrix products: 55.2 us -> 65.8 us
  local copies, waits for them, and re-layouts: 15.9 us -> 9.31 us
    reduce_scatter x0 -> x1, waiting for transfers between devices: none -> 16.1 us  [on_device(): lax.psum_scatter(halves.reshape(near * tok_count, share), 'expert', scatt...]
    all_gather x1, waiting for transfers between devices: 92.2 us -> 77.3 us  [on_device(): slabs = lax.all_gather(normed_q, ('tensor', 'expert'), axis=0, tiled=False)]
    unnamed x9 -> x8, waiting for transfers between devices: 14.2 us -> 0.13 us
    dot_general x8, matrix products: 10.4 us -> 19.2 us  [on_device(): jnp.dot(x, gate_proj[loc, :, a * share:(a + 1) * share].T, preferred_elem...]
    unnamed x29 -> x19, local copies, waits for them, and re-layouts: 6.53 us -> 2.06 us
  transfers between devices with their start and end apart: 9 -> 9, of which waited for: 9 -> 9; matrix products, arithmetic and copies ran while one was open for 8% -> 9% of each run, Pallas kernels for 0% -> 0%
where the time goes in v9:
time: 379 us; the launch traced here: 378 us
  waiting for transfers between devices  272 us (72%)
  matrix products  65.8 us (17%)
  between operations  13.7 us (4%)
  other arithmetic  10.3 us (3%)
  local copies, waits for them, and re-layouts  9.31 us (2%)
  starting transfers between devices  6.46 us (2%)
    all_gather x1, waiting for transfers between devices, on_device(): slabs = lax.all_gather(normed_q, ('tensor', 'expert'), axis=0, tiled=False)  77.3 us
    all_gather x1, waiting for transfers between devices, on_device(): got = lax.all_gather(packet, 'expert', axis=0, tiled=False)  53.5 us
    reduce_scatter x1, waiting for transfers between devices, on_device(): lax.psum_scatter(total.astype(jnp.bfloat16).reshape(far, near * tok_count...  44 us
    reduce_scatter x1, waiting for transfers between devices, on_device(): lax.psum_scatter(partial, 'tensor', scatter_dimension=1, tiled=True)  30.1 us
    dot_general x8, matrix products, on_device(): jnp.dot(x, up_proj[loc, :, a * share:(a + 1) * share].T, preferred_elemen...  26.1 us
    all_gather x2, waiting for transfers between devices, on_device(): act_all = lax.all_gather(act, 'tensor', axis=1, tiled=True)  23.2 us
    dot_general x8, matrix products, on_device(): jnp.dot(x, gate_proj[loc, :, a * share:(a + 1) * share].T, preferred_elem...  19.2 us
    dot_general x2, matrix products, on_device(): jnp.dot(act_all, down_proj[loc], preferred_element_type=jnp.float32)  16.3 us
  transfers between devices with their start and end apart: 9, of which 9 were waited for; matrix products, arithmetic and copies ran while one was open for 9% of the time, Pallas kernels for 0%

profile of v9, /device:TPU:0, one launch (start us, length us, event | category | flops | bytes accessed | tf_op | source)
XLA Modules:
  0.0 377.9 jit_solution(15550247264111262949)
XLA Ops:
  10.8 53.5 %all-gather.13.cloned.1.call-done = bf16[1088,1024]{1,0:T(8,128)(2,1)} async-done(((bf16[136,1024]{1,0:T(8,128)(2,1)}), bf16[1088,1024]{1,0:T(8,128)(2,1)}) %all-gather.13.cloned.1.call-update) | async-done | bytes 2228240 | tf_op jit(solution)/shard_map/all_gather | solution.py:48
  64.3 4.2 %fusion.7 = f32[8,128,512]{2,1,0:T(8,128)} fusion(bf16[8,136,1024]{2,1,0:T(8,128)(2,1)} %bitcast.110, bf16[1024,512]{1,0:T(8,128)(2,1)S(1)} %copy-done), kind=kOutput, calls=%fused_computation.10 | convolution fusion | flops 1073741824 | bytes 5242880 | tf_op jit(solution)/shard_map/enh,hc->enc/dot_general | solution.py:49
  68.5 30.1 %reduce-scatter.4.cloned.1.call-done = f32[1024,128]{1,0:T(8,128)} async-done(((f32[1024,512]{1,0:T(8,128)}), f32[1024,128]{1,0:T(8,128)}) %reduce-scatter.4.cloned.1.call-update) | async-done | bytes 524304 | tf_op jit(solution)/shard_map/reduce_scatter | solution.py:56
  98.6 2.0 copy.40
  100.6 5.5 %all-to-all-start = ((f32[8,128,128]{1,2,0:T(8,128)}), f32[8,128,128]{1,2,0:T(8,128)S(1)}, u32[]{:S(2)}, u32[]{:S(2)}) async-start(f32[8,128,128]{1,2,0:T(8,128)} %copy.40), calls=%async_computation.1 | async-start | bytes 1048576 | tf_op jit(solution)/shard_map/all_to_all | solution.py:57
  106.8 13.8 %all-to-all-done = f32[8,128,128]{1,2,0:T(8,128)S(1)} async-done(((f32[8,128,128]{1,2,0:T(8,128)}), f32[8,128,128]{1,2,0:T(8,128)S(1)}, u32[]{:S(2)}, u32[]{:S(2)}) %all-to-all-start) | async-done | bytes 524320 | tf_op jit(solution)/shard_map/all_to_all | solution.py:57
  122.3 14.3 %all-gather.15.cloned.1.call-done = bf16[32,128,128]{2,1,0:T(8,128)(2,1)} async-done(((bf16[8,128,128]{2,1,0:T(8,128)(2,1)}), bf16[32,128,128]{2,1,0:T(8,128)(2,1)}) %all-gather.15.cloned.1.call-update) | async-done | bytes 1048592 | tf_op jit(solution)/shard_map/all_gather | solution.py:66
  139.4 1.9 reshape.100
  141.6 1.9 multiply_convert_fusion.2
  143.7 77.3 %all-gather.17.cloned.1.call-done = bf16[4096,1024]{1,0:T(8,128)(2,1)} async-done(((bf16[128,1024]{1,0:T(8,128)(2,1)}), bf16[4096,1024]{1,0:T(8,128)(2,1)}) %all-gather.17.cloned.1.call-update) | async-done | bytes 8388624 | tf_op jit(solution)/shard_map/all_gather | solution.py:77
  221.0 3.2 fusion.23
  224.2 3.1 fusion.39
  227.3 2.4 fusion.31
  229.7 2.4 fusion.11
  232.1 2.4 fusion.17
  234.5 2.4 fusion.33
  236.9 2.4 fusion.25
  239.4 3.8 %multiply_convert_fusion = bf16[1024,384]{1,0:T(8,128)(2,1)} fusion(f32[1024,384]{1,0:T(8,128)S(1)} %fusion.23, f32[1024,384]{1,0:T(8,128)S(1)} %fusion.39, f32[1024,384]{1,0:T(8,128)S(1)} %fusion.31, f32[1024,384]{1,0:T(8,128)S(1)} %fusion.11, f32[1024,384]{1,0:T(8,128)S(1)} %fusion.17, f32[1024,384]{1,0:T(8,128)S(1)} %fusion.33, ...), kind=kOutput, calls=%fused_computation.12 | convolution fusion | flops 810024960 | bytes 14680064 | tf_op jit(solution)/shard_map/dot_general | solution.py:90
  243.5 3.2 fusion.19
  246.7 3.4 fusion.35
  250.1 3.2 fusion.27
  253.3 2.4 fusion.14
  255.7 2.4 fusion.21
  258.1 2.4 fusion.37
  260.5 2.4 fusion.29
  262.9 3.8 %multiply_convert_fusion.1 = bf16[1024,384]{1,0:T(8,128)(2,1)} fusion(f32[1024,384]{1,0:T(8,128)S(1)} %fusion.19, f32[1024,384]{1,0:T(8,128)S(1)} %fusion.35, f32[1024,384]{1,0:T(8,128)S(1)} %fusion.27, f32[1024,384]{1,0:T(8,128)S(1)} %fusion.14, f32[1024,384]{1,0:T(8,128)S(1)} %fusion.21, f32[1024,384]{1,0:T(8,128)S(1)} %fusion.37, ...), kind=kOutput, calls=%fused_computation.13 | convolution fusion | flops 810024960 | bytes 14680064 | tf_op jit(solution)/shard_map/dot_general | solution.py:90
  270.4 7.7 %fusion = bf16[1024,1024]{1,0:T(8,128)(2,1)} fusion(bf16[1024,1536]{1,0:T(8,128)(2,1)} %all-gather.11.cloned.1.call-done, bf16[2,1536,1024]{2,1,0:T(8,128)(2,1)} %param.15), kind=kOutput, calls=%fused_computation.1 | convolution fusion | flops 3221225472 | bytes 8388608 | tf_op jit(solution)/shard_map/dot_general | solution.py:98
  278.1 22.3 %all-gather.9.cloned.1.call-done = bf16[1024,1536]{1,0:T(8,128)(2,1)} async-done(((bf16[1024,384]{1,0:T(8,128)(2,1)}), bf16[1024,1536]{1,0:T(8,128)(2,1)}) %all-gather.9.cloned.1.call-update) | async-done | bytes 3145744 | tf_op jit(solution)/shard_map/all_gather | solution.py:97
  300.4 8.6 %add_convert_fusion = bf16[1024,1024]{1,0:T(8,128)(2,1)} fusion(bf16[1024,1024]{1,0:T(8,128)(2,1)} %fusion, f32[1024]{0:T(1024)S(1)} %bitcast.108, f32[1024]{0:T(1024)S(1)} %bitcast.109, pred[1024]{0:T(1024)(128)(4,1)S(1)} %get-tuple-element.9, pred[1024]{0:T(1024)(128)(4,1)S(1)} %get-tuple-element.10, bf16[1024,1536]{1,0:T(8,128)(2,1)} %all-gather.9.cloned.1.call-done, ...), kind=kOutput, calls=%fused_computation | convolution fusion | flops 3230662656 | bytes 10496000 | tf_op jit(solution)/shard_map/dot_general | solution.py:98
  309.1 44.0 %reduce-scatter.6.cloned.1.call-done = bf16[1,256,1024]{2,1,0:T(8,128)(2,1)} async-done(((bf16[4,256,1024]{2,1,0:T(8,128)(2,1)}), bf16[1,256,1024]{2,1,0:T(8,128)(2,1)}) %reduce-scatter.6.cloned.1.call-update) | async-done | bytes 524304 | tf_op jit(solution)/shard_map/reduce_scatter | solution.py:107
  353.1 16.1 %reduce-scatter.8.cloned.1.call-done = bf16[128,1024]{1,0:T(8,128)(2,1)} async-done(((bf16[256,1024]{1,0:T(8,128)(2,1)}), bf16[128,1024]{1,0:T(8,128)(2,1)}) %reduce-scatter.8.cloned.1.call-update) | async-done | bytes 262160 | tf_op jit(solution)/shard_map/reduce_scatter | solution.py:111
  369.2 1.9 add_convert_fusion.1
  (60 shorter events, 13.9 us)
Async XLA Ops:
  6.5 57.7 %copy-start = (bf16[1024,512]{1,0:T(8,128)(2,1)S(1)}, bf16[1024,512]{1,0:T(8,128)(2,1)}, u32[]{:S(2)}) copy-start(bf16[1024,512]{1,0:T(8,128)(2,1)} %param.10) | copy-start | bytes 3145732
  6.5 57.7 %all-gather.13.cloned.1.call-start = ((), (), s32[]{:S(2)}) async-start(), calls=%async_computation.9 | async-start | bytes 2506752 | tf_op jit(solution)/shard_map/all_gather | solution.py:48
  10.8 87.8 %reduce-scatter.4.cloned.1.call-start = ((), (), s32[]{:S(2)}) async-start(), calls=%async_computation.4 | async-start | bytes 2621440 | tf_op jit(solution)/shard_map/reduce_scatter | solution.py:56
  68.5 37.7 %copy-start.3 = (bf16[128,4096]{1,0:T(8,128)(2,1)S(1)}, bf16[128,4096]{1,0:T(8,128)(2,1)}, u32[]{:S(2)}) copy-start(bf16[128,4096]{1,0:T(8,128)(2,1)} %param.11) | copy-start | bytes 3145732
  100.6 20.0 %all-to-all-start = ((f32[8,128,128]{1,2,0:T(8,128)}), f32[8,128,128]{1,2,0:T(8,128)S(1)}, u32[]{:S(2)}, u32[]{:S(2)}) async-start(f32[8,128,128]{1,2,0:T(8,128)} %copy.40), calls=%async_computation.1 | async-start | bytes 1048576 | tf_op jit(solution)/shard_map/all_to_all | solution.py:57
  106.1 30.5 %all-gather.15.cloned.1.call-start = ((), (), s32[]{:S(2)}) async-start(), calls=%async_computation.10 | async-start | bytes 1310720 | tf_op jit(solution)/shard_map/all_gather | solution.py:66
  121.6 99.5 %all-gather.17.cloned.1.call-start = ((), (), s32[]{:S(2)}) async-start(), calls=%async_computation.11 | async-start | bytes 8650752 | tf_op jit(solution)/shard_map/all_gather | solution.py:77
  139.4 1.9 copy-start.2
  143.4 127.0 %all-gather.11.cloned.1.call-start = ((), (), s32[]{:S(2)}) async-start(), calls=%async_computation.6 | async-start | bytes 3932160 | tf_op jit(solution)/shard_map/all_gather | solution.py:97
  221.0 6.3 %copy-start.4 = (bf16[4096,1024]{1,0:T(8,128)(2,1)S(1)}, bf16[4096,1024]{1,0:T(8,128)(2,1)}, u32[]{:S(2)}) copy-start(bf16[4096,1024]{1,0:T(8,128)(2,1)} %all-gather.17.cloned.1.call-done) | copy-start | bytes 25165828
  243.2 57.3 %all-gather.9.cloned.1.call-start = ((), (), s32[]{:S(2)}) async-start(), calls=%async_computation.5 | async-start | bytes 3932160 | tf_op jit(solution)/shard_map/all_gather | solution.py:97
  243.4 9.8 %slice-start = ((s8[8388608]{0:T(1024)(128)(4,1)}), s8[4194304]{0:T(1024)(128)(4,1)S(1)}, s32[]{:S(2)}) async-start(s8[8388608]{0:T(1024)(128)(4,1)} %bitcast.112), calls=%async_computation.12 | async-start | bytes 8388608
  246.6 6.6 %slice-start.1 = ((s8[8388608]{0:T(1024)(128)(4,1)}), s8[4194304]{0:T(1024)(128)(4,1)S(1)}, s32[]{:S(2)}) async-start(s8[8388608]{0:T(1024)(128)(4,1)} %bitcast.112), calls=%async_computation.13 | async-start | bytes 8388608
  266.8 86.3 %reduce-scatter.6.cloned.1.call-start = ((), (), s32[]{:S(2)}) async-start(), calls=%async_computation.7 | async-start | bytes 2621440 | tf_op jit(solution)/shard_map/reduce_scatter | solution.py:107
  300.4 70.7 %copy-start.1 = (bf16[1024,512]{1,0:T(8,128)(2,1)S(1)}, bf16[1024,512]{1,0:T(8,128)(2,1)}, u32[]{:S(2)}) copy-start(bf16[1024,512]{1,0:T(8,128)(2,1)} %param.10) | copy-start | bytes 3145732
  309.1 60.2 %reduce-scatter.8.cloned.1.call-start = ((), (), s32[]{:S(2)}) async-start(), calls=%async_computation.8 | async-start | bytes 786432 | tf_op jit(solution)/shard_map/reduce_scatter | solution.py:111
Sparse Core Ops, SparseCore 0:
  10.9 53.3 all-gather.12
  68.6 29.9 reduce-scatter.3
  121.7 14.8 all-gather.14
  143.6 77.4 all-gather.16
  243.3 27.0 all-gather.10
  271.9 28.4 all-gather.8
  309.2 43.8 reduce-scatter.5
  355.3 13.8 reduce-scatter.7

commit v10 on v9

--- a/solution.py
+++ b/solution.py
@@ -53,17 +53,30 @@
     parts = parts.reshape(groups, 3, tok_count, experts_all).astype(jnp.float32)
     w_all = (parts[:, 0] + parts[:, 1] + parts[:, 2]).reshape(all_tok, experts_all)
     w_mine = lax.dynamic_slice_in_dim(w_all, me_e * exp_local, exp_local, 1)
-    summed = lax.psum_scatter(partial, "tensor", scatter_dimension=1, tiled=True)
+    cores = 2 if tensor_ways % 2 == 0 else 1
+    chips = tensor_ways // cores
+    on_chip = [[y * cores + c for c in range(cores)] for y in range(chips)]
+    across = [[y * cores + c for y in range(chips)] for c in range(cores)]
+    blk_of = [(t % cores) * chips + t // cores for t in range(tensor_ways)]
+    holder = [blk_of.index(b) for b in range(tensor_ways)]
+    blk = lax.rem(me_t, cores) * chips + me_t // cores
+    halves_t = lax.psum_scatter(
+        partial, "tensor", scatter_dimension=1, tiled=True, axis_index_groups=on_chip
+    )
+    summed = lax.psum_scatter(
+        halves_t, "tensor", scatter_dimension=1, tiled=True, axis_index_groups=across
+    )
     mine = lax.all_to_all(
         summed.reshape(groups, tok_count, cols_et), "expert", 0, 0, tiled=False
     )
     res_cols = lax.dynamic_index_in_dim(
-        residual.reshape(tok_count, groups, tensor_ways, cols_et), me_t, 2, keepdims=False
+        residual.reshape(tok_count, groups, tensor_ways, cols_et), blk, 2, keepdims=False
     )
     state_ct = (jnp.transpose(res_cols, (1, 0, 2)).astype(jnp.float32) + mine).astype(
         jnp.bfloat16
     )
     state_all = lax.all_gather(state_ct, "tensor", axis=0, tiled=False)
+    state_all = jnp.stack([state_all[h] for h in holder])
     state = jnp.transpose(state_all, (2, 1, 0, 3)).reshape(tok_count, width)
     state_f = state.astype(jnp.float32)
 

time: 379 us -> 380 us (level)
  waiting for transfers between devices: 272 us -> 276 us
    reduce_scatter x1 -> x2, waiting for transfers between devices: 30.1 us -> 32.1 us  [the longest x1 23.8 us: on_device(): lax.psum_scatter(halves_t, 'tensor', scatter_dimension=1, tiled=True, axi...]
  transfers between devices with their start and end apart: 9 -> 10, of which waited for: 9 -> 10; matrix products, arithmetic and copies ran while one was open for 9% -> 9% of each run, Pallas kernels for 0% -> 0%
where the time goes in v10:
time: 380 us; the launch traced here: 379 us
  waiting for transfers between devices  276 us (73%)
  matrix products  63.6 us (17%)
  between operations  13.5 us (4%)
  local copies, waits for them, and re-layouts  10.6 us (3%)
  other arithmetic  9 us (2%)
  starting transfers between devices  6.51 us (2%)
    all_gather x1, waiting for transfers between devices, on_device(): slabs = lax.all_gather(normed_q, ('tensor', 'expert'), axis=0, tiled=False)  77.3 us
    all_gather x1, waiting for transfers between devices, on_device(): got = lax.all_gather(packet, 'expert', axis=0, tiled=False)  53.5 us
    reduce_scatter x1, waiting for transfers between devices, on_device(): lax.psum_scatter(total.astype(jnp.bfloat16).reshape(far, near * tok_count...  44 us
    dot_general x8, matrix products, on_device(): jnp.dot(x, up_proj[loc, :, a * share:(a + 1) * share].T, preferred_elemen...  26 us
    all_gather x2, waiting for transfers between devices, on_device(): act_all = lax.all_gather(act, 'tensor', axis=1, tiled=True)  24.8 us
    reduce_scatter x1, waiting for transfers between devices, on_device(): lax.psum_scatter(halves_t, 'tensor', scatter_dimension=1, tiled=True, axi...  23.8 us
    dot_general x8, matrix products, on_device(): jnp.dot(x, gate_proj[loc, :, a * share:(a + 1) * share].T, preferred_elem...  19.2 us
    reduce_scatter x1, waiting for transfers between devices, on_device(): lax.psum_scatter(halves.reshape(near * tok_count, share), 'expert', scatt...  16.2 us
  transfers between devices with their start and end apart: 10, of which 10 were waited for; matrix products, arithmetic and copies ran while one was open for 9% of the time, Pallas kernels for 0%

profile of v10, /device:TPU:0, one launch (start us, length us, event | category | flops | bytes accessed | tf_op | source)
XLA Modules:
  0.0 379.1 jit_solution(550422367323397671)
XLA Ops:
  10.8 53.5 %all-gather.13.cloned.1.call-done = bf16[1088,1024]{1,0:T(8,128)(2,1)} async-done(((bf16[136,1024]{1,0:T(8,128)(2,1)}), bf16[1088,1024]{1,0:T(8,128)(2,1)}) %all-gather.13.cloned.1.call-update) | async-done | bytes 2228240 | tf_op jit(solution)/shard_map/all_gather | solution.py:48
  64.3 4.2 %fusion.7 = f32[8,128,512]{2,1,0:T(8,128)} fusion(bf16[8,136,1024]{2,1,0:T(8,128)(2,1)} %bitcast.114, bf16[1024,512]{1,0:T(8,128)(2,1)S(1)} %copy-done), kind=kOutput, calls=%fused_computation.10 | convolution fusion | flops 1073741824 | bytes 5242880 | tf_op jit(solution)/shard_map/enh,hc->enc/dot_general | solution.py:49
  68.5 8.2 %reduce-scatter.5.cloned.1.call-done = f32[1024,256]{1,0:T(8,128)} async-done(((f32[1024,512]{1,0:T(8,128)}), f32[1024,256]{1,0:T(8,128)}) %reduce-scatter.5.cloned.1.call-update) | async-done | bytes 1048592 | tf_op jit(solution)/shard_map/reduce_scatter | solution.py:63
  76.8 23.8 %reduce-scatter.7.cloned.1.call-done = f32[1024,128]{1,0:T(8,128)} async-done(((f32[1024,256]{1,0:T(8,128)}), f32[1024,128]{1,0:T(8,128)}) %reduce-scatter.7.cloned.1.call-update) | async-done | bytes 524304 | tf_op jit(solution)/shard_map/reduce_scatter | solution.py:66
  100.6 2.0 copy.38
  102.7 5.5 %all-to-all-start = ((f32[8,128,128]{1,2,0:T(8,128)}), f32[8,128,128]{1,2,0:T(8,128)S(1)}, u32[]{:S(2)}, u32[]{:S(2)}) async-start(f32[8,128,128]{1,2,0:T(8,128)} %copy.38), calls=%async_computation.2 | async-start | bytes 1048576 | tf_op jit(solution)/shard_map/all_to_all | solution.py:69
  108.9 13.7 %all-to-all-done = f32[8,128,128]{1,2,0:T(8,128)S(1)} async-done(((f32[8,128,128]{1,2,0:T(8,128)}), f32[8,128,128]{1,2,0:T(8,128)S(1)}, u32[]{:S(2)}, u32[]{:S(2)}) %all-to-all-start) | async-done | bytes 524320 | tf_op jit(solution)/shard_map/all_to_all | solution.py:69
  124.3 14.3 %all-gather.15.cloned.1.call-done = bf16[32,128,128]{2,1,0:T(8,128)(2,1)} async-done(((bf16[8,128,128]{2,1,0:T(8,128)(2,1)}), bf16[32,128,128]{2,1,0:T(8,128)(2,1)}) %all-gather.15.cloned.1.call-update) | async-done | bytes 1048592 | tf_op jit(solution)/shard_map/all_gather | solution.py:78
  141.7 1.9 reshape.100
  145.7 77.3 %all-gather.17.cloned.1.call-done = bf16[4096,1024]{1,0:T(8,128)(2,1)} async-done(((bf16[128,1024]{1,0:T(8,128)(2,1)}), bf16[4096,1024]{1,0:T(8,128)(2,1)}) %all-gather.17.cloned.1.call-update) | async-done | bytes 8388624 | tf_op jit(solution)/shard_map/all_gather | solution.py:90
  223.1 3.2 fusion.23
  226.3 3.1 fusion.39
  229.4 2.4 fusion.31
  231.8 2.4 fusion.11
  234.2 2.4 fusion.17
  236.6 2.4 fusion.33
  239.0 2.4 fusion.25
  241.4 3.8 %multiply_convert_fusion = bf16[1024,384]{1,0:T(8,128)(2,1)} fusion(f32[1024,384]{1,0:T(8,128)S(1)} %fusion.23, f32[1024,384]{1,0:T(8,128)S(1)} %fusion.39, f32[1024,384]{1,0:T(8,128)S(1)} %fusion.31, f32[1024,384]{1,0:T(8,128)S(1)} %fusion.11, f32[1024,384]{1,0:T(8,128)S(1)} %fusion.17, f32[1024,384]{1,0:T(8,128)S(1)} %fusion.33, ...), kind=kOutput, calls=%fused_computation.12 | convolution fusion | flops 810024960 | bytes 14680064 | tf_op jit(solution)/shard_map/dot_general | solution.py:103
  245.5 3.2 fusion.19
  248.7 3.4 fusion.35
  252.1 3.2 fusion.27
  255.3 2.4 fusion.14
  257.7 2.4 fusion.21
  260.1 2.4 fusion.37
  262.5 2.4 fusion.29
  265.0 3.8 %multiply_convert_fusion.1 = bf16[1024,384]{1,0:T(8,128)(2,1)} fusion(f32[1024,384]{1,0:T(8,128)S(1)} %fusion.19, f32[1024,384]{1,0:T(8,128)S(1)} %fusion.35, f32[1024,384]{1,0:T(8,128)S(1)} %fusion.27, f32[1024,384]{1,0:T(8,128)S(1)} %fusion.14, f32[1024,384]{1,0:T(8,128)S(1)} %fusion.21, f32[1024,384]{1,0:T(8,128)S(1)} %fusion.37, ...), kind=kOutput, calls=%fused_computation.13 | convolution fusion | flops 810024960 | bytes 14680064 | tf_op jit(solution)/shard_map/dot_general | solution.py:103
  272.5 6.3 %fusion = bf16[1024,1024]{1,0:T(8,128)(2,1)S(1)} fusion(bf16[1024,1536]{1,0:T(8,128)(2,1)} %all-gather.11.cloned.1.call-done, bf16[2,1536,1024]{2,1,0:T(8,128)(2,1)} %param.15), kind=kOutput, calls=%fused_computation.1 | convolution fusion | flops 3221225472 | bytes 8388608 | tf_op jit(solution)/shard_map/dot_general | solution.py:111
  278.7 23.8 %all-gather.9.cloned.1.call-done = bf16[1024,1536]{1,0:T(8,128)(2,1)} async-done(((bf16[1024,384]{1,0:T(8,128)(2,1)}), bf16[1024,1536]{1,0:T(8,128)(2,1)}) %all-gather.9.cloned.1.call-update) | async-done | bytes 3145744 | tf_op jit(solution)/shard_map/all_gather | solution.py:110
  302.5 7.9 %add_convert_fusion = bf16[1024,1024]{1,0:T(8,128)(2,1)} fusion(bf16[1024,1024]{1,0:T(8,128)(2,1)S(1)} %fusion, f32[1024]{0:T(1024)S(1)} %bitcast.112, f32[1024]{0:T(1024)S(1)} %bitcast.113, pred[1024]{0:T(1024)(128)(4,1)S(1)} %get-tuple-element.13, pred[1024]{0:T(1024)(128)(4,1)S(1)} %get-tuple-element.14, ...), kind=kOutput, calls=%fused_computation | convolution fusion | flops 3230662656 | bytes 10496000 | tf_op jit(solution)/shard_map/dot_general | solution.py:111
  310.5 44.0 %reduce-scatter.9.cloned.1.call-done = bf16[1,256,1024]{2,1,0:T(8,128)(2,1)} async-done(((bf16[4,256,1024]{2,1,0:T(8,128)(2,1)}), bf16[1,256,1024]{2,1,0:T(8,128)(2,1)}) %reduce-scatter.9.cloned.1.call-update) | async-done | bytes 524304 | tf_op jit(solution)/shard_map/reduce_scatter | solution.py:120
  354.5 16.2 %reduce-scatter.11.cloned.1.call-done = bf16[128,1024]{1,0:T(8,128)(2,1)} async-done(((bf16[256,1024]{1,0:T(8,128)(2,1)}), bf16[128,1024]{1,0:T(8,128)(2,1)}) %reduce-scatter.11.cloned.1.call-update) | async-done | bytes 262160 | tf_op jit(solution)/shard_map/reduce_scatter | solution.py:124
  370.7 1.9 add_convert_fusion.1
  (62 shorter events, 15.9 us)
Async XLA Ops:
  6.5 57.7 %copy-start = (bf16[1024,512]{1,0:T(8,128)(2,1)S(1)}, bf16[1024,512]{1,0:T(8,128)(2,1)}, u32[]{:S(2)}) copy-start(bf16[1024,512]{1,0:T(8,128)(2,1)} %param.10) | copy-start | bytes 3145732
  6.5 57.7 %all-gather.13.cloned.1.call-start = ((), (), s32[]{:S(2)}) async-start(), calls=%async_computation.11 | async-start | bytes 2506752 | tf_op jit(solution)/shard_map/all_gather | solution.py:48
  10.8 66.0 %reduce-scatter.5.cloned.1.call-start = ((), (), s32[]{:S(2)}) async-start(), calls=%async_computation.5 | async-start | bytes 3145728 | tf_op jit(solution)/shard_map/reduce_scatter | solution.py:63
  68.5 39.8 %copy-start.2 = (bf16[128,4096]{1,0:T(8,128)(2,1)S(1)}, bf16[128,4096]{1,0:T(8,128)(2,1)}, u32[]{:S(2)}) copy-start(bf16[128,4096]{1,0:T(8,128)(2,1)} %param.11) | copy-start | bytes 3145732
  68.5 32.1 %reduce-scatter.7.cloned.1.call-start = ((), (), s32[]{:S(2)}) async-start(), calls=%async_computation.6 | async-start | bytes 1572864 | tf_op jit(solution)/shard_map/reduce_scatter | solution.py:66
  102.7 20.0 %all-to-all-start = ((f32[8,128,128]{1,2,0:T(8,128)}), f32[8,128,128]{1,2,0:T(8,128)S(1)}, u32[]{:S(2)}, u32[]{:S(2)}) async-start(f32[8,128,128]{1,2,0:T(8,128)} %copy.38), calls=%async_computation.2 | async-start | bytes 1048576 | tf_op jit(solution)/shard_map/all_to_all | solution.py:69
  108.2 30.4 %all-gather.15.cloned.1.call-start = ((), (), s32[]{:S(2)}) async-start(), calls=%async_computation.12 | async-start | bytes 1310720 | tf_op jit(solution)/shard_map/all_gather | solution.py:78
  123.6 99.5 %all-gather.17.cloned.1.call-start = ((), (), s32[]{:S(2)}) async-start(), calls=%async_computation.13 | async-start | bytes 8650752 | tf_op jit(solution)/shard_map/all_gather | solution.py:90
  145.5 127.0 %all-gather.11.cloned.1.call-start = ((), (), s32[]{:S(2)}) async-start(), calls=%async_computation.8 | async-start | bytes 3932160 | tf_op jit(solution)/shard_map/all_gather | solution.py:110
  223.1 6.3 %copy-start.3 = (bf16[4096,1024]{1,0:T(8,128)(2,1)S(1)}, bf16[4096,1024]{1,0:T(8,128)(2,1)}, u32[]{:S(2)}) copy-start(bf16[4096,1024]{1,0:T(8,128)(2,1)} %all-gather.17.cloned.1.call-done) | copy-start | bytes 25165828
  245.2 57.3 %all-gather.9.cloned.1.call-start = ((), (), s32[]{:S(2)}) async-start(), calls=%async_computation.7 | async-start | bytes 3932160 | tf_op jit(solution)/shard_map/all_gather | solution.py:110
  245.5 9.8 %slice-start = ((s8[8388608]{0:T(1024)(128)(4,1)}), s8[4194304]{0:T(1024)(128)(4,1)S(1)}, s32[]{:S(2)}) async-start(s8[8388608]{0:T(1024)(128)(4,1)} %bitcast.116), calls=%async_computation.14 | async-start | bytes 8388608
  248.7 6.6 %slice-start.1 = ((s8[8388608]{0:T(1024)(128)(4,1)}), s8[4194304]{0:T(1024)(128)(4,1)S(1)}, s32[]{:S(2)}) async-start(s8[8388608]{0:T(1024)(128)(4,1)} %bitcast.116), calls=%async_computation.15 | async-start | bytes 8388608
  268.8 85.7 %reduce-scatter.9.cloned.1.call-start = ((), (), s32[]{:S(2)}) async-start(), calls=%async_computation.9 | async-start | bytes 2621440 | tf_op jit(solution)/shard_map/reduce_scatter | solution.py:120
  302.5 70.1 %copy-start.1 = (bf16[1024,512]{1,0:T(8,128)(2,1)S(1)}, bf16[1024,512]{1,0:T(8,128)(2,1)}, u32[]{:S(2)}) copy-start(bf16[1024,512]{1,0:T(8,128)(2,1)} %param.10) | copy-start | bytes 3145732
  310.5 60.3 %reduce-scatter.11.cloned.1.call-start = ((), (), s32[]{:S(2)}) async-start(), calls=%async_computation.10 | async-start | bytes 786432 | tf_op jit(solution)/shard_map/reduce_scatter | solution.py:124
Sparse Core Ops, SparseCore 0:
  10.9 53.3 all-gather.12
  68.6 8.1 reduce-scatter.4
  79.1 21.4 reduce-scatter.6
  123.7 14.8 all-gather.14
  145.6 77.4 all-gather.16
  245.3 27.0 all-gather.10
  274.0 28.4 all-gather.8
  310.6 43.8 reduce-scatter.8
  356.8 13.8 reduce-scatter.10

commit v11 on v9

--- a/solution.py
+++ b/solution.py
@@ -45,7 +45,13 @@
     coded = jnp.pad(coded, (0, extra * heads_w - coded.shape[0])).reshape(extra, heads_w)
     packet = jnp.concatenate([attn_heads, coded], axis=0)
 
-    got = lax.all_gather(packet, "expert", axis=0, tiled=False)
+    near = 2 if groups % 2 == 0 else 1
+    far = groups // near
+    pairs = [[z * near + x for x in range(near)] for z in range(far)]
+    lines = [[z * near + x for z in range(far)] for x in range(near)]
+    along_z = lax.all_gather(packet, "expert", axis=0, tiled=False, axis_index_groups=lines)
+    got = lax.all_gather(along_z, "expert", axis=0, tiled=False, axis_index_groups=pairs)
+    got = jnp.transpose(got, (1, 0, 2, 3)).reshape((groups,) + packet.shape)
     partial = jnp.einsum(
         "enh,hc->enc", got[:, :tok_count], out_proj, preferred_element_type=jnp.float32
     ).reshape(all_tok, cols_e)
@@ -100,10 +106,6 @@
         ).astype(jnp.bfloat16)
         w_tok = w_mine[:, loc][:, None]
         total = total + jnp.where(w_tok > 0, w_tok * out.astype(jnp.float32), 0.0)
-    near = 2 if groups % 2 == 0 else 1
-    far = groups // near
-    pairs = [[z * near + x for x in range(near)] for z in range(far)]
-    lines = [[z * near + x for z in range(far)] for x in range(near)]
     halves = lax.psum_scatter(
         total.astype(jnp.bfloat16).reshape(far, near * tok_count, share), "expert",
         scatter_dimension=0, tiled=True, axis_index_groups=lines,

time: 379 us -> 395 us (1.042)
  waiting for transfers between devices: 272 us -> 288 us
    all_gather x1 -> x2, waiting for transfers between devices: 53.5 us -> 67.4 us  [the longest x1 35.6 us: on_device(): lax.all_gather(along_z, 'expert', axis=0, tiled=False, axis_index_groups=...]
  transfers between devices with their start and end apart: 9 -> 10, of which waited for: 9 -> 10; matrix products, arithmetic and copies ran while one was open for 9% -> 9% of each run, Pallas kernels for 0% -> 0%
where the time goes in v11:
time: 395 us; the launch traced here: 394 us
  waiting for transfers between devices  288 us (73%)
  matrix products  64.2 us (16%)
  between operations  13.5 us (3%)
  local copies, waits for them, and re-layouts  11.2 us (3%)
  other arithmetic  10.3 us (3%)
  starting transfers between devices  6.49 us (2%)
    all_gather x1, waiting for transfers between devices, on_device(): slabs = lax.all_gather(normed_q, ('tensor', 'expert'), axis=0, tiled=False)  77.3 us
    reduce_scatter x1, waiting for transfers between devices, on_device(): lax.psum_scatter(total.astype(jnp.bfloat16).reshape(far, near * tok_count...  44 us
    all_gather x1, waiting for transfers between devices, on_device(): lax.all_gather(along_z, 'expert', axis=0, tiled=False, axis_index_groups=...  35.6 us
    all_gather x1, waiting for transfers between devices, on_device(): lax.all_gather(packet, 'expert', axis=0, tiled=False, axis_index_groups=l...  31.8 us
    reduce_scatter x1, waiting for transfers between devices, on_device(): lax.psum_scatter(partial, 'tensor', scatter_dimension=1, tiled=True)  31.6 us
    dot_general x8, matrix products, on_device(): jnp.dot(x, up_proj[loc, :, a * share:(a + 1) * share].T, preferred_elemen...  26 us
    all_gather x2, waiting for transfers between devices, on_device(): act_all = lax.all_gather(act, 'tensor', axis=1, tiled=True)  23.4 us
    dot_general x8, matrix products, on_device(): jnp.dot(x, gate_proj[loc, :, a * share:(a + 1) * share].T, preferred_elem...  19.2 us
  transfers between devices with their start and end apart: 10, of which 10 were waited for; matrix products, arithmetic and copies ran while one was open for 9% of the time, Pallas kernels for 0%

profile of v11, /device:TPU:0, one launch (start us, length us, event | category | flops | bytes accessed | tf_op | source)
XLA Modules:
  0.0 393.6 jit_solution(4687421589810715888)
XLA Ops:
  10.8 31.8 %all-gather.15.cloned.1.call-done = bf16[544,1024]{1,0:T(8,128)(2,1)} async-done(((bf16[136,1024]{1,0:T(8,128)(2,1)}), bf16[544,1024]{1,0:T(8,128)(2,1)}) %all-gather.15.cloned.1.call-update) | async-done | bytes 1114128 | tf_op jit(solution)/shard_map/all_gather | solution.py:52
  42.7 35.6 %all-gather.17.cloned.1.call-done = bf16[8,136,1024]{2,1,0:T(8,128)(2,1)} async-done(((bf16[4,136,1024]{2,1,0:T(8,128)(2,1)}), bf16[8,136,1024]{2,1,0:T(8,128)(2,1)}) %all-gather.17.cloned.1.call-update) | async-done | bytes 2228240 | tf_op jit(solution)/shard_map/all_gather | solution.py:53
  80.1 2.6 fusion.7
  82.8 31.6 %reduce-scatter.4.cloned.1.call-done = f32[1024,128]{1,0:T(8,128)} async-done(((f32[1024,512]{1,0:T(8,128)}), f32[1024,128]{1,0:T(8,128)}) %reduce-scatter.4.cloned.1.call-update) | async-done | bytes 524304 | tf_op jit(solution)/shard_map/reduce_scatter | solution.py:62
  114.4 2.0 copy.45
  116.4 5.5 %all-to-all-start = ((f32[8,128,128]{1,2,0:T(8,128)}), f32[8,128,128]{1,2,0:T(8,128)S(1)}, u32[]{:S(2)}, u32[]{:S(2)}) async-start(f32[8,128,128]{1,2,0:T(8,128)} %copy.45), calls=%async_computation.1 | async-start | bytes 1048576 | tf_op jit(solution)/shard_map/all_to_all | solution.py:63
  122.6 13.8 %all-to-all-done = f32[8,128,128]{1,2,0:T(8,128)S(1)} async-done(((f32[8,128,128]{1,2,0:T(8,128)}), f32[8,128,128]{1,2,0:T(8,128)S(1)}, u32[]{:S(2)}, u32[]{:S(2)}) %all-to-all-start) | async-done | bytes 524320 | tf_op jit(solution)/shard_map/all_to_all | solution.py:63
  138.1 14.3 %all-gather.19.cloned.1.call-done = bf16[32,128,128]{2,1,0:T(8,128)(2,1)} async-done(((bf16[8,128,128]{2,1,0:T(8,128)(2,1)}), bf16[32,128,128]{2,1,0:T(8,128)(2,1)}) %all-gather.19.cloned.1.call-update) | async-done | bytes 1048592 | tf_op jit(solution)/shard_map/all_gather | solution.py:72
  155.2 1.9 reshape.104
  159.5 77.3 %all-gather.21.cloned.1.call-done = bf16[4096,1024]{1,0:T(8,128)(2,1)} async-done(((bf16[128,1024]{1,0:T(8,128)(2,1)}), bf16[4096,1024]{1,0:T(8,128)(2,1)}) %all-gather.21.cloned.1.call-update) | async-done | bytes 8388624 | tf_op jit(solution)/shard_map/all_gather | solution.py:83
  236.8 3.2 fusion.23
  240.0 3.1 fusion.39
  243.1 2.4 fusion.31
  245.5 2.4 fusion.11
  248.0 2.4 fusion.17
  250.4 2.4 fusion.33
  252.8 2.4 fusion.25
  255.2 3.8 multiply_convert_fusion
  259.3 3.2 fusion.19
  262.5 3.4 fusion.35
  265.9 3.2 fusion.27
  269.1 2.4 fusion.14
  271.5 2.4 fusion.21
  273.9 2.4 fusion.37
  276.3 2.4 fusion.29
  278.7 3.8 multiply_convert_fusion.1
  286.2 7.7 %fusion = bf16[1024,1024]{1,0:T(8,128)(2,1)} fusion(bf16[1024,1536]{1,0:T(8,128)(2,1)} %all-gather.13.cloned.1.call-done, bf16[2,1536,1024]{2,1,0:T(8,128)(2,1)} %param.15), kind=kOutput, calls=%fused_computation.1 | convolution fusion | flops 3221225472 | bytes 8388608 | tf_op jit(solution)/shard_map/dot_general | solution.py:104
  293.9 22.5 %all-gather.11.cloned.1.call-done = bf16[1024,1536]{1,0:T(8,128)(2,1)} async-done(((bf16[1024,384]{1,0:T(8,128)(2,1)}), bf16[1024,1536]{1,0:T(8,128)(2,1)}) %all-gather.11.cloned.1.call-update) | async-done | bytes 3145744 | tf_op jit(solution)/shard_map/all_gather | solution.py:103
  316.4 8.6 %add_convert_fusion = bf16[1024,1024]{1,0:T(8,128)(2,1)} fusion(bf16[1024,1024]{1,0:T(8,128)(2,1)} %fusion, f32[1024]{0:T(1024)S(1)} %bitcast.116, f32[1024]{0:T(1024)S(1)} %bitcast.117, pred[1024]{0:T(1024)(128)(4,1)S(1)} %get-tuple-element.9, pred[1024]{0:T(1024)(128)(4,1)S(1)} %get-tuple-element.10, bf16[1024,1536]{1,0:T(8,128)(2,1)} %all-gather.11.cloned.1.call-done, ...), kind=kOutput, calls=%fused_computation | convolution fusion | flops 3230662656 | bytes 10496000 | tf_op jit(solution)/shard_map/dot_general | solution.py:104
  325.1 44.0 %reduce-scatter.6.cloned.1.call-done = bf16[1,256,1024]{2,1,0:T(8,128)(2,1)} async-done(((bf16[4,256,1024]{2,1,0:T(8,128)(2,1)}), bf16[1,256,1024]{2,1,0:T(8,128)(2,1)}) %reduce-scatter.6.cloned.1.call-update) | async-done | bytes 524304 | tf_op jit(solution)/shard_map/reduce_scatter | solution.py:109
  369.1 16.1 %reduce-scatter.8.cloned.1.call-done = bf16[128,1024]{1,0:T(8,128)(2,1)} async-done(((bf16[256,1024]{1,0:T(8,128)(2,1)}), bf16[128,1024]{1,0:T(8,128)(2,1)}) %reduce-scatter.8.cloned.1.call-update) | async-done | bytes 262160 | tf_op jit(solution)/shard_map/reduce_scatter | solution.py:113
  385.2 1.9 add_convert_fusion.1
  (66 shorter events, 17.7 us)
Async XLA Ops:
  6.5 73.6 %copy-start = (bf16[1024,512]{1,0:T(8,128)(2,1)S(1)}, bf16[1024,512]{1,0:T(8,128)(2,1)}, u32[]{:S(2)}) copy-start(bf16[1024,512]{1,0:T(8,128)(2,1)} %param.10) | copy-start | bytes 3145732
  6.5 36.1 %all-gather.15.cloned.1.call-start = ((), (), s32[]{:S(2)}) async-start(), calls=%async_computation.9 | async-start | bytes 1392640 | tf_op jit(solution)/shard_map/all_gather | solution.py:52
  10.8 67.5 %all-gather.17.cloned.1.call-start = ((), (), s32[]{:S(2)}) async-start(), calls=%async_computation.10 | async-start | bytes 3342336 | tf_op jit(solution)/shard_map/all_gather | solution.py:53
  42.6 71.7 %reduce-scatter.4.cloned.1.call-start = ((), (), s32[]{:S(2)}) async-start(), calls=%async_computation.4 | async-start | bytes 2621440 | tf_op jit(solution)/shard_map/reduce_scatter | solution.py:62
  80.1 2.6 copy-start.3
  82.7 39.2 %copy-start.4 = (bf16[128,4096]{1,0:T(8,128)(2,1)S(1)}, bf16[128,4096]{1,0:T(8,128)(2,1)}, u32[]{:S(2)}) copy-start(bf16[128,4096]{1,0:T(8,128)(2,1)} %param.11) | copy-start | bytes 3145732
  116.4 20.0 %all-to-all-start = ((f32[8,128,128]{1,2,0:T(8,128)}), f32[8,128,128]{1,2,0:T(8,128)S(1)}, u32[]{:S(2)}, u32[]{:S(2)}) async-start(f32[8,128,128]{1,2,0:T(8,128)} %copy.45), calls=%async_computation.1 | async-start | bytes 1048576 | tf_op jit(solution)/shard_map/all_to_all | solution.py:63
  121.9 30.4 %all-gather.19.cloned.1.call-start = ((), (), s32[]{:S(2)}) async-start(), calls=%async_computation.11 | async-start | bytes 1310720 | tf_op jit(solution)/shard_map/all_gather | solution.py:72
  137.3 99.5 %all-gather.21.cloned.1.call-start = ((), (), s32[]{:S(2)}) async-start(), calls=%async_computation.12 | async-start | bytes 8650752 | tf_op jit(solution)/shard_map/all_gather | solution.py:83
  155.2 1.9 copy-start.2
  159.3 127.0 %all-gather.13.cloned.1.call-start = ((), (), s32[]{:S(2)}) async-start(), calls=%async_computation.6 | async-start | bytes 3932160 | tf_op jit(solution)/shard_map/all_gather | solution.py:103
  236.8 6.3 %copy-start.5 = (bf16[4096,1024]{1,0:T(8,128)(2,1)S(1)}, bf16[4096,1024]{1,0:T(8,128)(2,1)}, u32[]{:S(2)}) copy-start(bf16[4096,1024]{1,0:T(8,128)(2,1)} %all-gather.21.cloned.1.call-done) | copy-start | bytes 25165828
  259.0 57.4 %all-gather.11.cloned.1.call-start = ((), (), s32[]{:S(2)}) async-start(), calls=%async_computation.5 | async-start | bytes 3932160 | tf_op jit(solution)/shard_map/all_gather | solution.py:103
  259.3 9.8 %slice-start = ((s8[8388608]{0:T(1024)(128)(4,1)}), s8[4194304]{0:T(1024)(128)(4,1)S(1)}, s32[]{:S(2)}) async-start(s8[8388608]{0:T(1024)(128)(4,1)} %bitcast.118), calls=%async_computation.13 | async-start | bytes 8388608
  262.5 6.6 %slice-start.1 = ((s8[8388608]{0:T(1024)(128)(4,1)}), s8[4194304]{0:T(1024)(128)(4,1)S(1)}, s32[]{:S(2)}) async-start(s8[8388608]{0:T(1024)(128)(4,1)} %bitcast.118), calls=%async_computation.14 | async-start | bytes 8388608
  282.6 86.5 %reduce-scatter.6.cloned.1.call-start = ((), (), s32[]{:S(2)}) async-start(), calls=%async_computation.7 | async-start | bytes 2621440 | tf_op jit(solution)/shard_map/reduce_scatter | solution.py:109
  316.4 70.7 %copy-start.1 = (bf16[1024,512]{1,0:T(8,128)(2,1)S(1)}, bf16[1024,512]{1,0:T(8,128)(2,1)}, u32[]{:S(2)}) copy-start(bf16[1024,512]{1,0:T(8,128)(2,1)} %param.10) | copy-start | bytes 3145732
  325.0 60.2 %reduce-scatter.8.cloned.1.call-start = ((), (), s32[]{:S(2)}) async-start(), calls=%async_computation.8 | async-start | bytes 786432 | tf_op jit(solution)/shard_map/reduce_scatter | solution.py:113
Sparse Core Ops, SparseCore 0:
  10.9 31.6 all-gather.14
  44.2 34.0 all-gather.16
  82.9 31.4 reduce-scatter.3
  137.5 14.8 all-gather.18
  159.4 77.4 all-gather.20
  259.1 27.0 all-gather.12
  287.9 28.4 all-gather.10
  325.1 43.8 reduce-scatter.5
  371.3 13.8 reduce-scatter.7

commit v12 on v9

--- a/solution.py
+++ b/solution.py
@@ -54,15 +54,14 @@
     w_all = (parts[:, 0] + parts[:, 1] + parts[:, 2]).reshape(all_tok, experts_all)
     w_mine = lax.dynamic_slice_in_dim(w_all, me_e * exp_local, exp_local, 1)
     summed = lax.psum_scatter(partial, "tensor", scatter_dimension=1, tiled=True)
-    mine = lax.all_to_all(
-        summed.reshape(groups, tok_count, cols_et), "expert", 0, 0, tiled=False
-    )
-    res_cols = lax.dynamic_index_in_dim(
+    res_out = lax.dynamic_index_in_dim(
         residual.reshape(tok_count, groups, tensor_ways, cols_et), me_t, 2, keepdims=False
     )
-    state_ct = (jnp.transpose(res_cols, (1, 0, 2)).astype(jnp.float32) + mine).astype(
-        jnp.bfloat16
-    )
+    res_in = lax.all_to_all(jnp.transpose(res_out, (1, 0, 2)), "expert", 0, 0, tiled=False)
+    state_slab = (
+        res_in.astype(jnp.float32) + summed.reshape(groups, tok_count, cols_et)
+    ).astype(jnp.bfloat16)
+    state_ct = lax.all_to_all(state_slab, "expert", 0, 0, tiled=False)
     state_all = lax.all_gather(state_ct, "tensor", axis=0, tiled=False)
     state = jnp.transpose(state_all, (2, 1, 0, 3)).reshape(tok_count, width)
     state_f = state.astype(jnp.float32)

time: 379 us -> 371 us (0.979)
  waiting for transfers between devices: 272 us -> 245 us
  blocking collectives: 0 us -> 26.1 us
  starting transfers between devices: 6.46 us -> 0.96 us
    all_to_all x0 -> x2, blocking collectives: none -> 26.1 us  [the longest x1 14.3 us: on_device(): state_ct = lax.all_to_all(state_slab, 'expert', 0, 0, tiled=False)]
    reduce_scatter x1, waiting for transfers between devices: 30.1 us -> 16.3 us  [on_device(): lax.psum_scatter(partial, 'tensor', scatter_dimension=1, tiled=True)]
    all_to_all x1 -> x0, waiting for transfers between devices: 13.8 us -> none  [on_device(): lax.all_to_all(summed.reshape(groups, tok_count, cols_et), 'expert', 0, 0...]
    all_to_all x1 -> x0, starting transfers between devices: 5.51 us -> none  [on_device(): lax.all_to_all(summed.reshape(groups, tok_count, cols_et), 'expert', 0, 0...]
  transfers between devices with their start and end apart: 9 -> 8, of which waited for: 9 -> 8; matrix products, arithmetic and copies ran while one was open for 9% -> 9% of each run, Pallas kernels for 0% -> 0%
where the time goes in v12:
time: 371 us; the launch traced here: 370 us
  waiting for transfers between devices  245 us (66%)
  matrix products  65.8 us (18%)
  blocking collectives  26.1 us (7%)
  between operations  13.7 us (4%)
  other arithmetic  11.3 us (3%)
  local copies, waits for them, and re-layouts  7.78 us (2%)
    all_gather x1, waiting for transfers between devices, on_device(): slabs = lax.all_gather(normed_q, ('tensor', 'expert'), axis=0, tiled=False)  77.3 us
    all_gather x1, waiting for transfers between devices, on_device(): got = lax.all_gather(packet, 'expert', axis=0, tiled=False)  53.5 us
    reduce_scatter x1, waiting for transfers between devices, on_device(): lax.psum_scatter(total.astype(jnp.bfloat16).reshape(far, near * tok_count...  44 us
    dot_general x8, matrix products, on_device(): jnp.dot(x, up_proj[loc, :, a * share:(a + 1) * share].T, preferred_elemen...  26.1 us
    all_gather x2, waiting for transfers between devices, on_device(): act_all = lax.all_gather(act, 'tensor', axis=1, tiled=True)  23.2 us
    dot_general x8, matrix products, on_device(): jnp.dot(x, gate_proj[loc, :, a * share:(a + 1) * share].T, preferred_elem...  19.2 us
    dot_general x2, matrix products, on_device(): jnp.dot(act_all, down_proj[loc], preferred_element_type=jnp.float32)  16.3 us
    reduce_scatter x1, waiting for transfers between devices, on_device(): lax.psum_scatter(partial, 'tensor', scatter_dimension=1, tiled=True)  16.3 us
  transfers between devices with their start and end apart: 8, of which 8 were waited for; matrix products, arithmetic and copies ran while one was open for 9% of the time, Pallas kernels for 0%

profile of v12, /device:TPU:0, one launch (start us, length us, event | category | flops | bytes accessed | tf_op | source)
XLA Modules:
  0.0 370.4 jit_solution(12673345084612807280)
XLA Ops:
  9.1 1.7 pad_maximum_fusion
  10.8 53.5 %all-gather.13.cloned.1.call-done = bf16[1088,1024]{1,0:T(8,128)(2,1)} async-done(((bf16[136,1024]{1,0:T(8,128)(2,1)}), bf16[1088,1024]{1,0:T(8,128)(2,1)}) %all-gather.13.cloned.1.call-update) | async-done | bytes 2228240 | tf_op jit(solution)/shard_map/all_gather | solution.py:48
  64.3 4.2 %fusion.7 = f32[8,128,512]{2,1,0:T(8,128)} fusion(bf16[8,136,1024]{2,1,0:T(8,128)(2,1)} %bitcast.105, bf16[1024,512]{1,0:T(8,128)(2,1)S(1)} %copy-done), kind=kOutput, calls=%fused_computation.10 | convolution fusion | flops 1073741824 | bytes 5242880 | tf_op jit(solution)/shard_map/enh,hc->enc/dot_general | solution.py:49
  70.5 11.7 %all_to_all.10 = bf16[8,128,128]{2,1,0:T(8,128)(2,1)S(1)} all-to-all(bf16[8,128,128]{2,1,0:T(8,128)(2,1)S(1)} %copy.43), channel_id=1, replica_groups=mesh['expert'=8,'tensor'=4] {'expert'}, dimensions={0} | all-to-all | bytes 524288 | tf_op jit(solution)/shard_map/all_to_all | solution.py:60
  82.3 16.3 %reduce-scatter.4.cloned.1.call-done = f32[1024,128]{1,0:T(8,128)} async-done(((f32[1024,512]{1,0:T(8,128)}), f32[1024,128]{1,0:T(8,128)}) %reduce-scatter.4.cloned.1.call-update) | async-done | bytes 524304 | tf_op jit(solution)/shard_map/reduce_scatter | solution.py:56
  99.7 14.3 %all_to_all.11 = bf16[8,128,128]{2,1,0:T(8,128)(2,1)} all-to-all(bf16[8,128,128]{2,1,0:T(8,128)(2,1)S(1)} %add_convert_fusion.2), channel_id=1, replica_groups=mesh['expert'=8,'tensor'=4] {'expert'}, dimensions={0} | all-to-all | bytes 524288 | tf_op jit(solution)/shard_map/all_to_all | solution.py:64
  114.8 14.2 %all-gather.15.cloned.1.call-done = bf16[32,128,128]{2,1,0:T(8,128)(2,1)} async-done(((bf16[8,128,128]{2,1,0:T(8,128)(2,1)}), bf16[32,128,128]{2,1,0:T(8,128)(2,1)}) %all-gather.15.cloned.1.call-update) | async-done | bytes 1048592 | tf_op jit(solution)/shard_map/all_gather | solution.py:65
  131.8 1.9 reshape.98
  134.0 1.9 multiply_convert_fusion.2
  136.1 77.3 %all-gather.17.cloned.1.call-done = bf16[4096,1024]{1,0:T(8,128)(2,1)} async-done(((bf16[128,1024]{1,0:T(8,128)(2,1)}), bf16[4096,1024]{1,0:T(8,128)(2,1)}) %all-gather.17.cloned.1.call-update) | async-done | bytes 8388624 | tf_op jit(solution)/shard_map/all_gather | solution.py:76
  213.5 3.2 fusion.23
  216.6 3.1 fusion.39
  219.8 2.4 fusion.31
  222.2 2.4 fusion.11
  224.6 2.4 fusion.17
  227.0 2.4 fusion.33
  229.4 2.4 fusion.25
  231.8 3.8 %multiply_convert_fusion = bf16[1024,384]{1,0:T(8,128)(2,1)} fusion(f32[1024,384]{1,0:T(8,128)S(1)} %fusion.23, f32[1024,384]{1,0:T(8,128)S(1)} %fusion.39, f32[1024,384]{1,0:T(8,128)S(1)} %fusion.31, f32[1024,384]{1,0:T(8,128)S(1)} %fusion.11, f32[1024,384]{1,0:T(8,128)S(1)} %fusion.17, f32[1024,384]{1,0:T(8,128)S(1)} %fusion.33, ...), kind=kOutput, calls=%fused_computation.12 | convolution fusion | flops 810024960 | bytes 14680064 | tf_op jit(solution)/shard_map/dot_general | solution.py:89
  235.9 3.2 fusion.19
  239.1 3.4 fusion.35
  242.5 3.2 fusion.27
  245.7 2.4 fusion.14
  248.1 2.4 fusion.21
  250.5 2.4 fusion.37
  252.9 2.4 fusion.29
  255.4 3.8 %multiply_convert_fusion.1 = bf16[1024,384]{1,0:T(8,128)(2,1)} fusion(f32[1024,384]{1,0:T(8,128)S(1)} %fusion.19, f32[1024,384]{1,0:T(8,128)S(1)} %fusion.35, f32[1024,384]{1,0:T(8,128)S(1)} %fusion.27, f32[1024,384]{1,0:T(8,128)S(1)} %fusion.14, f32[1024,384]{1,0:T(8,128)S(1)} %fusion.21, f32[1024,384]{1,0:T(8,128)S(1)} %fusion.37, ...), kind=kOutput, calls=%fused_computation.13 | convolution fusion | flops 810024960 | bytes 14680064 | tf_op jit(solution)/shard_map/dot_general | solution.py:89
  262.9 7.7 %fusion = bf16[1024,1024]{1,0:T(8,128)(2,1)} fusion(bf16[1024,1536]{1,0:T(8,128)(2,1)} %all-gather.11.cloned.1.call-done, bf16[2,1536,1024]{2,1,0:T(8,128)(2,1)} %param.15), kind=kOutput, calls=%fused_computation.1 | convolution fusion | flops 3221225472 | bytes 8388608 | tf_op jit(solution)/shard_map/dot_general | solution.py:97
  270.6 22.3 %all-gather.9.cloned.1.call-done = bf16[1024,1536]{1,0:T(8,128)(2,1)} async-done(((bf16[1024,384]{1,0:T(8,128)(2,1)}), bf16[1024,1536]{1,0:T(8,128)(2,1)}) %all-gather.9.cloned.1.call-update) | async-done | bytes 3145744 | tf_op jit(solution)/shard_map/all_gather | solution.py:96
  292.9 8.6 %add_convert_fusion = bf16[1024,1024]{1,0:T(8,128)(2,1)} fusion(bf16[1024,1024]{1,0:T(8,128)(2,1)} %fusion, f32[1024]{0:T(1024)S(1)} %bitcast.103, f32[1024]{0:T(1024)S(1)} %bitcast.104, pred[1024]{0:T(1024)(128)(4,1)S(1)} %get-tuple-element.9, pred[1024]{0:T(1024)(128)(4,1)S(1)} %get-tuple-element.10, bf16[1024,1536]{1,0:T(8,128)(2,1)} %all-gather.9.cloned.1.call-done, ...), kind=kOutput, calls=%fused_computation | convolution fusion | flops 3230662656 | bytes 10496000 | tf_op jit(solution)/shard_map/dot_general | solution.py:97
  301.5 44.0 %reduce-scatter.6.cloned.1.call-done = bf16[1,256,1024]{2,1,0:T(8,128)(2,1)} async-done(((bf16[4,256,1024]{2,1,0:T(8,128)(2,1)}), bf16[1,256,1024]{2,1,0:T(8,128)(2,1)}) %reduce-scatter.6.cloned.1.call-update) | async-done | bytes 524304 | tf_op jit(solution)/shard_map/reduce_scatter | solution.py:106
  345.5 16.1 %reduce-scatter.8.cloned.1.call-done = bf16[128,1024]{1,0:T(8,128)(2,1)} async-done(((bf16[256,1024]{1,0:T(8,128)(2,1)}), bf16[128,1024]{1,0:T(8,128)(2,1)}) %reduce-scatter.8.cloned.1.call-update) | async-done | bytes 262160 | tf_op jit(solution)/shard_map/reduce_scatter | solution.py:110
  361.6 1.9 add_convert_fusion.1
  (60 shorter events, 13.8 us)
Async XLA Ops:
  6.5 57.7 %copy-start = (bf16[1024,512]{1,0:T(8,128)(2,1)S(1)}, bf16[1024,512]{1,0:T(8,128)(2,1)}, u32[]{:S(2)}) copy-start(bf16[1024,512]{1,0:T(8,128)(2,1)} %param.10) | copy-start | bytes 3145732
  6.5 57.7 %all-gather.13.cloned.1.call-start = ((), (), s32[]{:S(2)}) async-start(), calls=%async_computation.10 | async-start | bytes 2506752 | tf_op jit(solution)/shard_map/all_gather | solution.py:48
  10.8 87.8 %reduce-scatter.4.cloned.1.call-start = ((), (), s32[]{:S(2)}) async-start(), calls=%async_computation.5 | async-start | bytes 2621440 | tf_op jit(solution)/shard_map/reduce_scatter | solution.py:56
  68.4 1.2 copy-start.3
  68.5 60.5 %all-gather.15.cloned.1.call-start = ((), (), s32[]{:S(2)}) async-start(), calls=%async_computation.11 | async-start | bytes 1310720 | tf_op jit(solution)/shard_map/all_gather | solution.py:65
  114.0 99.4 %all-gather.17.cloned.1.call-start = ((), (), s32[]{:S(2)}) async-start(), calls=%async_computation.12 | async-start | bytes 8650752 | tf_op jit(solution)/shard_map/all_gather | solution.py:76
  131.8 1.9 copy-start.2
  135.9 127.0 %all-gather.11.cloned.1.call-start = ((), (), s32[]{:S(2)}) async-start(), calls=%async_computation.7 | async-start | bytes 3932160 | tf_op jit(solution)/shard_map/all_gather | solution.py:96
  213.5 6.3 %copy-start.4 = (bf16[4096,1024]{1,0:T(8,128)(2,1)S(1)}, bf16[4096,1024]{1,0:T(8,128)(2,1)}, u32[]{:S(2)}) copy-start(bf16[4096,1024]{1,0:T(8,128)(2,1)} %all-gather.17.cloned.1.call-done) | copy-start | bytes 25165828
  235.6 57.3 %all-gather.9.cloned.1.call-start = ((), (), s32[]{:S(2)}) async-start(), calls=%async_computation.6 | async-start | bytes 3932160 | tf_op jit(solution)/shard_map/all_gather | solution.py:96
  235.9 9.8 %slice-start = ((s8[8388608]{0:T(1024)(128)(4,1)}), s8[4194304]{0:T(1024)(128)(4,1)S(1)}, s32[]{:S(2)}) async-start(s8[8388608]{0:T(1024)(128)(4,1)} %bitcast.107), calls=%async_computation.13 | async-start | bytes 8388608
  239.1 6.6 %slice-start.1 = ((s8[8388608]{0:T(1024)(128)(4,1)}), s8[4194304]{0:T(1024)(128)(4,1)S(1)}, s32[]{:S(2)}) async-start(s8[8388608]{0:T(1024)(128)(4,1)} %bitcast.107), calls=%async_computation.14 | async-start | bytes 8388608
  259.2 86.3 %reduce-scatter.6.cloned.1.call-start = ((), (), s32[]{:S(2)}) async-start(), calls=%async_computation.8 | async-start | bytes 2621440 | tf_op jit(solution)/shard_map/reduce_scatter | solution.py:106
  292.9 70.7 %copy-start.1 = (bf16[1024,512]{1,0:T(8,128)(2,1)S(1)}, bf16[1024,512]{1,0:T(8,128)(2,1)}, u32[]{:S(2)}) copy-start(bf16[1024,512]{1,0:T(8,128)(2,1)} %param.10) | copy-start | bytes 3145732
  301.5 60.2 %reduce-scatter.8.cloned.1.call-start = ((), (), s32[]{:S(2)}) async-start(), calls=%async_computation.9 | async-start | bytes 786432 | tf_op jit(solution)/shard_map/reduce_scatter | solution.py:110
Sparse Core Ops, SparseCore 0:
  10.9 53.3 all-gather.12
  68.6 29.9 reduce-scatter.3
  114.2 14.7 all-gather.14
  136.0 77.4 all-gather.16
  235.7 27.0 all-gather.10
  264.3 28.4 all-gather.8
  301.6 43.8 reduce-scatter.5
  347.8 13.8 reduce-scatter.7

commit v13 on v12

--- a/solution.py
+++ b/solution.py
@@ -63,12 +63,15 @@
     ).astype(jnp.bfloat16)
     state_ct = lax.all_to_all(state_slab, "expert", 0, 0, tiled=False)
     state_all = lax.all_gather(state_ct, "tensor", axis=0, tiled=False)
-    state = jnp.transpose(state_all, (2, 1, 0, 3)).reshape(tok_count, width)
-    state_f = state.astype(jnp.float32)
+    state_sq = state_all.astype(jnp.float32)
 
-    squares = jnp.sum(state_f * state_f, axis=1, keepdims=True)
+    squares = jnp.sum(state_sq * state_sq, axis=(0, 1, 3))[:, None]
     scale = lax.rsqrt(squares / width + EPS)
-    state_q = lax.dynamic_slice_in_dim(state_f, me_t * share, share, 1)
+    per = share // cols_e
+    quarter = lax.dynamic_slice_in_dim(state_all, me_t * per, per, 1)
+    state_q = jnp.transpose(quarter, (2, 1, 0, 3)).reshape(tok_count, share).astype(
+        jnp.float32
+    )
     gain_q = lax.dynamic_slice_in_dim(norm_gain, me_t * share, share, 0).astype(jnp.float32)
     normed_q = (state_q * scale * gain_q).astype(jnp.bfloat16)
 
@@ -112,7 +115,7 @@
         tiled=True, axis_index_groups=pairs,
     )
     mixture = mixture.astype(jnp.float32)
-    state_out = lax.dynamic_slice_in_dim(state_f, me_t * share, share, 1)
+    state_out = state_q
     return (state_out + mixture).astype(jnp.bfloat16)
 
 

time: 371 us -> 368 us (level)
  no operation moved by 1% of the time
where the time goes in v13:
time: 368 us; the launch traced here: 367 us
  waiting for transfers between devices  245 us (67%)
  matrix products  65.6 us (18%)
  blocking collectives  26.1 us (7%)
  between operations  13.7 us (4%)
  other arithmetic  10.8 us (3%)
  local copies, waits for them, and re-layouts  5.09 us (1%)
    all_gather x1, waiting for transfers between devices, on_device(): slabs = lax.all_gather(normed_q, ('tensor', 'expert'), axis=0, tiled=False)  77.5 us
    all_gather x1, waiting for transfers between devices, on_device(): got = lax.all_gather(packet, 'expert', axis=0, tiled=False)  53.5 us
    reduce_scatter x1, waiting for transfers between devices, on_device(): lax.psum_scatter(total.astype(jnp.bfloat16).reshape(far, near * tok_count...  44 us
    dot_general x8, matrix products, on_device(): jnp.dot(x, up_proj[loc, :, a * share:(a + 1) * share].T, preferred_elemen...  26.1 us
    all_gather x2, waiting for transfers between devices, on_device(): act_all = lax.all_gather(act, 'tensor', axis=1, tiled=True)  23.4 us
    dot_general x8, matrix products, on_device(): jnp.dot(x, gate_proj[loc, :, a * share:(a + 1) * share].T, preferred_elem...  19.2 us
    reduce_scatter x1, waiting for transfers between devices, on_device(): lax.psum_scatter(partial, 'tensor', scatter_dimension=1, tiled=True)  16.3 us
    reduce_scatter x1, waiting for transfers between devices, on_device(): lax.psum_scatter(halves.reshape(near * tok_count, share), 'expert', scatt...  16.1 us
  transfers between devices with their start and end apart: 8, of which 8 were waited for; matrix products, arithmetic and copies ran while one was open for 9% of the time, Pallas kernels for 0%

profile of v13, /device:TPU:0, one launch (start us, length us, event | category | flops | bytes accessed | tf_op | source)
XLA Modules:
  0.0 367.1 jit_solution(6350593082458220748)
XLA Ops:
  9.1 1.7 pad_maximum_fusion
  10.8 53.5 %all-gather.13.cloned.1.call-done = bf16[1088,1024]{1,0:T(8,128)(2,1)} async-done(((bf16[136,1024]{1,0:T(8,128)(2,1)}), bf16[1088,1024]{1,0:T(8,128)(2,1)}) %all-gather.13.cloned.1.call-update) | async-done | bytes 2228240 | tf_op jit(solution)/shard_map/all_gather | solution.py:48
  64.3 4.2 %fusion.6 = f32[8,128,512]{2,1,0:T(8,128)} fusion(bf16[8,136,1024]{2,1,0:T(8,128)(2,1)} %bitcast.104, bf16[1024,512]{1,0:T(8,128)(2,1)S(1)} %copy-done), kind=kOutput, calls=%fused_computation.7 | convolution fusion | flops 1073741824 | bytes 5242880 | tf_op jit(solution)/shard_map/enh,hc->enc/dot_general | solution.py:49
  68.5 1.1 copy-done.2
  70.5 11.7 %all_to_all.10 = bf16[8,128,128]{2,1,0:T(8,128)(2,1)S(1)} all-to-all(bf16[8,128,128]{2,1,0:T(8,128)(2,1)S(1)} %copy.43), channel_id=1, replica_groups=mesh['expert'=8,'tensor'=4] {'expert'}, dimensions={0} | all-to-all | bytes 524288 | tf_op jit(solution)/shard_map/all_to_all | solution.py:60
  82.3 16.3 %reduce-scatter.4.cloned.1.call-done = f32[1024,128]{1,0:T(8,128)} async-done(((f32[1024,512]{1,0:T(8,128)}), f32[1024,128]{1,0:T(8,128)}) %reduce-scatter.4.cloned.1.call-update) | async-done | bytes 524304 | tf_op jit(solution)/shard_map/reduce_scatter | solution.py:56
  99.7 14.3 %all_to_all.11 = bf16[8,128,128]{2,1,0:T(8,128)(2,1)} all-to-all(bf16[8,128,128]{2,1,0:T(8,128)(2,1)S(1)} %add_convert_fusion.2), channel_id=1, replica_groups=mesh['expert'=8,'tensor'=4] {'expert'}, dimensions={0} | all-to-all | bytes 524288 | tf_op jit(solution)/shard_map/all_to_all | solution.py:64
  114.8 14.2 %all-gather.15.cloned.1.call-done = bf16[32,128,128]{2,1,0:T(8,128)(2,1)} async-done(((bf16[8,128,128]{2,1,0:T(8,128)(2,1)}), bf16[32,128,128]{2,1,0:T(8,128)(2,1)}) %all-gather.15.cloned.1.call-update) | async-done | bytes 1048592 | tf_op jit(solution)/shard_map/all_gather | solution.py:65
  129.0 1.5 multiply_reduce_fusion
  133.0 77.5 %all-gather.17.cloned.1.call-done = bf16[4096,1024]{1,0:T(8,128)(2,1)} async-done(((bf16[128,1024]{1,0:T(8,128)(2,1)}), bf16[4096,1024]{1,0:T(8,128)(2,1)}) %all-gather.17.cloned.1.call-update) | async-done | bytes 8388624 | tf_op jit(solution)/shard_map/all_gather | solution.py:79
  210.5 3.2 fusion.22
  213.7 3.1 fusion.38
  216.8 2.4 fusion.30
  219.2 2.4 fusion.10
  221.6 2.4 fusion.16
  224.0 2.4 fusion.32
  226.4 2.4 fusion.24
  228.8 3.8 %multiply_convert_fusion = bf16[1024,384]{1,0:T(8,128)(2,1)} fusion(f32[1024,384]{1,0:T(8,128)S(1)} %fusion.22, f32[1024,384]{1,0:T(8,128)S(1)} %fusion.38, f32[1024,384]{1,0:T(8,128)S(1)} %fusion.30, f32[1024,384]{1,0:T(8,128)S(1)} %fusion.10, f32[1024,384]{1,0:T(8,128)S(1)} %fusion.16, f32[1024,384]{1,0:T(8,128)S(1)} %fusion.32, ...), kind=kOutput, calls=%fused_computation.10 | convolution fusion | flops 810024960 | bytes 14680064 | tf_op jit(solution)/shard_map/dot_general | solution.py:92
  232.9 3.2 fusion.18
  236.1 3.4 fusion.34
  239.5 3.2 fusion.26
  242.7 2.4 fusion.13
  245.1 2.4 fusion.20
  247.5 2.4 fusion.36
  249.9 2.4 fusion.28
  252.3 3.8 %multiply_convert_fusion.1 = bf16[1024,384]{1,0:T(8,128)(2,1)} fusion(f32[1024,384]{1,0:T(8,128)S(1)} %fusion.18, f32[1024,384]{1,0:T(8,128)S(1)} %fusion.34, f32[1024,384]{1,0:T(8,128)S(1)} %fusion.26, f32[1024,384]{1,0:T(8,128)S(1)} %fusion.13, f32[1024,384]{1,0:T(8,128)S(1)} %fusion.20, f32[1024,384]{1,0:T(8,128)S(1)} %fusion.36, ...), kind=kOutput, calls=%fused_computation.11 | convolution fusion | flops 810024960 | bytes 14680064 | tf_op jit(solution)/shard_map/dot_general | solution.py:92
  259.9 7.6 %fusion = bf16[1024,1024]{1,0:T(8,128)(2,1)} fusion(bf16[1024,1536]{1,0:T(8,128)(2,1)} %all-gather.11.cloned.1.call-done, bf16[2,1536,1024]{2,1,0:T(8,128)(2,1)} %param.15), kind=kOutput, calls=%fused_computation.1 | convolution fusion | flops 3221225472 | bytes 8388608 | tf_op jit(solution)/shard_map/dot_general | solution.py:100
  267.5 22.4 %all-gather.9.cloned.1.call-done = bf16[1024,1536]{1,0:T(8,128)(2,1)} async-done(((bf16[1024,384]{1,0:T(8,128)(2,1)}), bf16[1024,1536]{1,0:T(8,128)(2,1)}) %all-gather.9.cloned.1.call-update) | async-done | bytes 3145744 | tf_op jit(solution)/shard_map/all_gather | solution.py:99
  289.9 8.5 %add_convert_fusion = bf16[1024,1024]{1,0:T(8,128)(2,1)} fusion(bf16[1024,1024]{1,0:T(8,128)(2,1)} %fusion, f32[1024]{0:T(1024)S(1)} %bitcast.102, f32[1024]{0:T(1024)S(1)} %bitcast.103, pred[1024]{0:T(1024)(128)(4,1)S(1)} %get-tuple-element.9, pred[1024]{0:T(1024)(128)(4,1)S(1)} %get-tuple-element.10, bf16[1024,1536]{1,0:T(8,128)(2,1)} %all-gather.9.cloned.1.call-done, ...), kind=kOutput, calls=%fused_computation | convolution fusion | flops 3230662656 | bytes 10496000 | tf_op jit(solution)/shard_map/dot_general | solution.py:100
  298.5 44.0 %reduce-scatter.6.cloned.1.call-done = bf16[1,256,1024]{2,1,0:T(8,128)(2,1)} async-done(((bf16[4,256,1024]{2,1,0:T(8,128)(2,1)}), bf16[1,256,1024]{2,1,0:T(8,128)(2,1)}) %reduce-scatter.6.cloned.1.call-update) | async-done | bytes 524304 | tf_op jit(solution)/shard_map/reduce_scatter | solution.py:109
  342.5 16.1 %reduce-scatter.8.cloned.1.call-done = bf16[128,1024]{1,0:T(8,128)(2,1)} async-done(((bf16[256,1024]{1,0:T(8,128)(2,1)}), bf16[128,1024]{1,0:T(8,128)(2,1)}) %reduce-scatter.8.cloned.1.call-update) | async-done | bytes 262160 | tf_op jit(solution)/shard_map/reduce_scatter | solution.py:113
  358.6 1.7 add_convert_fusion.1
  (58 shorter events, 11.7 us)
Async XLA Ops:
  6.5 57.7 %copy-start = (bf16[1024,512]{1,0:T(8,128)(2,1)S(1)}, bf16[1024,512]{1,0:T(8,128)(2,1)}, u32[]{:S(2)}) copy-start(bf16[1024,512]{1,0:T(8,128)(2,1)} %param.10) | copy-start | bytes 3145732
  6.5 57.7 %all-gather.13.cloned.1.call-start = ((), (), s32[]{:S(2)}) async-start(), calls=%async_computation.10 | async-start | bytes 2506752 | tf_op jit(solution)/shard_map/all_gather | solution.py:48
  10.8 87.8 %reduce-scatter.4.cloned.1.call-start = ((), (), s32[]{:S(2)}) async-start(), calls=%async_computation.5 | async-start | bytes 2621440 | tf_op jit(solution)/shard_map/reduce_scatter | solution.py:56
  68.4 1.2 copy-start.2
  68.5 60.5 %all-gather.15.cloned.1.call-start = ((), (), s32[]{:S(2)}) async-start(), calls=%async_computation.11 | async-start | bytes 1310720 | tf_op jit(solution)/shard_map/all_gather | solution.py:65
  114.0 96.5 %all-gather.17.cloned.1.call-start = ((), (), s32[]{:S(2)}) async-start(), calls=%async_computation.12 | async-start | bytes 8650752 | tf_op jit(solution)/shard_map/all_gather | solution.py:79
  132.9 127.0 %all-gather.11.cloned.1.call-start = ((), (), s32[]{:S(2)}) async-start(), calls=%async_computation.7 | async-start | bytes 3932160 | tf_op jit(solution)/shard_map/all_gather | solution.py:99
  210.5 6.3 %copy-start.3 = (bf16[4096,1024]{1,0:T(8,128)(2,1)S(1)}, bf16[4096,1024]{1,0:T(8,128)(2,1)}, u32[]{:S(2)}) copy-start(bf16[4096,1024]{1,0:T(8,128)(2,1)} %all-gather.17.cloned.1.call-done) | copy-start | bytes 25165828
  232.6 57.3 %all-gather.9.cloned.1.call-start = ((), (), s32[]{:S(2)}) async-start(), calls=%async_computation.6 | async-start | bytes 3932160 | tf_op jit(solution)/shard_map/all_gather | solution.py:99
  232.9 9.8 %slice-start = ((s8[8388608]{0:T(1024)(128)(4,1)}), s8[4194304]{0:T(1024)(128)(4,1)S(1)}, s32[]{:S(2)}) async-start(s8[8388608]{0:T(1024)(128)(4,1)} %bitcast.106), calls=%async_computation.13 | async-start | bytes 8388608
  236.1 6.6 %slice-start.1 = ((s8[8388608]{0:T(1024)(128)(4,1)}), s8[4194304]{0:T(1024)(128)(4,1)S(1)}, s32[]{:S(2)}) async-start(s8[8388608]{0:T(1024)(128)(4,1)} %bitcast.106), calls=%async_computation.14 | async-start | bytes 8388608
  256.2 86.2 %reduce-scatter.6.cloned.1.call-start = ((), (), s32[]{:S(2)}) async-start(), calls=%async_computation.8 | async-start | bytes 2621440 | tf_op jit(solution)/shard_map/reduce_scatter | solution.py:109
  289.9 70.4 %copy-start.1 = (bf16[1024,512]{1,0:T(8,128)(2,1)S(1)}, bf16[1024,512]{1,0:T(8,128)(2,1)}, u32[]{:S(2)}) copy-start(bf16[1024,512]{1,0:T(8,128)(2,1)} %param.10) | copy-start | bytes 3145732
  298.4 60.2 %reduce-scatter.8.cloned.1.call-start = ((), (), s32[]{:S(2)}) async-start(), calls=%async_computation.9 | async-start | bytes 786432 | tf_op jit(solution)/shard_map/reduce_scatter | solution.py:113
Sparse Core Ops, SparseCore 0:
  10.9 53.3 all-gather.12
  68.6 29.9 reduce-scatter.3
  114.1 14.7 all-gather.14
  133.0 77.4 all-gather.16
  232.8 27.0 all-gather.10
  261.4 28.4 all-gather.8
  298.5 43.8 reduce-scatter.5
  344.7 13.8 reduce-scatter.7

commit v14 on v13

--- a/solution.py
+++ b/solution.py
@@ -61,15 +61,18 @@
     state_slab = (
         res_in.astype(jnp.float32) + summed.reshape(groups, tok_count, cols_et)
     ).astype(jnp.bfloat16)
-    state_ct = lax.all_to_all(state_slab, "expert", 0, 0, tiled=False)
-    state_all = lax.all_gather(state_ct, "tensor", axis=0, tiled=False)
+    fan = jnp.broadcast_to(state_slab[:, None], (groups, tensor_ways) + state_slab.shape[1:])
+    state_all = lax.all_to_all(
+        fan.reshape((groups * tensor_ways,) + state_slab.shape[1:]),
+        ("expert", "tensor"), 0, 0, tiled=False,
+    ).reshape((groups, tensor_ways) + state_slab.shape[1:])
     state_sq = state_all.astype(jnp.float32)
 
     squares = jnp.sum(state_sq * state_sq, axis=(0, 1, 3))[:, None]
     scale = lax.rsqrt(squares / width + EPS)
     per = share // cols_e
-    quarter = lax.dynamic_slice_in_dim(state_all, me_t * per, per, 1)
-    state_q = jnp.transpose(quarter, (2, 1, 0, 3)).reshape(tok_count, share).astype(
+    quarter = lax.dynamic_slice_in_dim(state_all, me_t * per, per, 0)
+    state_q = jnp.transpose(quarter, (2, 0, 1, 3)).reshape(tok_count, share).astype(
         jnp.float32
     )
     gain_q = lax.dynamic_slice_in_dim(norm_gain, me_t * share, share, 0).astype(jnp.float32)

time: 368 us -> 368 us (level)
  blocking collectives: 26.1 us -> 11.8 us
  waiting for transfers between devices: 245 us -> 255 us
  starting transfers between devices: 0.7 us -> 5.25 us
    all_to_all x0 -> x1, waiting for transfers between devices: none -> 25.5 us  [on_device(): lax.all_to_all(fan.reshape((groups * tensor_ways,) + state_slab.shape[1:]...]
    all_to_all x1 -> x0, blocking collectives: 14.3 us -> none  [on_device(): state_ct = lax.all_to_all(state_slab, 'expert', 0, 0, tiled=False)]
    all_gather x1 -> x0, waiting for transfers between devices: 14.2 us -> none  [on_device(): state_all = lax.all_gather(state_ct, 'tensor', axis=0, tiled=False)]
    all_to_all x0 -> x1, starting transfers between devices: none -> 4.6 us  [on_device(): lax.all_to_all(fan.reshape((groups * tensor_ways,) + state_slab.shape[1:]...]
where the time goes in v14:
time: 368 us; the launch traced here: 367 us
  waiting for transfers between devices  255 us (69%)
  matrix products  65.6 us (18%)
  between operations  13.7 us (4%)
  blocking collectives  11.8 us (3%)
  other arithmetic  8.69 us (2%)
  local copies, waits for them, and re-layouts  6.36 us (2%)
  starting transfers between devices  5.25 us (1%)
    all_gather x1, waiting for transfers between devices, on_device(): slabs = lax.all_gather(normed_q, ('tensor', 'expert'), axis=0, tiled=False)  76.5 us
    all_gather x1, waiting for transfers between devices, on_device(): got = lax.all_gather(packet, 'expert', axis=0, tiled=False)  53.5 us
    reduce_scatter x1, waiting for transfers between devices, on_device(): lax.psum_scatter(total.astype(jnp.bfloat16).reshape(far, near * tok_count...  44 us
    dot_general x8, matrix products, on_device(): jnp.dot(x, up_proj[loc, :, a * share:(a + 1) * share].T, preferred_elemen...  26.1 us
    all_to_all x1, waiting for transfers between devices, on_device(): lax.all_to_all(fan.reshape((groups * tensor_ways,) + state_slab.shape[1:]...  25.5 us
    all_gather x2, waiting for transfers between devices, on_device(): act_all = lax.all_gather(act, 'tensor', axis=1, tiled=True)  23.4 us
    dot_general x8, matrix products, on_device(): jnp.dot(x, gate_proj[loc, :, a * share:(a + 1) * share].T, preferred_elem...  19.2 us
    reduce_scatter x1, waiting for transfers between devices, on_device(): lax.psum_scatter(partial, 'tensor', scatter_dimension=1, tiled=True)  16.3 us
  transfers between devices with their start and end apart: 8, of which 8 were waited for; matrix products, arithmetic and copies ran while one was open for 9% of the time, Pallas kernels for 0%

profile of v14, /device:TPU:0, one launch (start us, length us, event | category | flops | bytes accessed | tf_op | source)
XLA Modules:
  0.0 366.7 jit_solution(4695612170875004184)
XLA Ops:
  9.1 1.7 pad_maximum_fusion
  10.8 53.5 %all-gather.11.cloned.1.call-done = bf16[1088,1024]{1,0:T(8,128)(2,1)} async-done(((bf16[136,1024]{1,0:T(8,128)(2,1)}), bf16[1088,1024]{1,0:T(8,128)(2,1)}) %all-gather.11.cloned.1.call-update) | async-done | bytes 2228240 | tf_op jit(solution)/shard_map/all_gather | solution.py:48
  64.3 4.2 %fusion.6 = f32[8,128,512]{2,1,0:T(8,128)} fusion(bf16[8,136,1024]{2,1,0:T(8,128)(2,1)} %bitcast.106, bf16[1024,512]{1,0:T(8,128)(2,1)S(1)} %copy-done), kind=kOutput, calls=%fused_computation.7 | convolution fusion | flops 1073741824 | bytes 5242880 | tf_op jit(solution)/shard_map/enh,hc->enc/dot_general | solution.py:49
  68.5 1.2 copy-done.2
  70.6 11.8 %all_to_all.10 = bf16[8,128,128]{2,1,0:T(8,128)(2,1)S(1)} all-to-all(bf16[8,128,128]{2,1,0:T(8,128)(2,1)S(1)} %copy.32), channel_id=1, replica_groups=mesh['expert'=8,'tensor'=4] {'expert'}, dimensions={0} | all-to-all | bytes 524288 | tf_op jit(solution)/shard_map/all_to_all | solution.py:60
  82.3 16.3 %reduce-scatter.4.cloned.1.call-done = f32[1024,128]{1,0:T(8,128)} async-done(((f32[1024,512]{1,0:T(8,128)}), f32[1024,128]{1,0:T(8,128)}) %reduce-scatter.4.cloned.1.call-update) | async-done | bytes 524304 | tf_op jit(solution)/shard_map/reduce_scatter | solution.py:56
  99.7 1.2 broadcast_in_dim.48
  100.9 4.6 %all-to-all-start.1 = ((bf16[32,128,128]{2,1,0:T(8,128)(2,1)}), bf16[32,128,128]{2,1,0:T(8,128)(2,1)S(1)}, u32[]{:S(2)}, u32[]{:S(2)}) async-start(bf16[32,128,128]{2,1,0:T(8,128)(2,1)} %bitcast.9), calls=%async_computation.2 | async-start | bytes 2097152 | tf_op jit(solution)/shard_map/all_to_all | solution.py:65
  106.3 25.5 %all-to-all-done.1 = bf16[32,128,128]{2,1,0:T(8,128)(2,1)S(1)} async-done(((bf16[32,128,128]{2,1,0:T(8,128)(2,1)}), bf16[32,128,128]{2,1,0:T(8,128)(2,1)S(1)}, u32[]{:S(2)}, u32[]{:S(2)}) %all-to-all-start.1) | async-done | bytes 1048608 | tf_op jit(solution)/shard_map/all_to_all | solution.py:65
  133.6 76.5 %all-gather.13.cloned.1.call-done = bf16[4096,1024]{1,0:T(8,128)(2,1)} async-done(((bf16[128,1024]{1,0:T(8,128)(2,1)}), bf16[4096,1024]{1,0:T(8,128)(2,1)}) %all-gather.13.cloned.1.call-update) | async-done | bytes 8388624 | tf_op jit(solution)/shard_map/all_gather | solution.py:82
  210.1 3.2 fusion.22
  213.3 3.1 fusion.38
  216.4 2.4 fusion.30
  218.8 2.4 fusion.10
  221.2 2.4 fusion.16
  223.6 2.4 fusion.32
  226.0 2.4 fusion.24
  228.4 3.8 %multiply_convert_fusion = bf16[1024,384]{1,0:T(8,128)(2,1)} fusion(f32[1024,384]{1,0:T(8,128)S(1)} %fusion.22, f32[1024,384]{1,0:T(8,128)S(1)} %fusion.38, f32[1024,384]{1,0:T(8,128)S(1)} %fusion.30, f32[1024,384]{1,0:T(8,128)S(1)} %fusion.10, f32[1024,384]{1,0:T(8,128)S(1)} %fusion.16, f32[1024,384]{1,0:T(8,128)S(1)} %fusion.32, ...), kind=kOutput, calls=%fused_computation.10 | convolution fusion | flops 810024960 | bytes 14680064 | tf_op jit(solution)/shard_map/dot_general | solution.py:95
  232.5 3.2 fusion.18
  235.7 3.4 fusion.34
  239.1 3.2 fusion.26
  242.3 2.4 fusion.13
  244.7 2.4 fusion.20
  247.1 2.4 fusion.36
  249.6 2.4 fusion.28
  252.0 3.8 %multiply_convert_fusion.1 = bf16[1024,384]{1,0:T(8,128)(2,1)} fusion(f32[1024,384]{1,0:T(8,128)S(1)} %fusion.18, f32[1024,384]{1,0:T(8,128)S(1)} %fusion.34, f32[1024,384]{1,0:T(8,128)S(1)} %fusion.26, f32[1024,384]{1,0:T(8,128)S(1)} %fusion.13, f32[1024,384]{1,0:T(8,128)S(1)} %fusion.20, f32[1024,384]{1,0:T(8,128)S(1)} %fusion.36, ...), kind=kOutput, calls=%fused_computation.11 | convolution fusion | flops 810024960 | bytes 14680064 | tf_op jit(solution)/shard_map/dot_general | solution.py:95
  259.5 7.6 %fusion = bf16[1024,1024]{1,0:T(8,128)(2,1)} fusion(bf16[1024,1536]{1,0:T(8,128)(2,1)} %all-gather.9.cloned.1.call-done, bf16[2,1536,1024]{2,1,0:T(8,128)(2,1)} %param.15), kind=kOutput, calls=%fused_computation.1 | convolution fusion | flops 3221225472 | bytes 8388608 | tf_op jit(solution)/shard_map/dot_general | solution.py:103
  267.1 22.4 %all-gather.7.cloned.1.call-done = bf16[1024,1536]{1,0:T(8,128)(2,1)} async-done(((bf16[1024,384]{1,0:T(8,128)(2,1)}), bf16[1024,1536]{1,0:T(8,128)(2,1)}) %all-gather.7.cloned.1.call-update) | async-done | bytes 3145744 | tf_op jit(solution)/shard_map/all_gather | solution.py:102
  289.5 8.5 %add_convert_fusion = bf16[1024,1024]{1,0:T(8,128)(2,1)} fusion(bf16[1024,1024]{1,0:T(8,128)(2,1)} %fusion, f32[1024]{0:T(1024)S(1)} %bitcast.104, f32[1024]{0:T(1024)S(1)} %bitcast.105, pred[1024]{0:T(1024)(128)(4,1)S(1)} %get-tuple-element.9, pred[1024]{0:T(1024)(128)(4,1)S(1)} %get-tuple-element.10, bf16[1024,1536]{1,0:T(8,128)(2,1)} %all-gather.7.cloned.1.call-done, ...), kind=kOutput, calls=%fused_computation | convolution fusion | flops 3230662656 | bytes 10496000 | tf_op jit(solution)/shard_map/dot_general | solution.py:103
  298.1 44.0 %reduce-scatter.6.cloned.1.call-done = bf16[1,256,1024]{2,1,0:T(8,128)(2,1)} async-done(((bf16[4,256,1024]{2,1,0:T(8,128)(2,1)}), bf16[1,256,1024]{2,1,0:T(8,128)(2,1)}) %reduce-scatter.6.cloned.1.call-update) | async-done | bytes 524304 | tf_op jit(solution)/shard_map/reduce_scatter | solution.py:112
  342.1 16.1 %reduce-scatter.8.cloned.1.call-done = bf16[128,1024]{1,0:T(8,128)(2,1)} async-done(((bf16[256,1024]{1,0:T(8,128)(2,1)}), bf16[128,1024]{1,0:T(8,128)(2,1)}) %reduce-scatter.8.cloned.1.call-update) | async-done | bytes 262160 | tf_op jit(solution)/shard_map/reduce_scatter | solution.py:116
  358.2 1.7 add_convert_fusion.1
  (57 shorter events, 11.0 us)
Async XLA Ops:
  6.5 57.7 %copy-start = (bf16[1024,512]{1,0:T(8,128)(2,1)S(1)}, bf16[1024,512]{1,0:T(8,128)(2,1)}, u32[]{:S(2)}) copy-start(bf16[1024,512]{1,0:T(8,128)(2,1)} %param.10) | copy-start | bytes 3145732
  6.5 57.7 %all-gather.11.cloned.1.call-start = ((), (), s32[]{:S(2)}) async-start(), calls=%async_computation.10 | async-start | bytes 2506752 | tf_op jit(solution)/shard_map/all_gather | solution.py:48
  10.8 87.8 %reduce-scatter.4.cloned.1.call-start = ((), (), s32[]{:S(2)}) async-start(), calls=%async_computation.5 | async-start | bytes 2621440 | tf_op jit(solution)/shard_map/reduce_scatter | solution.py:56
  68.5 1.2 copy-start.2
  100.9 30.8 %all-to-all-start.1 = ((bf16[32,128,128]{2,1,0:T(8,128)(2,1)}), bf16[32,128,128]{2,1,0:T(8,128)(2,1)S(1)}, u32[]{:S(2)}, u32[]{:S(2)}) async-start(bf16[32,128,128]{2,1,0:T(8,128)(2,1)} %bitcast.9), calls=%async_computation.2 | async-start | bytes 2097152 | tf_op jit(solution)/shard_map/all_to_all | solution.py:65
  105.5 104.6 %all-gather.13.cloned.1.call-start = ((), (), s32[]{:S(2)}) async-start(), calls=%async_computation.11 | async-start | bytes 8650752 | tf_op jit(solution)/shard_map/all_gather | solution.py:82
  133.5 126.0 %all-gather.9.cloned.1.call-start = ((), (), s32[]{:S(2)}) async-start(), calls=%async_computation.7 | async-start | bytes 3932160 | tf_op jit(solution)/shard_map/all_gather | solution.py:102
  210.1 6.3 %copy-start.3 = (bf16[4096,1024]{1,0:T(8,128)(2,1)S(1)}, bf16[4096,1024]{1,0:T(8,128)(2,1)}, u32[]{:S(2)}) copy-start(bf16[4096,1024]{1,0:T(8,128)(2,1)} %all-gather.13.cloned.1.call-done) | copy-start | bytes 25165828
  232.3 57.3 %all-gather.7.cloned.1.call-start = ((), (), s32[]{:S(2)}) async-start(), calls=%async_computation.6 | async-start | bytes 3932160 | tf_op jit(solution)/shard_map/all_gather | solution.py:102
  232.5 9.8 %slice-start = ((s8[8388608]{0:T(1024)(128)(4,1)}), s8[4194304]{0:T(1024)(128)(4,1)S(1)}, s32[]{:S(2)}) async-start(s8[8388608]{0:T(1024)(128)(4,1)} %bitcast.108), calls=%async_computation.12 | async-start | bytes 8388608
  235.7 6.6 %slice-start.1 = ((s8[8388608]{0:T(1024)(128)(4,1)}), s8[4194304]{0:T(1024)(128)(4,1)S(1)}, s32[]{:S(2)}) async-start(s8[8388608]{0:T(1024)(128)(4,1)} %bitcast.108), calls=%async_computation.13 | async-start | bytes 8388608
  255.8 86.2 %reduce-scatter.6.cloned.1.call-start = ((), (), s32[]{:S(2)}) async-start(), calls=%async_computation.8 | async-start | bytes 2621440 | tf_op jit(solution)/shard_map/reduce_scatter | solution.py:112
  289.5 70.4 %copy-start.1 = (bf16[1024,512]{1,0:T(8,128)(2,1)S(1)}, bf16[1024,512]{1,0:T(8,128)(2,1)}, u32[]{:S(2)}) copy-start(bf16[1024,512]{1,0:T(8,128)(2,1)} %param.10) | copy-start | bytes 3145732
  298.0 60.2 %reduce-scatter.8.cloned.1.call-start = ((), (), s32[]{:S(2)}) async-start(), calls=%async_computation.9 | async-start | bytes 786432 | tf_op jit(solution)/shard_map/reduce_scatter | solution.py:116
Sparse Core Ops, SparseCore 0:
  10.9 53.3 all-gather.10
  68.6 29.9 reduce-scatter.3
  133.6 76.4 all-gather.12
  232.4 27.0 all-gather.8
  261.0 28.4 all-gather.6
  298.1 43.8 reduce-scatter.5
  344.3 13.8 reduce-scatter.7

commit v15 on v13

--- a/solution.py
+++ b/solution.py
@@ -101,7 +101,7 @@
             act_all, down_proj[loc], preferred_element_type=jnp.float32
         ).astype(jnp.bfloat16)
         w_tok = w_mine[:, loc][:, None]
-        total = total + jnp.where(w_tok > 0, w_tok * out.astype(jnp.float32), 0.0)
+        total = total + w_tok * out.astype(jnp.float32)
     near = 2 if groups % 2 == 0 else 1
     far = groups // near
     pairs = [[z * near + x for x in range(near)] for z in range(far)]

time: 368 us -> 368 us (level)
  no operation moved by 1% of the time
where the time goes in v15:
time: 368 us; the launch traced here: 367 us
  waiting for transfers between devices  245 us (67%)
  matrix products  65.5 us (18%)
  blocking collectives  26.1 us (7%)
  between operations  13.7 us (4%)
  other arithmetic  10.8 us (3%)
  local copies, waits for them, and re-layouts  5.09 us (1%)
    all_gather x1, waiting for transfers between devices, on_device(): slabs = lax.all_gather(normed_q, ('tensor', 'expert'), axis=0, tiled=False)  77.5 us
    all_gather x1, waiting for transfers between devices, on_device(): got = lax.all_gather(packet, 'expert', axis=0, tiled=False)  53.5 us
    reduce_scatter x1, waiting for transfers between devices, on_device(): lax.psum_scatter(total.astype(jnp.bfloat16).reshape(far, near * tok_count...  44 us
    dot_general x8, matrix products, on_device(): jnp.dot(x, up_proj[loc, :, a * share:(a + 1) * share].T, preferred_elemen...  26.1 us
    all_gather x2, waiting for transfers between devices, on_device(): act_all = lax.all_gather(act, 'tensor', axis=1, tiled=True)  23.4 us
    dot_general x8, matrix products, on_device(): jnp.dot(x, gate_proj[loc, :, a * share:(a + 1) * share].T, preferred_elem...  19.2 us
    reduce_scatter x1, waiting for transfers between devices, on_device(): lax.psum_scatter(partial, 'tensor', scatter_dimension=1, tiled=True)  16.3 us
    reduce_scatter x1, waiting for transfers between devices, on_device(): lax.psum_scatter(halves.reshape(near * tok_count, share), 'expert', scatt...  16.1 us
  transfers between devices with their start and end apart: 8, of which 8 were waited for; matrix products, arithmetic and copies ran while one was open for 9% of the time, Pallas kernels for 0%

profile of v15, /device:TPU:0, one launch (start us, length us, event | category | flops | bytes accessed | tf_op | source)
XLA Modules:
  0.0 367.0 jit_solution(12519567455784577258)
XLA Ops:
  9.1 1.7 pad_maximum_fusion
  10.8 53.5 %all-gather.13.cloned.1.call-done = bf16[1088,1024]{1,0:T(8,128)(2,1)} async-done(((bf16[136,1024]{1,0:T(8,128)(2,1)}), bf16[1088,1024]{1,0:T(8,128)(2,1)}) %all-gather.13.cloned.1.call-update) | async-done | bytes 2228240 | tf_op jit(solution)/shard_map/all_gather | solution.py:48
  64.3 4.2 %fusion.6 = f32[8,128,512]{2,1,0:T(8,128)} fusion(bf16[8,136,1024]{2,1,0:T(8,128)(2,1)} %bitcast.102, bf16[1024,512]{1,0:T(8,128)(2,1)S(1)} %copy-done), kind=kOutput, calls=%fused_computation.7 | convolution fusion | flops 1073741824 | bytes 5242880 | tf_op jit(solution)/shard_map/enh,hc->enc/dot_general | solution.py:49
  68.5 1.1 copy-done.2
  70.5 11.8 %all_to_all.10 = bf16[8,128,128]{2,1,0:T(8,128)(2,1)S(1)} all-to-all(bf16[8,128,128]{2,1,0:T(8,128)(2,1)S(1)} %copy.43), channel_id=1, replica_groups=mesh['expert'=8,'tensor'=4] {'expert'}, dimensions={0} | all-to-all | bytes 524288 | tf_op jit(solution)/shard_map/all_to_all | solution.py:60
  82.3 16.3 %reduce-scatter.4.cloned.1.call-done = f32[1024,128]{1,0:T(8,128)} async-done(((f32[1024,512]{1,0:T(8,128)}), f32[1024,128]{1,0:T(8,128)}) %reduce-scatter.4.cloned.1.call-update) | async-done | bytes 524304 | tf_op jit(solution)/shard_map/reduce_scatter | solution.py:56
  99.7 14.3 %all_to_all.11 = bf16[8,128,128]{2,1,0:T(8,128)(2,1)} all-to-all(bf16[8,128,128]{2,1,0:T(8,128)(2,1)S(1)} %add_convert_fusion.2), channel_id=1, replica_groups=mesh['expert'=8,'tensor'=4] {'expert'}, dimensions={0} | all-to-all | bytes 524288 | tf_op jit(solution)/shard_map/all_to_all | solution.py:64
  114.8 14.2 %all-gather.15.cloned.1.call-done = bf16[32,128,128]{2,1,0:T(8,128)(2,1)} async-done(((bf16[8,128,128]{2,1,0:T(8,128)(2,1)}), bf16[32,128,128]{2,1,0:T(8,128)(2,1)}) %all-gather.15.cloned.1.call-update) | async-done | bytes 1048592 | tf_op jit(solution)/shard_map/all_gather | solution.py:65
  129.0 1.5 multiply_reduce_fusion
  133.0 77.5 %all-gather.17.cloned.1.call-done = bf16[4096,1024]{1,0:T(8,128)(2,1)} async-done(((bf16[128,1024]{1,0:T(8,128)(2,1)}), bf16[4096,1024]{1,0:T(8,128)(2,1)}) %all-gather.17.cloned.1.call-update) | async-done | bytes 8388624 | tf_op jit(solution)/shard_map/all_gather | solution.py:79
  210.5 3.2 fusion.22
  213.7 3.1 fusion.38
  216.8 2.4 fusion.30
  219.2 2.4 fusion.10
  221.6 2.4 fusion.16
  224.0 2.4 fusion.32
  226.4 2.4 fusion.24
  228.8 3.8 %multiply_convert_fusion = bf16[1024,384]{1,0:T(8,128)(2,1)} fusion(f32[1024,384]{1,0:T(8,128)S(1)} %fusion.22, f32[1024,384]{1,0:T(8,128)S(1)} %fusion.38, f32[1024,384]{1,0:T(8,128)S(1)} %fusion.30, f32[1024,384]{1,0:T(8,128)S(1)} %fusion.10, f32[1024,384]{1,0:T(8,128)S(1)} %fusion.16, f32[1024,384]{1,0:T(8,128)S(1)} %fusion.32, ...), kind=kOutput, calls=%fused_computation.10 | convolution fusion | flops 810024960 | bytes 14680064 | tf_op jit(solution)/shard_map/dot_general | solution.py:92
  232.9 3.2 fusion.18
  236.1 3.4 fusion.34
  239.5 3.2 fusion.26
  242.7 2.4 fusion.13
  245.1 2.4 fusion.20
  247.5 2.4 fusion.36
  250.0 2.4 fusion.28
  252.4 3.8 %multiply_convert_fusion.1 = bf16[1024,384]{1,0:T(8,128)(2,1)} fusion(f32[1024,384]{1,0:T(8,128)S(1)} %fusion.18, f32[1024,384]{1,0:T(8,128)S(1)} %fusion.34, f32[1024,384]{1,0:T(8,128)S(1)} %fusion.26, f32[1024,384]{1,0:T(8,128)S(1)} %fusion.13, f32[1024,384]{1,0:T(8,128)S(1)} %fusion.20, f32[1024,384]{1,0:T(8,128)S(1)} %fusion.36, ...), kind=kOutput, calls=%fused_computation.11 | convolution fusion | flops 810024960 | bytes 14680064 | tf_op jit(solution)/shard_map/dot_general | solution.py:92
  259.9 7.6 %fusion = bf16[1024,1024]{1,0:T(8,128)(2,1)} fusion(bf16[1024,1536]{1,0:T(8,128)(2,1)} %all-gather.11.cloned.1.call-done, bf16[2,1536,1024]{2,1,0:T(8,128)(2,1)} %param.15), kind=kOutput, calls=%fused_computation.1 | convolution fusion | flops 3221225472 | bytes 8388608 | tf_op jit(solution)/shard_map/dot_general | solution.py:100
  267.5 22.4 %all-gather.9.cloned.1.call-done = bf16[1024,1536]{1,0:T(8,128)(2,1)} async-done(((bf16[1024,384]{1,0:T(8,128)(2,1)}), bf16[1024,1536]{1,0:T(8,128)(2,1)}) %all-gather.9.cloned.1.call-update) | async-done | bytes 3145744 | tf_op jit(solution)/shard_map/all_gather | solution.py:99
  289.9 8.3 %add_convert_fusion = bf16[1024,1024]{1,0:T(8,128)(2,1)} fusion(bf16[1024,1024]{1,0:T(8,128)(2,1)} %fusion, f32[1024]{0:T(1024)S(1)} %bitcast.104, f32[1024]{0:T(1024)S(1)} %bitcast.105, bf16[1024,1536]{1,0:T(8,128)(2,1)} %all-gather.9.cloned.1.call-done, bf16[2,1536,1024]{2,1,0:T(8,128)(2,1)} %param.15), kind=kOutput, calls=%fused_computation | convolution fusion | flops 3228565504 | bytes 10493952 | tf_op jit(solution)/shard_map/dot_general | solution.py:100
  298.3 44.0 %reduce-scatter.6.cloned.1.call-done = bf16[1,256,1024]{2,1,0:T(8,128)(2,1)} async-done(((bf16[4,256,1024]{2,1,0:T(8,128)(2,1)}), bf16[1,256,1024]{2,1,0:T(8,128)(2,1)}) %reduce-scatter.6.cloned.1.call-update) | async-done | bytes 524304 | tf_op jit(solution)/shard_map/reduce_scatter | solution.py:109
  342.3 16.1 %reduce-scatter.8.cloned.1.call-done = bf16[128,1024]{1,0:T(8,128)(2,1)} async-done(((bf16[256,1024]{1,0:T(8,128)(2,1)}), bf16[128,1024]{1,0:T(8,128)(2,1)}) %reduce-scatter.8.cloned.1.call-update) | async-done | bytes 262160 | tf_op jit(solution)/shard_map/reduce_scatter | solution.py:113
  358.4 1.7 add_convert_fusion.1
  (57 shorter events, 11.7 us)
Async XLA Ops:
  6.5 57.7 %copy-start = (bf16[1024,512]{1,0:T(8,128)(2,1)S(1)}, bf16[1024,512]{1,0:T(8,128)(2,1)}, u32[]{:S(2)}) copy-start(bf16[1024,512]{1,0:T(8,128)(2,1)} %param.10) | copy-start | bytes 3145732
  6.5 57.7 %all-gather.13.cloned.1.call-start = ((), (), s32[]{:S(2)}) async-start(), calls=%async_computation.10 | async-start | bytes 2506752 | tf_op jit(solution)/shard_map/all_gather | solution.py:48
  10.7 87.8 %reduce-scatter.4.cloned.1.call-start = ((), (), s32[]{:S(2)}) async-start(), calls=%async_computation.5 | async-start | bytes 2621440 | tf_op jit(solution)/shard_map/reduce_scatter | solution.py:56
  68.4 1.2 copy-start.2
  68.5 60.5 %all-gather.15.cloned.1.call-start = ((), (), s32[]{:S(2)}) async-start(), calls=%async_computation.11 | async-start | bytes 1310720 | tf_op jit(solution)/shard_map/all_gather | solution.py:65
  114.0 96.5 %all-gather.17.cloned.1.call-start = ((), (), s32[]{:S(2)}) async-start(), calls=%async_computation.12 | async-start | bytes 8650752 | tf_op jit(solution)/shard_map/all_gather | solution.py:79
  132.9 127.0 %all-gather.11.cloned.1.call-start = ((), (), s32[]{:S(2)}) async-start(), calls=%async_computation.7 | async-start | bytes 3932160 | tf_op jit(solution)/shard_map/all_gather | solution.py:99
  210.5 6.3 %copy-start.3 = (bf16[4096,1024]{1,0:T(8,128)(2,1)S(1)}, bf16[4096,1024]{1,0:T(8,128)(2,1)}, u32[]{:S(2)}) copy-start(bf16[4096,1024]{1,0:T(8,128)(2,1)} %all-gather.17.cloned.1.call-done) | copy-start | bytes 25165828
  232.7 57.3 %all-gather.9.cloned.1.call-start = ((), (), s32[]{:S(2)}) async-start(), calls=%async_computation.6 | async-start | bytes 3932160 | tf_op jit(solution)/shard_map/all_gather | solution.py:99
  232.9 9.8 %slice-start = ((s8[8388608]{0:T(1024)(128)(4,1)}), s8[4194304]{0:T(1024)(128)(4,1)S(1)}, s32[]{:S(2)}) async-start(s8[8388608]{0:T(1024)(128)(4,1)} %bitcast.106), calls=%async_computation.13 | async-start | bytes 8388608
  236.1 6.6 %slice-start.1 = ((s8[8388608]{0:T(1024)(128)(4,1)}), s8[4194304]{0:T(1024)(128)(4,1)S(1)}, s32[]{:S(2)}) async-start(s8[8388608]{0:T(1024)(128)(4,1)} %bitcast.106), calls=%async_computation.14 | async-start | bytes 8388608
  256.2 86.1 %reduce-scatter.6.cloned.1.call-start = ((), (), s32[]{:S(2)}) async-start(), calls=%async_computation.8 | async-start | bytes 2621440 | tf_op jit(solution)/shard_map/reduce_scatter | solution.py:109
  289.9 70.2 %copy-start.1 = (bf16[1024,512]{1,0:T(8,128)(2,1)S(1)}, bf16[1024,512]{1,0:T(8,128)(2,1)}, u32[]{:S(2)}) copy-start(bf16[1024,512]{1,0:T(8,128)(2,1)} %param.10) | copy-start | bytes 3145732
  298.3 60.2 %reduce-scatter.8.cloned.1.call-start = ((), (), s32[]{:S(2)}) async-start(), calls=%async_computation.9 | async-start | bytes 786432 | tf_op jit(solution)/shard_map/reduce_scatter | solution.py:113
Sparse Core Ops, SparseCore 0:
  10.9 53.3 all-gather.12
  68.6 29.9 reduce-scatter.3
  114.2 14.7 all-gather.14
  133.1 77.4 all-gather.16
  232.8 27.0 all-gather.10
  261.4 28.4 all-gather.8
  298.4 43.8 reduce-scatter.5
  344.5 13.8 reduce-scatter.7
